TPU v7x, 128 devices: a whole 4x4x4 slice. The times are simulated.
128 devices in a mesh: dp: 32 (over z, x, core), blk: 4 (over y).
Axes of the slice: x: 4, y: 4, z: 4, core: 2. Of those that a mesh axis runs over, the one named last changes fastest.
Arguments:
- embeddings: bfloat16 [32768, 768], P(('dp', 'blk')), may hold values from -6 to 6
- point_group: int32 [32768, 1], P(('dp', 'blk')), may hold values from 0 to 31; in each aligned block of 256 rows (0 to 255, 256 to 511, ...) at most 16 rows name the same one
- point_cluster: int32 [32768], P(('dp', 'blk')), may hold values from 0 to 31
- point_order: int32 [32768], P(('dp', 'blk')), may hold values from 0 to 32767, each once
Outputs:
- nearest: float32 [32768], P(('dp', 'blk'))
Inputs may be any that keep to these rules, and one draw needn't show every extreme that they name: `point_group`: among the rows of one device at most 16 name the same group, a bound that some blocks reach. `point_order`: every value appears once.
All inputs are finite; a program needn't handle non-finite values.
Results may differ from a plain program's by a relative error of at most 0.00077.
Values may be sent and summed in bfloat16 or wider, within the bound.
No kernel may reach another device: no remote copies, remote signals or barrier semaphores. Data moves between devices by JAX's collectives and lax.ppermute only.
A program may use at most 64 MiB of HBM per device.

v0:
```python
import jax
import jax.numpy as jnp
from jax import lax
from jax.sharding import PartitionSpec as P

CLG = 32


def normalize(embeddings):
    values = embeddings.astype(jnp.float32)
    scale = lax.rsqrt(jnp.mean(values * values, axis=1, keepdims=True) + 1e-06)
    width = embeddings.shape[1]
    return (values * scale * width ** (-0.5)).astype(jnp.bfloat16)


def strongest(current, query, keys):
    query_rows, query_labels, query_order = query
    key_rows, key_labels, key_order = keys
    count = key_rows.shape[0]
    step = 512
    tiles = (
        key_rows.reshape(count // step, step, key_rows.shape[1]),
        key_labels.reshape(count // step, step),
        key_order.reshape(count // step, step),
    )

    def visit(best, block):
        rows, labels, order = block
        scores = lax.dot_general(
            query_rows, rows, (((1,), (1,)), ((), ())), preferred_element_type=jnp.float32
        )
        mask = (query_labels[:, None] == labels[None, :]) & (order[None, :] < query_order[:, None])
        return (jnp.maximum(best, jnp.max(jnp.where(mask, scores, -2.0), axis=1)), None)

    best, unused = lax.scan(visit, current, tiles)
    return best


def body(embeddings, point_group, point_cluster, point_order):
    groups = lax.axis_size("dp")
    blocks = lax.axis_size("blk")
    points = embeddings.shape[0]
    width = embeddings.shape[1]
    capacity = 2 * points // groups
    slots = groups * capacity
    unit = normalize(embeddings)
    group = point_group[:, 0]
    labels = group * CLG + point_cluster
    onehot = (group[:, None] == jnp.arange(groups, dtype=jnp.int32)[None, :]).astype(jnp.int32)
    before = jnp.cumsum(onehot, axis=0) - onehot
    target = group * capacity + jnp.sum(before * onehot, axis=1)
    send_rows = jnp.zeros((slots, width), jnp.bfloat16).at[target].set(unit)
    send_labels = jnp.full((slots,), -1, jnp.int32).at[target].set(labels)
    send_order = jnp.zeros((slots,), jnp.int32).at[target].set(point_order)
    floor_init = jnp.full((slots,), -2.0, jnp.float32)

    def widen(array):
        rest = array.shape[1:]
        sectioned = array.reshape((groups, 1, capacity) + rest)
        sectioned = jnp.broadcast_to(sectioned, (groups, blocks, capacity) + rest)
        return sectioned.reshape((groups * blocks * capacity,) + rest)

    arrived = (
        lax.all_to_all(widen(send_rows), ("dp", "blk"), split_axis=0, concat_axis=0, tiled=True),
        lax.all_to_all(widen(send_labels), ("dp", "blk"), split_axis=0, concat_axis=0, tiled=True),
        lax.all_to_all(widen(send_order), ("dp", "blk"), split_axis=0, concat_axis=0, tiled=True),
    )
    own_block = lax.axis_index("blk")

    def pick(array):
        rest = array.shape[1:]
        shaped = array.reshape((groups, blocks, capacity) + rest)
        return lax.dynamic_index_in_dim(shaped, own_block, 1, keepdims=False).reshape(
            (slots,) + rest
        )

    query = (pick(arrived[0]), pick(arrived[1]), pick(arrived[2]))
    best = strongest(floor_init, query, arrived)
    answer = jnp.where(best > -1.5, best, -1.0)
    returned = lax.all_to_all(answer, "dp", split_axis=0, concat_axis=0, tiled=True)
    return returned[target]


def solution(mesh):
    in_specs = (P(("dp", "blk"), None), P(("dp", "blk"), None), P(("dp", "blk")), P(("dp", "blk")))
    out_specs = P(("dp", "blk"))
    return jax.shard_map(body, mesh=mesh, in_specs=in_specs, out_specs=out_specs, check_vma=False)
```

profile of v0, /device:TPU:1, one launch (start us, length us, event | category | flops | bytes accessed | tf_op | source)
XLA Modules:
  0.0 113.0 jit_solution(5989285394249019429)
XLA Ops:
  1.5 0.8 fusion.15
  3.0 0.7 multiply_add_fusion
  3.7 1.4 %scatter_custom_fusion = s32[512]{0:T(512)S(1)} fusion(s32[256]{0:T(256)S(1)} %bitcast.80, s32[256]{0:T(256)S(1)} %multiply_add_fusion, s32[]{:T(128)} %constant.56.clone.1), kind=kCustom, calls=%fused_computation.38 | custom fusion | bytes 2052 | tf_op jit(solution)/shard_map/scatter | solution.py:53
  5.8 11.5 %all-to-all-start = ((s32[128,16,1]{1,2,0:T(1,128)}), s32[128,16,1]{1,2,0:T(1,128)S(1)}, u32[]{:S(2)}, u32[]{:S(2)}) async-start(s32[128,16,1]{1,2,0:T(1,128)} %bitcast.5), calls=%async_computation | async-start | bytes 131072 | tf_op jit(solution)/shard_map/all_to_all | solution.py:65
  17.3 1.2 %fusion.5 = f32[256]{0:T(256)S(1)} fusion(bf16[256,768]{1,0:T(8,128)(2,1)} %param.6), kind=kLoop, calls=%fused_computation.15 | loop fusion | flops 589568 | bytes 394240 | tf_op jit(solution)/shard_map/reduce_sum | solution.py:11
  18.4 1.6 %scatter_custom_fusion.1 = s32[512]{0:T(512)S(1)} fusion(s32[256]{0:T(256)S(1)} %bitcast.81, s32[256]{0:T(256)} %param.9, s32[]{:T(128)} %constant.16.clone.1), kind=kCustom, calls=%fused_computation.35 | custom fusion | bytes 2560 | tf_op jit(solution)/shard_map/scatter | solution.py:54
  20.1 6.9 %all-to-all-done = s32[128,16,1]{1,2,0:T(1,128)S(1)} async-done(((s32[128,16,1]{1,2,0:T(1,128)}), s32[128,16,1]{1,2,0:T(1,128)S(1)}, u32[]{:S(2)}, u32[]{:S(2)}) %all-to-all-start) | async-done | bytes 8224 | tf_op jit(solution)/shard_map/all_to_all | solution.py:65
  27.6 4.2 %all-to-all-start.1 = ((s32[128,16,1]{1,2,0:T(1,128)}), s32[128,16,1]{1,2,0:T(1,128)S(1)}, u32[]{:S(2)}, u32[]{:S(2)}) async-start(s32[128,16,1]{1,2,0:T(1,128)} %bitcast.8), calls=%async_computation.1 | async-start | bytes 131072 | tf_op jit(solution)/shard_map/all_to_all | solution.py:66
  31.8 2.4 %scatter_custom_fusion.2 = bf16[512,768]{1,0:T(8,128)(2,1)S(1)} fusion(s32[256]{0:T(256)S(1)} %bitcast.82, bf16[256,768]{1,0:T(8,128)(2,1)} %param.6, f32[]{:T(128)} %constant.37.clone.1, f32[256]{0:T(256)S(1)} %add_rsqrt_fusion, bf16[]{:T(256)} %constant.27.clone.1), kind=kCustom, calls=%fused_computation.18 | custom fusion | flops 786432 | bytes 1180678 | tf_op jit(solution)/shard_map/scatter | solution.py:52
  34.2 7.3 %all-to-all-done.1 = s32[128,16,1]{1,2,0:T(1,128)S(1)} async-done(((s32[128,16,1]{1,2,0:T(1,128)}), s32[128,16,1]{1,2,0:T(1,128)S(1)}, u32[]{:S(2)}, u32[]{:S(2)}) %all-to-all-start.1) | async-done | bytes 8224 | tf_op jit(solution)/shard_map/all_to_all | solution.py:66
  41.5 1.9 %broadcast_in_dim.58 = bf16[32,4,16,768]{3,2,1,0:T(8,128)(2,1)} broadcast(bf16[32,16,768]{2,1,0:T(8,128)(2,1)S(1)} %bitcast.67), dimensions={0,2,3} | broadcast | bytes 3932160 | tf_op jit(solution)/shard_map/broadcast_in_dim | solution.py:60
  43.4 4.2 %all-to-all-start.2 = ((bf16[128,16,768]{2,1,0:T(8,128)(2,1)}), bf16[128,16,768]{2,1,0:T(8,128)(2,1)S(1)}, u32[]{:S(2)}, u32[]{:S(2)}) async-start(bf16[128,16,768]{2,1,0:T(8,128)(2,1)} %bitcast.12), calls=%async_computation.2 | async-start | bytes 6291456 | tf_op jit(solution)/shard_map/all_to_all | solution.py:64
  48.1 0.7 reduce.11
  48.9 0.7 reduce.12
  50.0 39.5 %all-to-all-done.2 = bf16[128,16,768]{2,1,0:T(8,128)(2,1)S(1)} async-done(((bf16[128,16,768]{2,1,0:T(8,128)(2,1)}), bf16[128,16,768]{2,1,0:T(8,128)(2,1)S(1)}, u32[]{:S(2)}, u32[]{:S(2)}) %all-to-all-start.2) | async-done | bytes 3145760 | tf_op jit(solution)/shard_map/all_to_all | solution.py:64
  89.4 0.9 constant_dynamic-slice_fusion.2
  90.4 7.3 %while.12 = (s32[]{:T(128)}, f32[512]{0:T(512)S(1)}, s32[32,16]{1,0:T(8,128)}, s32[4,512]{1,0:T(4,128)S(1)}, s32[4,512]{1,0:T(4,128)S(1)}, /*index=5*/s32[32,16]...) while((s32[]{:T(128)}, f32[512]{0:T(512)S(1)}, ...), condition=%wide.wide.region_9.10_spmd.clone, body=%wide.wide.region_7.9_spmd.clone.sunk | while | flops 403964416 | bytes 1597583 | solution.py:35
  90.4 1.8 %fusion.30 = f32[512]{0:T(512)S(1)} fusion(bf16[512,768]{1,0:T(8,128)(2,1)} %get-tuple-element.222, bf16[4,512,768]{2,1,0:T(8,128)(2,1)S(1)} %get-tuple-element.221, s32[]{:T(128)S(6)} %copy.14, s32[512]{0:T(512)S(1)} %get-tuple-element.223, s32[512]{0:T(512)S(1)} %get-tuple-element.224, s32[512]{0:T(512)S(1)} %bitcast.75, s32[512]{0:T(512)S(1)} %bitcast.76), kind=kOutput, calls=%fused_computation.6.clone.clone.1 | convolution fusion | flops 403963392 | bytes 1583108 | tf_op jit(solution)/shard_map/while/body/eval_jaxpr/dot_general | solution.py:29
  92.2 1.8 %fusion.30 = f32[512]{0:T(512)S(1)} fusion(bf16[512,768]{1,0:T(8,128)(2,1)} %get-tuple-element.222, bf16[4,512,768]{2,1,0:T(8,128)(2,1)S(1)} %get-tuple-element.221, s32[]{:T(128)S(6)} %copy.14, s32[512]{0:T(512)S(1)} %get-tuple-element.223, s32[512]{0:T(512)S(1)} %get-tuple-element.224, s32[512]{0:T(512)S(1)} %bitcast.75, s32[512]{0:T(512)S(1)} %bitcast.76), kind=kOutput, calls=%fused_computation.6.clone.clone.1 | convolution fusion | flops 403963392 | bytes 1583108 | tf_op jit(solution)/shard_map/while/body/eval_jaxpr/dot_general | solution.py:29
  94.1 1.8 %fusion.30 = f32[512]{0:T(512)S(1)} fusion(bf16[512,768]{1,0:T(8,128)(2,1)} %get-tuple-element.222, bf16[4,512,768]{2,1,0:T(8,128)(2,1)S(1)} %get-tuple-element.221, s32[]{:T(128)S(6)} %copy.14, s32[512]{0:T(512)S(1)} %get-tuple-element.223, s32[512]{0:T(512)S(1)} %get-tuple-element.224, s32[512]{0:T(512)S(1)} %bitcast.75, s32[512]{0:T(512)S(1)} %bitcast.76), kind=kOutput, calls=%fused_computation.6.clone.clone.1 | convolution fusion | flops 403963392 | bytes 1583108 | tf_op jit(solution)/shard_map/while/body/eval_jaxpr/dot_general | solution.py:29
  95.9 1.8 %fusion.30 = f32[512]{0:T(512)S(1)} fusion(bf16[512,768]{1,0:T(8,128)(2,1)} %get-tuple-element.222, bf16[4,512,768]{2,1,0:T(8,128)(2,1)S(1)} %get-tuple-element.221, s32[]{:T(128)S(6)} %copy.14, s32[512]{0:T(512)S(1)} %get-tuple-element.223, s32[512]{0:T(512)S(1)} %get-tuple-element.224, s32[512]{0:T(512)S(1)} %bitcast.75, s32[512]{0:T(512)S(1)} %bitcast.76), kind=kOutput, calls=%fused_computation.6.clone.clone.1 | convolution fusion | flops 403963392 | bytes 1583108 | tf_op jit(solution)/shard_map/while/body/eval_jaxpr/dot_general | solution.py:29
  98.4 3.7 %all-to-all-start.3 = ((f32[32,16,1]{1,2,0:T(1,128)}), f32[32,16,1]{1,2,0:T(1,128)S(1)}, u32[]{:S(2)}, u32[]{:S(2)}) async-start(f32[32,16,1]{1,2,0:T(1,128)} %bitcast.16), calls=%async_computation.3 | async-start | bytes 32768 | tf_op jit(solution)/shard_map/all_to_all | solution.py:80
  102.1 7.1 %all-to-all-done.3 = f32[32,16,1]{1,2,0:T(1,128)S(1)} async-done(((f32[32,16,1]{1,2,0:T(1,128)}), f32[32,16,1]{1,2,0:T(1,128)S(1)}, u32[]{:S(2)}, u32[]{:S(2)}) %all-to-all-start.3) | async-done | bytes 2080 | tf_op jit(solution)/shard_map/all_to_all | solution.py:80
  110.5 2.5 %gather_fusion = f32[256]{0:T(256)} fusion(f32[512]{0:T(512)S(1)} %all_to_all.34, s32[1024]{0:T(1024)S(1)} %pad_clamp_fusion), kind=kCustom, calls=%fused_computation | custom fusion | bytes 3072 | tf_op jit(solution)/shard_map/gather | solution.py:81
  (37 shorter events, 6.5 us)
Async XLA Ops:
  5.8 21.2 %all-to-all-start = ((s32[128,16,1]{1,2,0:T(1,128)}), s32[128,16,1]{1,2,0:T(1,128)S(1)}, u32[]{:S(2)}, u32[]{:S(2)}) async-start(s32[128,16,1]{1,2,0:T(1,128)} %bitcast.5), calls=%async_computation | async-start | bytes 131072 | tf_op jit(solution)/shard_map/all_to_all | solution.py:65
  27.6 14.0 %all-to-all-start.1 = ((s32[128,16,1]{1,2,0:T(1,128)}), s32[128,16,1]{1,2,0:T(1,128)S(1)}, u32[]{:S(2)}, u32[]{:S(2)}) async-start(s32[128,16,1]{1,2,0:T(1,128)} %bitcast.8), calls=%async_computation.1 | async-start | bytes 131072 | tf_op jit(solution)/shard_map/all_to_all | solution.py:66
  43.4 46.0 %all-to-all-start.2 = ((bf16[128,16,768]{2,1,0:T(8,128)(2,1)}), bf16[128,16,768]{2,1,0:T(8,128)(2,1)S(1)}, u32[]{:S(2)}, u32[]{:S(2)}) async-start(bf16[128,16,768]{2,1,0:T(8,128)(2,1)} %bitcast.12), calls=%async_computation.2 | async-start | bytes 6291456 | tf_op jit(solution)/shard_map/all_to_all | solution.py:64
  49.8 40.6 %copy-start = (s32[32,1,16]{2,1,0:T(1,128)}, s32[32,1,16]{2,1,0:T(1,128)S(1)}, u32[]{:S(2)}) copy-start(s32[32,1,16]{2,1,0:T(1,128)S(1)} %constant_dynamic-slice_fusion.3) | copy-start | bytes 6148
  49.9 40.5 %copy-start.1 = (s32[32,1,16]{2,1,0:T(1,128)}, s32[32,1,16]{2,1,0:T(1,128)S(1)}, u32[]{:S(2)}) copy-start(s32[32,1,16]{2,1,0:T(1,128)S(1)} %constant_dynamic-slice_fusion.4) | copy-start | bytes 6148
  98.4 10.7 %all-to-all-start.3 = ((f32[32,16,1]{1,2,0:T(1,128)}), f32[32,16,1]{1,2,0:T(1,128)S(1)}, u32[]{:S(2)}, u32[]{:S(2)}) async-start(f32[32,16,1]{1,2,0:T(1,128)} %bitcast.16), calls=%async_computation.3 | async-start | bytes 32768 | tf_op jit(solution)/shard_map/all_to_all | solution.py:80
where the time goes:
time: 114 us; the launch traced here: 113 us
  waiting for transfers between devices  60.7 us (53%)
  starting transfers between devices  23.5 us (21%)
  local copies, waits for them, and re-layouts  12.1 us (11%)
  other arithmetic  9.2 us (8%)
  matrix products  7.14 us (6%)
    all_to_all x1, waiting for transfers between devices, body(): lax.all_to_all(widen(send_rows), ('dp', 'blk'), split_axis=0, concat_axis...  39.5 us
    all_to_all x1, starting transfers between devices, body(): lax.all_to_all(widen(send_labels), ('dp', 'blk'), split_axis=0, concat_ax...  11.5 us
    all_to_all x1, waiting for transfers between devices, body(): lax.all_to_all(widen(send_order), ('dp', 'blk'), split_axis=0, concat_axi...  7.31 us
    dot_general x4, matrix products, visit(): lax.dot_general(query_rows, rows, (((1,), (1,)), ((), ())), preferred_ele...  7.14 us
    all_to_all x1, waiting for transfers between devices, body(): lax.all_to_all(answer, 'dp', split_axis=0, concat_axis=0, tiled=True)  7.07 us
    all_to_all x1, waiting for transfers between devices, body(): lax.all_to_all(widen(send_labels), ('dp', 'blk'), split_axis=0, concat_ax...  6.88 us
    all_to_all x1, starting transfers between devices, body(): lax.all_to_all(widen(send_rows), ('dp', 'blk'), split_axis=0, concat_axis...  4.2 us
    all_to_all x1, starting transfers between devices, body(): lax.all_to_all(widen(send_order), ('dp', 'blk'), split_axis=0, concat_axi...  4.18 us
  transfers between devices with their start and end apart: 4, of which 4 were waited for; matrix products, arithmetic and copies ran while one was open for 7% of the time, Pallas kernels for 0%

commit v1 on v0

v1 whole, which is shorter than its diff:
```python
import numpy as np
import jax
import jax.numpy as jnp
from jax import lax
from jax.sharding import PartitionSpec as P

CLG = 32
EXTRA = 128


def normalize(embeddings):
    values = embeddings.astype(jnp.float32)
    scale = lax.rsqrt(jnp.mean(values * values, axis=1, keepdims=True) + 1e-06)
    width = embeddings.shape[1]
    return (values * scale * width ** (-0.5)).astype(jnp.bfloat16)


def layout(zs, xs, ys):
    def lin(z, x, c, y):
        return ((z * xs + x) * 2 + c) * ys + y

    count = zs * xs * 2 * ys
    dev_of = np.zeros((zs * xs + zs * ys, 4), np.int32)
    nxt = np.zeros(count, np.int32)
    for z in range(zs):
        for x in range(xs):
            for y in range(ys):
                dev_of[z * xs + x, y] = lin(z, x, 0, y)
                dev_of[zs * xs + z * ys + y, x] = lin(z, x, 1, y)
                nxt[lin(z, x, 0, y)] = lin(z, x, 0, (y + 1) % ys)
                nxt[lin(z, x, 1, y)] = lin(z, (x + 1) % xs, 1, y)
    return dev_of, nxt


def strongest(query, keys):
    query_rows, query_cluster, query_order = query
    key_rows, key_cluster, key_order = keys
    count = key_rows.shape[0]
    step = 512
    tiles = (
        key_rows.reshape(count // step, step, key_rows.shape[1]),
        key_cluster.reshape(count // step, step),
        key_order.reshape(count // step, step),
    )

    def visit(best, block):
        rows, cluster, order = block
        scores = lax.dot_general(
            query_rows, rows, (((1,), (1,)), ((), ())), preferred_element_type=jnp.float32
        )
        mask = (query_cluster[:, None] == cluster[None, :]) & (order[None, :] < query_order[:, None])
        return (jnp.maximum(best, jnp.max(jnp.where(mask, scores, -2.0), axis=1)), None)

    init = jnp.full((query_rows.shape[0],), -2.0, jnp.float32)
    best, unused = lax.scan(visit, init, tiles)
    return best


def split_meta(rows, width):
    cluster = rows[:, width].astype(jnp.float32)
    order = rows[:, width + 1].astype(jnp.float32) * 256.0 + rows[:, width + 2].astype(jnp.float32)
    return rows[:, :width], cluster, order


def body(embeddings, point_group, point_cluster, point_order, dev_of, nxt):
    devices = nxt.shape[0]
    width = embeddings.shape[1]
    unit = normalize(embeddings)
    group = point_group[:, 0]
    groups = dev_of.shape[0]
    onehot = (group[:, None] == jnp.arange(groups, dtype=jnp.int32)[None, :]).astype(jnp.int32)
    before = jnp.cumsum(onehot, axis=0) - onehot
    rank = jnp.sum(before * onehot, axis=1)
    target = jnp.asarray(dev_of)[group, rank // 4] * 4 + rank % 4
    meta = jnp.stack(
        [point_cluster, point_order // 256, point_order % 256], axis=1
    ).astype(jnp.bfloat16)
    packed = jnp.concatenate(
        [unit, meta, jnp.zeros((unit.shape[0], EXTRA - 3), jnp.bfloat16)], axis=1
    )
    empty = jnp.zeros((devices * 4, width + EXTRA), jnp.bfloat16).at[:, width].set(-1.0)
    send = empty.at[target].set(packed)
    own = lax.all_to_all(send, ("dp", "blk"), split_axis=0, concat_axis=0, tiled=True)
    forward = [(i, int(nxt[i])) for i in range(devices)]
    backward = [(int(nxt[i]), i) for i in range(devices)]
    from_prev = lax.ppermute(own, ("dp", "blk"), forward)
    from_next = lax.ppermute(own, ("dp", "blk"), backward)
    half = own.shape[0] // 2
    far_a = lax.ppermute(from_next[:half], ("dp", "blk"), backward)
    far_b = lax.ppermute(from_prev[half:], ("dp", "blk"), forward)
    keys = jnp.concatenate([own, from_prev, from_next, far_a, far_b], axis=0)
    best = strongest(split_meta(own, width), split_meta(keys, width))
    answer = jnp.where(best > -1.5, best, -1.0)
    returned = lax.all_to_all(answer, ("dp", "blk"), split_axis=0, concat_axis=0, tiled=True)
    return returned[target]


def solution(mesh):
    zs, xs, ys = 4, 4, 4
    dev_of, nxt = layout(zs, xs, ys)
    in_specs = (P(("dp", "blk"), None), P(("dp", "blk"), None), P(("dp", "blk")), P(("dp", "blk")))
    out_specs = P(("dp", "blk"))

    def run(embeddings, point_group, point_cluster, point_order):
        return body(embeddings, point_group, point_cluster, point_order, dev_of, nxt)

    return jax.shard_map(run, mesh=mesh, in_specs=in_specs, out_specs=out_specs, check_vma=False)
```

time: 114 us -> 96.9 us (0.85)
  waiting for transfers between devices: 60.7 us -> 29.1 us
  blocking collectives: 0 us -> 29.2 us
  starting transfers between devices: 23.5 us -> 9.55 us
    all_to_all x4 -> x1, waiting for transfers between devices: 60.7 us -> 9.79 us  [body(): lax.all_to_all(answer, ('dp', 'blk'), split_axis=0, concat_axis=0, tiled=...]
    all_to_all x0 -> x1, blocking collectives: none -> 29.2 us  [body(): lax.all_to_all(send, ('dp', 'blk'), split_axis=0, concat_axis=0, tiled=True)]
    ppermute x0 -> x4, waiting for transfers between devices: none -> 19.3 us  [the longest x1 11.1 us: body(): from_next = lax.ppermute(own, ('dp', 'blk'), backward)]
    all_to_all x4 -> x1, starting transfers between devices: 23.5 us -> 5.68 us  [body(): lax.all_to_all(answer, ('dp', 'blk'), split_axis=0, concat_axis=0, tiled=...]
    ppermute x0 -> x4, starting transfers between devices: none -> 3.87 us  [the longest x1 2.26 us: body(): far_a = lax.ppermute(from_next[:half], ('dp', 'blk'), backward)]
    broadcast_in_dim x5 -> x1, local copies, waits for them, and re-layouts: 3.32 us -> 0.01 us  [body(): jnp.zeros((unit.shape[0], EXTRA - 3), jnp.bfloat16)]
    scatter x1 -> x0, other arithmetic: 2.43 us -> none  [body(): send_rows = jnp.zeros((slots, width), jnp.bfloat16).at[target].set(unit)]
    gather x0 -> x1, local copies, waits for them, and re-layouts: none -> 2.29 us  [body(): target = jnp.asarray(dev_of)[group, rank // 4] * 4 + rank % 4]
  transfers between devices with their start and end apart: 4 -> 5, of which waited for: 4 -> 4; matrix products, arithmetic and copies ran while one was open for 7% -> 2% of each run, Pallas kernels for 0% -> 0%
where the time goes in v1:
time: 96.9 us; the launch traced here: 96.4 us
  blocking collectives  29.2 us (30%)
  waiting for transfers between devices  29.1 us (30%)
  local copies, waits for them, and re-layouts  11.3 us (12%)
  starting transfers between devices  9.55 us (10%)
  other arithmetic  9.07 us (9%)
  matrix products  7.14 us (7%)
    all_to_all x1, blocking collectives, body(): lax.all_to_all(send, ('dp', 'blk'), split_axis=0, concat_axis=0, tiled=True)  29.2 us
    ppermute x1, waiting for transfers between devices, body(): from_next = lax.ppermute(own, ('dp', 'blk'), backward)  11.1 us
    all_to_all x1, waiting for transfers between devices, body(): lax.all_to_all(answer, ('dp', 'blk'), split_axis=0, concat_axis=0, tiled=...  9.79 us
    dot_general x4, matrix products, visit(): lax.dot_general(query_rows, rows, (((1,), (1,)), ((), ())), preferred_ele...  7.14 us
    all_to_all x1, starting transfers between devices, body(): lax.all_to_all(answer, ('dp', 'blk'), split_axis=0, concat_axis=0, tiled=...  5.68 us
    ppermute x1, waiting for transfers between devices, body(): far_b = lax.ppermute(from_prev[half:], ('dp', 'blk'), forward)  4.47 us
    ppermute x1, waiting for transfers between devices, body(): far_a = lax.ppermute(from_next[:half], ('dp', 'blk'), backward)  3.75 us
    another operation x5, other arithmetic  2.62 us
  transfers between devices with their start and end apart: 5, of which 4 were waited for; matrix products, arithmetic and copies ran while one was open for 2% of the time, Pallas kernels for 0%

profile of v1, /device:TPU:1, one launch (start us, length us, event | category | flops | bytes accessed | tf_op | source)
XLA Modules:
  0.0 96.4 jit_solution(1313137890135343279)
XLA Ops:
  2.1 0.8 fusion.10
  2.9 0.7 fusion.15
  3.6 2.3 %gather_fusion = s32[256]{0:T(256)S(1)} fusion(s32[32,4]{1,0:T(8,128)} %constant.127.clone, s32[256]{0:T(256)S(1)} %bitcast.51), kind=kCustom, calls=%fused_computation | custom fusion | bytes 4096 | tf_op jit(solution)/shard_map/gather | solution.py:74
  6.8 1.2 %fusion.5 = f32[256]{0:T(256)S(1)} fusion(bf16[256,768]{1,0:T(8,128)(2,1)} %param.9), kind=kLoop, calls=%fused_computation.16 | loop fusion | flops 589568 | bytes 394240 | tf_op jit(solution)/shard_map/reduce_sum | solution.py:13
  8.0 1.2 %fusion.7 = bf16[256,768]{1,0:T(8,128)(2,1)S(1)} fusion(bf16[256,768]{1,0:T(8,128)(2,1)} %param.9, f32[256]{0:T(256)S(1)} %add_rsqrt_fusion), kind=kLoop, calls=%fused_computation.18 | loop fusion | flops 786432 | bytes 787456 | tf_op jit(solution)/shard_map/convert_element_type | solution.py:15
  11.0 2.2 %scatter_fusion = bf16[512,896]{1,0:T(8,128)(2,1)S(1)} fusion(bf16[512,896]{1,0:T(8,128)(2,1)S(1)} %scatter.15, s32[256]{0:T(256)S(1)} %bitcast.55, bf16[256,896]{1,0:T(8,128)(2,1)S(1)} %concatenate.13), kind=kCustom, calls=%fused_computation.2 | custom fusion | bytes 1377280 | tf_op jit(solution)/shard_map/scatter | solution.py:82
  13.4 29.2 %all_to_all.24 = bf16[128,4,896]{2,1,0:T(4,128)(2,1)S(1)} all-to-all(bf16[128,4,896]{2,1,0:T(4,128)(2,1)S(1)} %all_to_all.16), channel_id=1, replica_groups=mesh['dp'=32,'blk'=4] {'dp','blk'}, dimensions={0} | all-to-all | bytes 1835008 | tf_op jit(solution)/shard_map/all_to_all | solution.py:83
  42.8 1.1 %collective-permute-start.1 = (bf16[512,896]{1,0:T(8,128)(2,1)S(1)}, bf16[512,896]{1,0:T(8,128)(2,1)S(1)}, u32[]{:S(2)}, u32[]{:S(2)}) collective-permute-start(bf16[512,896]{1,0:T(8,128)(2,1)S(1)} %all_to_all.18), channel_id=1, source_target_pairs={{1,0},{2,1},{3,2},{0,3},{12,4},{13,5},{14,6},{15,7},{9,8},{10,9},{... | collective-permute-start | bytes 2752520 | tf_op jit(solution)/shard_map/ppermute | solution.py:87
  44.4 11.1 %collective-permute-done.1 = bf16[512,896]{1,0:T(8,128)(2,1)S(1)} collective-permute-done((bf16[512,896]{1,0:T(8,128)(2,1)S(1)}, bf16[512,896]{1,0:T(8,128)(2,1)S(1)}, u32[]{:S(2)}, u32[]{:S(2)}) %collective-permute-start.1) | collective-permute-done | bytes 917536 | tf_op jit(solution)/shard_map/ppermute | solution.py:87
  55.5 2.3 %collective-permute-start.2 = (bf16[256,896]{1,0:T(8,128)(2,1)S(1)}, bf16[256,896]{1,0:T(8,128)(2,1)S(1)}, u32[]{:S(2)}, u32[]{:S(2)}) collective-permute-start(bf16[256,896]{1,0:T(8,128)(2,1)S(1)} %slice.68), channel_id=1, source_target_pairs={{1,0},{2,1},{3,2},{0,3},{12,4},{13,5},{14,6},{15,7},{9,8},{10,9},{... | collective-permute-start | bytes 1376264 | tf_op jit(solution)/shard_map/ppermute | solution.py:89
  57.8 0.9 slice.76
  59.4 3.7 %collective-permute-done.2 = bf16[256,896]{1,0:T(8,128)(2,1)S(1)} collective-permute-done((bf16[256,896]{1,0:T(8,128)(2,1)S(1)}, bf16[256,896]{1,0:T(8,128)(2,1)S(1)}, u32[]{:S(2)}, u32[]{:S(2)}) %collective-permute-start.2) | collective-permute-done | bytes 458784 | tf_op jit(solution)/shard_map/ppermute | solution.py:89
  63.2 4.5 %collective-permute-done.3 = bf16[256,896]{1,0:T(8,128)(2,1)S(1)} collective-permute-done((bf16[256,896]{1,0:T(8,128)(2,1)S(1)}, bf16[256,896]{1,0:T(8,128)(2,1)S(1)}, u32[]{:S(2)}, u32[]{:S(2)}) %collective-permute-start.3) | collective-permute-done | bytes 458784 | tf_op jit(solution)/shard_map/ppermute | solution.py:90
  67.8 0.8 add_reduce_fusion
  68.8 7.4 %while.12 = (s32[]{:T(128)}, f32[512]{0:T(512)S(1)}, f32[512]{0:T(512)S(1)}, f32[4,512]{1,0:T(4,128)S(1)}, f32[4,512]{1,0:T(4,128)S(1)}, /*index=5*/f32[512]{0:T...) while((s32[]{:T(128)}, f32[512]{0:T(512)S(1)}, ...), condition=%wide.region_8.9_spmd.clone, body=%wide.region_6.8_spmd.clone.sunk | while | flops 403964416 | bytes 1597559 | solution.py:55
  68.8 1.8 %fusion.26 = f32[512]{0:T(512)S(1)} fusion(bf16[512,768]{1,0:T(8,128)(2,1)} %get-tuple-element.191, bf16[4,512,768]{2,1,0:T(8,128)(2,1)S(1)} %get-tuple-element.190, s32[]{:T(128)} %get-tuple-element.174, f32[512]{0:T(512)S(1)} %get-tuple-element.189, f32[512]{0:T(512)S(1)} %get-tuple-element.186, f32[512]{0:T(512)S(1)} %bitcast.53, f32[512]{0:T(512)S(1)} %bitcast.54), kind=kOutput, calls=%fused_computation.5.clone.1 | convolution fusion | flops 403963392 | bytes 1583108 | tf_op jit(solution)/shard_map/while/body/eval_jaxpr/dot_general | solution.py:48
  70.7 1.8 %fusion.26 = f32[512]{0:T(512)S(1)} fusion(bf16[512,768]{1,0:T(8,128)(2,1)} %get-tuple-element.191, bf16[4,512,768]{2,1,0:T(8,128)(2,1)S(1)} %get-tuple-element.190, s32[]{:T(128)} %get-tuple-element.174, f32[512]{0:T(512)S(1)} %get-tuple-element.189, f32[512]{0:T(512)S(1)} %get-tuple-element.186, f32[512]{0:T(512)S(1)} %bitcast.53, f32[512]{0:T(512)S(1)} %bitcast.54), kind=kOutput, calls=%fused_computation.5.clone.1 | convolution fusion | flops 403963392 | bytes 1583108 | tf_op jit(solution)/shard_map/while/body/eval_jaxpr/dot_general | solution.py:48
  72.5 1.8 %fusion.26 = f32[512]{0:T(512)S(1)} fusion(bf16[512,768]{1,0:T(8,128)(2,1)} %get-tuple-element.191, bf16[4,512,768]{2,1,0:T(8,128)(2,1)S(1)} %get-tuple-element.190, s32[]{:T(128)} %get-tuple-element.174, f32[512]{0:T(512)S(1)} %get-tuple-element.189, f32[512]{0:T(512)S(1)} %get-tuple-element.186, f32[512]{0:T(512)S(1)} %bitcast.53, f32[512]{0:T(512)S(1)} %bitcast.54), kind=kOutput, calls=%fused_computation.5.clone.1 | convolution fusion | flops 403963392 | bytes 1583108 | tf_op jit(solution)/shard_map/while/body/eval_jaxpr/dot_general | solution.py:48
  74.4 1.8 %fusion.26 = f32[512]{0:T(512)S(1)} fusion(bf16[512,768]{1,0:T(8,128)(2,1)} %get-tuple-element.191, bf16[4,512,768]{2,1,0:T(8,128)(2,1)S(1)} %get-tuple-element.190, s32[]{:T(128)} %get-tuple-element.174, f32[512]{0:T(512)S(1)} %get-tuple-element.189, f32[512]{0:T(512)S(1)} %get-tuple-element.186, f32[512]{0:T(512)S(1)} %bitcast.53, f32[512]{0:T(512)S(1)} %bitcast.54), kind=kOutput, calls=%fused_computation.5.clone.1 | convolution fusion | flops 403963392 | bytes 1583108 | tf_op jit(solution)/shard_map/while/body/eval_jaxpr/dot_general | solution.py:48
  76.2 0.7 all_to_all.19
  76.9 5.7 %all-to-all-start.1 = ((f32[128,4,1]{1,2,0:T(1,128)}), f32[128,4,1]{1,2,0:T(1,128)S(1)}, u32[]{:S(2)}, u32[]{:S(2)}) async-start(f32[128,4,1]{1,2,0:T(1,128)} %bitcast.9), calls=%async_computation.1 | async-start | bytes 131072 | tf_op jit(solution)/shard_map/all_to_all | solution.py:94
  82.6 9.8 %all-to-all-done.1 = f32[128,4,1]{1,2,0:T(1,128)S(1)} async-done(((f32[128,4,1]{1,2,0:T(1,128)}), f32[128,4,1]{1,2,0:T(1,128)S(1)}, u32[]{:S(2)}, u32[]{:S(2)}) %all-to-all-start.1) | async-done | bytes 2080 | tf_op jit(solution)/shard_map/all_to_all | solution.py:94
  92.9 0.8 reduce.21
  93.8 2.5 %gather_fusion.1 = f32[256]{0:T(256)} fusion(f32[512]{0:T(512)S(1)} %all_to_all.21, s32[1024]{0:T(1024)S(1)} %pad_clamp_fusion), kind=kCustom, calls=%fused_computation.1 | custom fusion | bytes 3072 | tf_op jit(solution)/shard_map/gather | solution.py:95
  (47 shorter events, 6.9 us)
Async XLA Ops:
  42.8 12.6 %collective-permute-start.1 = (bf16[512,896]{1,0:T(8,128)(2,1)S(1)}, bf16[512,896]{1,0:T(8,128)(2,1)S(1)}, u32[]{:S(2)}, u32[]{:S(2)}) collective-permute-start(bf16[512,896]{1,0:T(8,128)(2,1)S(1)} %all_to_all.18), channel_id=1, source_target_pairs={{1,0},{2,1},{3,2},{0,3},{12,4},{13,5},{14,6},{15,7},{9,8},{10,9},{... | collective-permute-start | bytes 2752520 | tf_op jit(solution)/shard_map/ppermute | solution.py:87
  43.9 14.9 %collective-permute-start = (bf16[512,896]{1,0:T(8,128)(2,1)S(1)}, bf16[512,896]{1,0:T(8,128)(2,1)S(1)}, u32[]{:S(2)}, u32[]{:S(2)}) collective-permute-start(bf16[512,896]{1,0:T(8,128)(2,1)S(1)} %all_to_all.18), channel_id=1, source_target_pairs={{0,1},{1,2},{2,3},{3,0},{4,12},{5,13},{6,14},{7,15},{8,9},{9,10},{... | collective-permute-start | bytes 2752520 | tf_op jit(solution)/shard_map/ppermute | solution.py:86
  55.5 7.7 %collective-permute-start.2 = (bf16[256,896]{1,0:T(8,128)(2,1)S(1)}, bf16[256,896]{1,0:T(8,128)(2,1)S(1)}, u32[]{:S(2)}, u32[]{:S(2)}) collective-permute-start(bf16[256,896]{1,0:T(8,128)(2,1)S(1)} %slice.68), channel_id=1, source_target_pairs={{1,0},{2,1},{3,2},{0,3},{12,4},{13,5},{14,6},{15,7},{9,8},{10,9},{... | collective-permute-start | bytes 1376264 | tf_op jit(solution)/shard_map/ppermute | solution.py:89
  58.8 8.9 %collective-permute-start.3 = (bf16[256,896]{1,0:T(8,128)(2,1)S(1)}, bf16[256,896]{1,0:T(8,128)(2,1)S(1)}, u32[]{:S(2)}, u32[]{:S(2)}) collective-permute-start(bf16[256,896]{1,0:T(8,128)(2,1)S(1)} %slice.69), channel_id=1, source_target_pairs={{0,1},{1,2},{2,3},{3,0},{4,12},{5,13},{6,14},{7,15},{8,9},{9,10},{... | collective-permute-start | bytes 1376264 | tf_op jit(solution)/shard_map/ppermute | solution.py:90
  76.9 15.5 %all-to-all-start.1 = ((f32[128,4,1]{1,2,0:T(1,128)}), f32[128,4,1]{1,2,0:T(1,128)S(1)}, u32[]{:S(2)}, u32[]{:S(2)}) async-start(f32[128,4,1]{1,2,0:T(1,128)} %bitcast.9), calls=%async_computation.1 | async-start | bytes 131072 | tf_op jit(solution)/shard_map/all_to_all | solution.py:94

commit v2 on v1

v2 whole, which is shorter than its diff:
```python
import numpy as np
import jax
import jax.numpy as jnp
from jax import lax
from jax.sharding import PartitionSpec as P

EXTRA = 128


def normalize(embeddings):
    values = embeddings.astype(jnp.float32)
    scale = lax.rsqrt(jnp.mean(values * values, axis=1, keepdims=True) + 1e-06)
    width = embeddings.shape[1]
    return (values * scale * width ** (-0.5)).astype(jnp.bfloat16)


def ring_of(zs, xs, ys):
    def lin(z, x, c, y):
        return ((z * xs + x) * 2 + c) * ys + y

    nxt = np.zeros(zs * xs * 2 * ys, np.int32)
    for z in range(zs):
        for x in range(xs):
            for y in range(ys):
                nxt[lin(z, x, 0, y)] = lin(z, x, 0, (y + 1) % ys)
                nxt[lin(z, x, 1, y)] = lin(z, (x + 1) % xs, 1, y)
    return nxt


def device_of(group, place, zs, xs, ys):
    first = group * 2 * ys + place
    other = group - zs * xs
    second = ((other // ys * xs + place) * 2 + 1) * ys + other % ys
    return jnp.where(group < zs * xs, first, second)


def split_meta(rows, width):
    cluster = rows[:, width].astype(jnp.float32) - 1.0
    order = rows[:, width + 1].astype(jnp.float32) * 256.0 + rows[:, width + 2].astype(jnp.float32)
    return rows[:, :width], cluster, order


def best_over(query, keys):
    query_rows, query_cluster, query_order = query
    key_rows, key_cluster, key_order = keys
    scores = lax.dot_general(
        query_rows, key_rows, (((1,), (1,)), ((), ())), preferred_element_type=jnp.float32
    )
    mask = (query_cluster[:, None] == key_cluster[None, :]) & (key_order[None, :] < query_order[:, None])
    return jnp.max(jnp.where(mask, scores, -2.0), axis=1)


def body(embeddings, point_group, point_cluster, point_order, nxt, dims):
    zs, xs, ys = dims
    devices = nxt.shape[0]
    points, width = embeddings.shape
    slots = devices * 4
    unit = normalize(embeddings)
    group = point_group[:, 0]
    index = jnp.arange(points, dtype=jnp.int32)
    same = (group[:, None] == group[None, :]) & (index[None, :] < index[:, None])
    rank = jnp.sum(same.astype(jnp.int32), axis=1)
    target = device_of(group, rank // 4, zs, xs, ys) * 4 + rank % 4
    meta = jnp.stack(
        [point_cluster + 1, point_order // 256, point_order % 256], axis=1
    ).astype(jnp.bfloat16)
    packed = jnp.concatenate(
        [unit, meta, jnp.zeros((points, EXTRA - 3), jnp.bfloat16)], axis=1
    )
    place = (target[None, :] == jnp.arange(slots, dtype=jnp.int32)[:, None]).astype(jnp.bfloat16)
    send = lax.dot_general(
        place, packed, (((1,), (0,)), ((), ())), preferred_element_type=jnp.float32
    ).astype(jnp.bfloat16)
    own = lax.all_to_all(send, ("dp", "blk"), split_axis=0, concat_axis=0, tiled=True)
    forward = [(i, int(nxt[i])) for i in range(devices)]
    backward = [(int(nxt[i]), i) for i in range(devices)]
    from_prev = lax.ppermute(own, ("dp", "blk"), forward)
    from_next = lax.ppermute(own, ("dp", "blk"), backward)
    half = own.shape[0] // 2
    far_a = lax.ppermute(from_next[:half], ("dp", "blk"), backward)
    far_b = lax.ppermute(from_prev[half:], ("dp", "blk"), forward)
    query = split_meta(own, width)
    best = best_over(query, query)
    best = jnp.maximum(best, best_over(query, split_meta(from_prev, width)))
    best = jnp.maximum(best, best_over(query, split_meta(from_next, width)))
    best = jnp.maximum(best, best_over(query, split_meta(far_a, width)))
    best = jnp.maximum(best, best_over(query, split_meta(far_b, width)))
    answer = jnp.where(best > -1.5, best, -1.0)
    returned = lax.all_to_all(answer, ("dp", "blk"), split_axis=0, concat_axis=0, tiled=True)
    pick = target[:, None] == jnp.arange(slots, dtype=jnp.int32)[None, :]
    return jnp.max(jnp.where(pick, returned[None, :], -jnp.inf), axis=1)


def solution(mesh):
    dims = (4, 4, 4)
    nxt = ring_of(*dims)
    in_specs = (P(("dp", "blk"), None), P(("dp", "blk"), None), P(("dp", "blk")), P(("dp", "blk")))
    out_specs = P(("dp", "blk"))

    def run(embeddings, point_group, point_cluster, point_order):
        return body(embeddings, point_group, point_cluster, point_order, nxt, dims)

    return jax.shard_map(run, mesh=mesh, in_specs=in_specs, out_specs=out_specs, check_vma=False)
```

time: 96.9 us -> 79.8 us (0.82)
  local copies, waits for them, and re-layouts: 11.3 us -> 1.84 us
  matrix products: 7.14 us -> 3.26 us
  waiting for transfers between devices: 29.1 us -> 26.6 us
    gather x2 -> x0, local copies, waits for them, and re-layouts: 4.8 us -> none  [the longest x1 2.51 us: body(): return returned[target]]
    dot_general x4 -> x6, matrix products: 7.14 us -> 3.26 us  [the longest x5 2.83 us: best_over(): lax.dot_general(query_rows, key_rows, (((1,), (1,)), ((), ())), preferred...]
    scatter x3 -> x0, local copies, waits for them, and re-layouts: 2.23 us -> none  [the longest x1 2.15 us: body(): send = empty.at[target].set(packed)]
    sub x0 -> x5, other arithmetic: none -> 1.32 us  [split_meta(): cluster = rows[:, width].astype(jnp.float32) - 1.0]
    another operation x5 -> x2, other arithmetic: 2.62 us -> 1.38 us
    ppermute x1, waiting for transfers between devices: 4.47 us -> 3.32 us  [body(): far_b = lax.ppermute(from_prev[half:], ('dp', 'blk'), forward)]
    slice x2 -> x0, local copies, waits for them, and re-layouts: 1.13 us -> none  [split_meta(): return (rows[:, :width], cluster, order)]
  transfers between devices with their start and end apart: 5 -> 5, of which waited for: 4 -> 4; matrix products, arithmetic and copies ran while one was open for 2% -> 4% of each run, Pallas kernels for 0% -> 0%
where the time goes in v2:
time: 79.8 us; the launch traced here: 79.5 us
  blocking collectives  29.2 us (37%)
  waiting for transfers between devices  26.6 us (33%)
  starting transfers between devices  9.56 us (12%)
  other arithmetic  8.88 us (11%)
  matrix products  3.26 us (4%)
  local copies, waits for them, and re-layouts  1.84 us (2%)
    all_to_all x1, blocking collectives, body(): lax.all_to_all(send, ('dp', 'blk'), split_axis=0, concat_axis=0, tiled=True)  29.2 us
    ppermute x1, waiting for transfers between devices, body(): from_next = lax.ppermute(own, ('dp', 'blk'), backward)  10.1 us
    all_to_all x1, waiting for transfers between devices, body(): lax.all_to_all(answer, ('dp', 'blk'), split_axis=0, concat_axis=0, tiled=...  9.76 us
    all_to_all x1, starting transfers between devices, body(): lax.all_to_all(answer, ('dp', 'blk'), split_axis=0, concat_axis=0, tiled=...  5.69 us
    ppermute x1, waiting for transfers between devices, body(): far_a = lax.ppermute(from_next[:half], ('dp', 'blk'), backward)  3.38 us
    ppermute x1, waiting for transfers between devices, body(): far_b = lax.ppermute(from_prev[half:], ('dp', 'blk'), forward)  3.32 us
    dot_general x5, matrix products, best_over(): lax.dot_general(query_rows, key_rows, (((1,), (1,)), ((), ())), preferred...  2.83 us
    ppermute x1, starting transfers between devices, body(): far_a = lax.ppermute(from_next[:half], ('dp', 'blk'), backward)  2.26 us
  transfers between devices with their start and end apart: 5, of which 4 were waited for; matrix products, arithmetic and copies ran while one was open for 4% of the time, Pallas kernels for 0%

profile of v2, /device:TPU:1, one launch (start us, length us, event | category | flops | bytes accessed | tf_op | source)
XLA Modules:
  0.0 79.5 jit_solution(15455042804183007471)
XLA Ops:
  0.0 0.7 add_convert_fusion
  0.7 0.9 %convert_reduce_fusion = s32[256]{0:T(256)S(1)} fusion(s32[256]{0:T(256)} %bitcast.6), kind=kLoop, calls=%fused_computation.35 | loop fusion | flops 327424 | bytes 2048 | tf_op jit(solution)/shard_map/reduce_sum | solution.py:62
  1.6 0.7 fusion.22
  2.3 1.2 %fusion.5 = f32[256]{0:T(256)S(1)} fusion(bf16[256,768]{1,0:T(8,128)(2,1)} %param.4), kind=kLoop, calls=%fused_computation.13 | loop fusion | flops 589568 | bytes 394240 | tf_op jit(solution)/shard_map/reduce_sum | solution.py:12
  3.5 0.7 fusion.24
  4.5 1.2 %fusion.7 = bf16[256,768]{1,0:T(8,128)(2,1)S(1)} fusion(bf16[256,768]{1,0:T(8,128)(2,1)} %param.4, f32[256]{0:T(256)S(1)} %add_rsqrt_fusion), kind=kLoop, calls=%fused_computation.15 | loop fusion | flops 786432 | bytes 787456 | tf_op jit(solution)/shard_map/convert_element_type | solution.py:14
  6.0 0.4 convolution_convert_fusion
  6.7 29.2 %all_to_all.18 = bf16[128,4,896]{2,1,0:T(4,128)(2,1)S(1)} all-to-all(bf16[128,4,896]{2,1,0:T(4,128)(2,1)S(1)} %all_to_all.12), channel_id=1, replica_groups=mesh['dp'=32,'blk'=4] {'dp','blk'}, dimensions={0} | all-to-all | bytes 1835008 | tf_op jit(solution)/shard_map/all_to_all | solution.py:74
  36.1 1.1 %collective-permute-start.1 = (bf16[512,896]{1,0:T(8,128)(2,1)S(1)}, bf16[512,896]{1,0:T(8,128)(2,1)S(1)}, u32[]{:S(2)}, u32[]{:S(2)}) collective-permute-start(bf16[512,896]{1,0:T(8,128)(2,1)S(1)} %all_to_all.14), channel_id=1, source_target_pairs={{1,0},{2,1},{3,2},{0,3},{12,4},{13,5},{14,6},{15,7},{9,8},{10,9},{... | collective-permute-start | bytes 2752520 | tf_op jit(solution)/shard_map/ppermute | solution.py:78
  37.1 0.5 collective-permute-start
  37.9 0.7 fusion
  38.6 10.1 %collective-permute-done.1 = bf16[512,896]{1,0:T(8,128)(2,1)S(1)} collective-permute-done((bf16[512,896]{1,0:T(8,128)(2,1)S(1)}, bf16[512,896]{1,0:T(8,128)(2,1)S(1)}, u32[]{:S(2)}, u32[]{:S(2)}) %collective-permute-start.1) | collective-permute-done | bytes 917536 | tf_op jit(solution)/shard_map/ppermute | solution.py:78
  48.7 2.3 %collective-permute-start.2 = (bf16[256,896]{1,0:T(8,128)(2,1)S(1)}, bf16[256,896]{1,0:T(8,128)(2,1)S(1)}, u32[]{:S(2)}, u32[]{:S(2)}) collective-permute-start(bf16[256,896]{1,0:T(8,128)(2,1)S(1)} %slice.100), channel_id=1, source_target_pairs={{1,0},{2,1},{3,2},{0,3},{12,4},{13,5},{14,6},{15,7},{9,8},{10,9},{... | collective-permute-start | bytes 1376264 | tf_op jit(solution)/shard_map/ppermute | solution.py:80
  51.4 0.7 fusion.2
  52.4 0.7 fusion.1
  53.1 3.4 %collective-permute-done.2 = bf16[256,896]{1,0:T(8,128)(2,1)S(1)} collective-permute-done((bf16[256,896]{1,0:T(8,128)(2,1)S(1)}, bf16[256,896]{1,0:T(8,128)(2,1)S(1)}, u32[]{:S(2)}, u32[]{:S(2)}) %collective-permute-start.2) | collective-permute-done | bytes 458784 | tf_op jit(solution)/shard_map/ppermute | solution.py:80
  56.6 3.3 %collective-permute-done.3 = bf16[256,896]{1,0:T(8,128)(2,1)S(1)} collective-permute-done((bf16[256,896]{1,0:T(8,128)(2,1)S(1)}, bf16[256,896]{1,0:T(8,128)(2,1)S(1)}, u32[]{:S(2)}, u32[]{:S(2)}) %collective-permute-start.3) | collective-permute-done | bytes 458784 | tf_op jit(solution)/shard_map/ppermute | solution.py:81
  60.2 0.4 fusion.3
  61.2 0.6 compare_select_fusion
  61.8 5.7 %all-to-all-start.1 = ((f32[128,4,1]{1,2,0:T(1,128)}), f32[128,4,1]{1,2,0:T(1,128)S(1)}, u32[]{:S(2)}, u32[]{:S(2)}) async-start(f32[128,4,1]{1,2,0:T(1,128)} %bitcast.3), calls=%async_computation.1 | async-start | bytes 131072 | tf_op jit(solution)/shard_map/all_to_all | solution.py:89
  67.5 9.8 %all-to-all-done.1 = f32[128,4,1]{1,2,0:T(1,128)S(1)} async-done(((f32[128,4,1]{1,2,0:T(1,128)}), f32[128,4,1]{1,2,0:T(1,128)S(1)}, u32[]{:S(2)}, u32[]{:S(2)}) %all-to-all-start.1) | async-done | bytes 2080 | tf_op jit(solution)/shard_map/all_to_all | solution.py:89
  77.3 0.5 broadcast.432
  77.8 0.8 %reduce.23 = f32[128,4]{1,0:T(8,128)S(1)} reduce(f32[128,4,1]{1,2,0:T(1,128)S(1)} %all-to-all-done.1, f32[]{:T(128)} %broadcast.432), dimensions={2}, to_apply=%all_to_all.15.reduce_sub_computation.3 | reduce | bytes 4100 | tf_op jit(solution)/shard_map/all_to_all | solution.py:89
  78.7 0.8 select_reduce_fusion
  (24 shorter events, 3.2 us)
Async XLA Ops:
  36.1 12.6 %collective-permute-start.1 = (bf16[512,896]{1,0:T(8,128)(2,1)S(1)}, bf16[512,896]{1,0:T(8,128)(2,1)S(1)}, u32[]{:S(2)}, u32[]{:S(2)}) collective-permute-start(bf16[512,896]{1,0:T(8,128)(2,1)S(1)} %all_to_all.14), channel_id=1, source_target_pairs={{1,0},{2,1},{3,2},{0,3},{12,4},{13,5},{14,6},{15,7},{9,8},{10,9},{... | collective-permute-start | bytes 2752520 | tf_op jit(solution)/shard_map/ppermute | solution.py:78
  37.1 13.9 %collective-permute-start = (bf16[512,896]{1,0:T(8,128)(2,1)S(1)}, bf16[512,896]{1,0:T(8,128)(2,1)S(1)}, u32[]{:S(2)}, u32[]{:S(2)}) collective-permute-start(bf16[512,896]{1,0:T(8,128)(2,1)S(1)} %all_to_all.14), channel_id=1, source_target_pairs={{0,1},{1,2},{2,3},{3,0},{4,12},{5,13},{6,14},{7,15},{8,9},{9,10},{... | collective-permute-start | bytes 2752520 | tf_op jit(solution)/shard_map/ppermute | solution.py:77
  48.7 7.7 %collective-permute-start.2 = (bf16[256,896]{1,0:T(8,128)(2,1)S(1)}, bf16[256,896]{1,0:T(8,128)(2,1)S(1)}, u32[]{:S(2)}, u32[]{:S(2)}) collective-permute-start(bf16[256,896]{1,0:T(8,128)(2,1)S(1)} %slice.100), channel_id=1, source_target_pairs={{1,0},{2,1},{3,2},{0,3},{12,4},{13,5},{14,6},{15,7},{9,8},{10,9},{... | collective-permute-start | bytes 1376264 | tf_op jit(solution)/shard_map/ppermute | solution.py:80
  51.0 8.9 %collective-permute-start.3 = (bf16[256,896]{1,0:T(8,128)(2,1)S(1)}, bf16[256,896]{1,0:T(8,128)(2,1)S(1)}, u32[]{:S(2)}, u32[]{:S(2)}) collective-permute-start(bf16[256,896]{1,0:T(8,128)(2,1)S(1)} %slice.105), channel_id=1, source_target_pairs={{0,1},{1,2},{2,3},{3,0},{4,12},{5,13},{6,14},{7,15},{8,9},{9,10},{... | collective-permute-start | bytes 1376264 | tf_op jit(solution)/shard_map/ppermute | solution.py:81
  60.6 6.9 %copy-start = (s32[256,1]{0,1:T(1,128)S(1)}, s32[256,1]{0,1:T(1,128)}, u32[]{:S(2)}) copy-start(s32[256,1]{0,1:T(1,128)} %param.5) | copy-start | bytes 3076
  61.8 15.5 %all-to-all-start.1 = ((f32[128,4,1]{1,2,0:T(1,128)}), f32[128,4,1]{1,2,0:T(1,128)S(1)}, u32[]{:S(2)}, u32[]{:S(2)}) async-start(f32[128,4,1]{1,2,0:T(1,128)} %bitcast.3), calls=%async_computation.1 | async-start | bytes 131072 | tf_op jit(solution)/shard_map/all_to_all | solution.py:89

commit v3 on v2

--- a/solution.py
+++ b/solution.py
@@ -74,19 +74,22 @@
     own = lax.all_to_all(send, ("dp", "blk"), split_axis=0, concat_axis=0, tiled=True)
     forward = [(i, int(nxt[i])) for i in range(devices)]
     backward = [(int(nxt[i]), i) for i in range(devices)]
-    from_prev = lax.ppermute(own, ("dp", "blk"), forward)
-    from_next = lax.ppermute(own, ("dp", "blk"), backward)
     half = own.shape[0] // 2
-    far_a = lax.ppermute(from_next[:half], ("dp", "blk"), backward)
-    far_b = lax.ppermute(from_prev[half:], ("dp", "blk"), forward)
+    own_a, own_b = own[:half], own[half:]
+    prev_b = lax.ppermute(own_b, ("dp", "blk"), forward)
+    next_a = lax.ppermute(own_a, ("dp", "blk"), backward)
+    prev_a = lax.ppermute(own_a, ("dp", "blk"), forward)
+    next_b = lax.ppermute(own_b, ("dp", "blk"), backward)
+    far_b = lax.ppermute(prev_b, ("dp", "blk"), forward)
+    far_a = lax.ppermute(next_a, ("dp", "blk"), backward)
     query = split_meta(own, width)
     best = best_over(query, query)
-    best = jnp.maximum(best, best_over(query, split_meta(from_prev, width)))
-    best = jnp.maximum(best, best_over(query, split_meta(from_next, width)))
-    best = jnp.maximum(best, best_over(query, split_meta(far_a, width)))
-    best = jnp.maximum(best, best_over(query, split_meta(far_b, width)))
+    for block in (prev_b, next_a, prev_a, next_b, far_b, far_a):
+        best = jnp.maximum(best, best_over(query, split_meta(block, width)))
     answer = jnp.where(best > -1.5, best, -1.0)
-    returned = lax.all_to_all(answer, ("dp", "blk"), split_axis=0, concat_axis=0, tiled=True)
+    returned = lax.all_to_all(
+        answer.reshape(devices, 4), ("dp", "blk"), split_axis=0, concat_axis=0, tiled=False
+    ).reshape(slots)
     pick = target[:, None] == jnp.arange(slots, dtype=jnp.int32)[None, :]
     return jnp.max(jnp.where(pick, returned[None, :], -jnp.inf), axis=1)
 

time: 79.8 us -> 80.4 us (level)
  waiting for transfers between devices: 26.6 us -> 17.7 us
  matrix products: 3.26 us -> 6.68 us
  other arithmetic: 8.88 us -> 12.1 us
  starting transfers between devices: 9.56 us -> 11.7 us
    ppermute x4 -> x6, waiting for transfers between devices: 16.8 us -> 7.9 us  [the longest x1 2.92 us: body(): far_b = lax.ppermute(prev_b, ('dp', 'blk'), forward)]
    dot_general x5 -> x7, matrix products: 2.83 us -> 6.24 us  [best_over(): lax.dot_general(query_rows, key_rows, (((1,), (1,)), ((), ())), preferred...]
    sub x5 -> x7, other arithmetic: 1.32 us -> 4.51 us  [split_meta(): cluster = rows[:, width].astype(jnp.float32) - 1.0]
    ppermute x4 -> x6, starting transfers between devices: 3.87 us -> 6 us  [the longest x1 2.26 us: body(): next_b = lax.ppermute(own_b, ('dp', 'blk'), backward)]
  transfers between devices with their start and end apart: 5 -> 7, of which waited for: 4 -> 5; matrix products, arithmetic and copies ran while one was open for 4% -> 12% of each run, Pallas kernels for 0% -> 0%
where the time goes in v3:
time: 80.4 us; the launch traced here: 79.8 us
  blocking collectives  29.2 us (36%)
  waiting for transfers between devices  17.7 us (22%)
  other arithmetic  12.1 us (15%)
  starting transfers between devices  11.7 us (15%)
  matrix products  6.68 us (8%)
  local copies, waits for them, and re-layouts  2.3 us (3%)
    all_to_all x1, blocking collectives, body(): lax.all_to_all(send, ('dp', 'blk'), split_axis=0, concat_axis=0, tiled=True)  29.2 us
    all_to_all x1, waiting for transfers between devices, body(): lax.all_to_all(answer.reshape(devices, 4), ('dp', 'blk'), split_axis=0, c...  9.76 us
    dot_general x7, matrix products, best_over(): lax.dot_general(query_rows, key_rows, (((1,), (1,)), ((), ())), preferred...  6.24 us
    all_to_all x1, starting transfers between devices, body(): lax.all_to_all(answer.reshape(devices, 4), ('dp', 'blk'), split_axis=0, c...  5.69 us
    sub x7, other arithmetic, split_meta(): cluster = rows[:, width].astype(jnp.float32) - 1.0  4.51 us
    ppermute x1, waiting for transfers between devices, body(): far_b = lax.ppermute(prev_b, ('dp', 'blk'), forward)  2.92 us
    ppermute x1, waiting for transfers between devices, body(): next_a = lax.ppermute(own_a, ('dp', 'blk'), backward)  2.71 us
    ppermute x1, starting transfers between devices, body(): next_b = lax.ppermute(own_b, ('dp', 'blk'), backward)  2.26 us
  transfers between devices with their start and end apart: 7, of which 5 were waited for; matrix products, arithmetic and copies ran while one was open for 12% of the time, Pallas kernels for 0%

profile of v3, /device:TPU:1, one launch (start us, length us, event | category | flops | bytes accessed | tf_op | source)
XLA Modules:
  0.0 79.8 jit_solution(6317010143416026546)
XLA Ops:
  0.0 0.7 add_convert_fusion
  0.7 0.9 %convert_reduce_fusion = s32[256]{0:T(256)S(1)} fusion(s32[256]{0:T(256)} %bitcast.5), kind=kLoop, calls=%fused_computation.32 | loop fusion | flops 327424 | bytes 2048 | tf_op jit(solution)/shard_map/reduce_sum | solution.py:62
  1.6 0.7 fusion.28
  2.3 1.2 %fusion.7 = f32[256]{0:T(256)S(1)} fusion(bf16[256,768]{1,0:T(8,128)(2,1)} %param.4), kind=kLoop, calls=%fused_computation.17 | loop fusion | flops 589568 | bytes 394240 | tf_op jit(solution)/shard_map/reduce_sum | solution.py:12
  3.5 0.7 fusion.30
  4.5 1.2 %fusion.9 = bf16[256,768]{1,0:T(8,128)(2,1)S(1)} fusion(bf16[256,768]{1,0:T(8,128)(2,1)} %param.4, f32[256]{0:T(256)S(1)} %add_rsqrt_fusion), kind=kLoop, calls=%fused_computation.19 | loop fusion | flops 786432 | bytes 787456 | tf_op jit(solution)/shard_map/convert_element_type | solution.py:14
  6.7 29.2 %all_to_all.18 = bf16[128,4,896]{2,1,0:T(4,128)(2,1)S(1)} all-to-all(bf16[128,4,896]{2,1,0:T(4,128)(2,1)S(1)} %all_to_all.12), channel_id=1, replica_groups=mesh['dp'=32,'blk'=4] {'dp','blk'}, dimensions={0} | all-to-all | bytes 1835008 | tf_op jit(solution)/shard_map/all_to_all | solution.py:74
  36.3 1.1 %collective-permute-start.1 = (bf16[256,896]{1,0:T(8,128)(2,1)S(1)}, bf16[256,896]{1,0:T(8,128)(2,1)S(1)}, u32[]{:S(2)}, u32[]{:S(2)}) collective-permute-start(bf16[256,896]{1,0:T(8,128)(2,1)S(1)} %slice.107), channel_id=1, source_target_pairs={{1,0},{2,1},{3,2},{0,3},{12,4},{13,5},{14,6},{15,7},{9,8},{10,9},{... | collective-permute-start | bytes 1376264 | tf_op jit(solution)/shard_map/ppermute | solution.py:80
  38.0 2.3 %collective-permute-start.3 = (bf16[256,896]{1,0:T(8,128)(2,1)S(1)}, bf16[256,896]{1,0:T(8,128)(2,1)}, u32[]{:S(2)}, u32[]{:S(2)}) collective-permute-start(bf16[256,896]{1,0:T(8,128)(2,1)S(1)} %slice.101), channel_id=1, source_target_pairs={{1,0},{2,1},{3,2},{0,3},{12,4},{13,5},{14,6},{15,7},{9,8},{10,9},{... | collective-permute-start | bytes 1376264 | tf_op jit(solution)/shard_map/ppermute | solution.py:82
  41.4 2.7 %collective-permute-done.1 = bf16[256,896]{1,0:T(8,128)(2,1)S(1)} collective-permute-done((bf16[256,896]{1,0:T(8,128)(2,1)S(1)}, bf16[256,896]{1,0:T(8,128)(2,1)S(1)}, u32[]{:S(2)}, u32[]{:S(2)}) %collective-permute-start.1) | collective-permute-done | bytes 458784 | tf_op jit(solution)/shard_map/ppermute | solution.py:80
  44.1 2.2 %collective-permute-start.5 = (bf16[256,896]{1,0:T(8,128)(2,1)S(1)}, bf16[256,896]{1,0:T(8,128)(2,1)S(1)}, u32[]{:S(2)}, u32[]{:S(2)}) collective-permute-start(bf16[256,896]{1,0:T(8,128)(2,1)S(1)} %collective-permute-done.1), channel_id=1, source_target_pairs={{1,0},{2,1},{3,2},{0,3},{12,4},{13,5},{14,6},{15,7},{9,8},{10,9},{... | collective-permute-start | bytes 1376264 | tf_op jit(solution)/shard_map/ppermute | solution.py:84
  46.5 1.3 %add_reduce_fusion.9 = (f32[256]{0:T(256)S(1)}, f32[256]{0:T(256)S(1)}) fusion(bf16[256,896]{1,0:T(8,128)(2,1)} %collective-permute-done.2), kind=kLoop, calls=%fused_computation.50 | loop fusion | flops 1536 | bytes 3584 | tf_op jit(solution)/shard_map/sub | solution.py:38
  47.8 1.2 %collective-permute-done.3 = bf16[256,896]{1,0:T(8,128)(2,1)} collective-permute-done((bf16[256,896]{1,0:T(8,128)(2,1)S(1)}, bf16[256,896]{1,0:T(8,128)(2,1)}, u32[]{:S(2)}, u32[]{:S(2)}) %collective-permute-start.3) | collective-permute-done | bytes 458784 | tf_op jit(solution)/shard_map/ppermute | solution.py:82
  49.0 1.2 %add_reduce_fusion.7 = (f32[256]{0:T(256)S(1)}, f32[256]{0:T(256)S(1)}) fusion(bf16[256,896]{1,0:T(8,128)(2,1)} %collective-permute-done.3), kind=kLoop, calls=%fused_computation.48 | loop fusion | flops 1536 | bytes 3584 | tf_op jit(solution)/shard_map/sub | solution.py:38
  50.2 1.0 %collective-permute-done = bf16[256,896]{1,0:T(8,128)(2,1)} collective-permute-done((bf16[256,896]{1,0:T(8,128)(2,1)S(1)}, bf16[256,896]{1,0:T(8,128)(2,1)}, u32[]{:S(2)}, u32[]{:S(2)}) %collective-permute-start) | collective-permute-done | bytes 458784 | tf_op jit(solution)/shard_map/ppermute | solution.py:79
  51.2 1.4 %fusion.3 = f32[512]{0:T(512)S(1)} fusion(bf16[256,896]{1,0:T(8,128)(2,1)} %collective-permute-done.2, f32[512]{0:T(512)S(1)} %get-tuple-element.6, f32[512]{0:T(512)S(1)} %get-tuple-element.5, f32[256]{0:T(256)S(1)} %get-tuple-element.12, f32[256]{0:T(256)S(1)} %get-tuple-element.11, bf16[512,896]{1,0:T(8,128)(2,1)S(1)} %all_to_all.14), kind=kOutput, calls=%fused_computation.11 | convolution fusion | flops 201981440 | bytes 1187840 | tf_op jit(solution)/shard_map/dot_general | solution.py:46
  53.1 1.4 %fusion.4 = f32[512]{0:T(512)S(1)} fusion(bf16[256,896]{1,0:T(8,128)(2,1)} %collective-permute-done.3, f32[512]{0:T(512)S(1)} %get-tuple-element.6, f32[512]{0:T(512)S(1)} %get-tuple-element.5, f32[256]{0:T(256)S(1)} %get-tuple-element.14, f32[256]{0:T(256)S(1)} %get-tuple-element.13, bf16[512,896]{1,0:T(8,128)(2,1)S(1)} %all_to_all.14), kind=kOutput, calls=%fused_computation.12 | convolution fusion | flops 201981440 | bytes 1187840 | tf_op jit(solution)/shard_map/dot_general | solution.py:46
  54.5 1.2 %add_reduce_fusion.13 = (f32[256]{0:T(256)S(1)}, f32[256]{0:T(256)S(1)}) fusion(bf16[256,896]{1,0:T(8,128)(2,1)} %collective-permute-done), kind=kLoop, calls=%fused_computation.54 | loop fusion | flops 1536 | bytes 3584 | tf_op jit(solution)/shard_map/sub | solution.py:38
  55.7 1.4 %fusion.1 = f32[512]{0:T(512)S(1)} fusion(bf16[256,896]{1,0:T(8,128)(2,1)} %collective-permute-done, f32[512]{0:T(512)S(1)} %get-tuple-element.6, f32[512]{0:T(512)S(1)} %get-tuple-element.5, f32[256]{0:T(256)S(1)} %get-tuple-element.8, f32[256]{0:T(256)S(1)} %get-tuple-element.7, bf16[512,896]{1,0:T(8,128)(2,1)S(1)} %all_to_all.14), kind=kOutput, calls=%fused_computation.9 | convolution fusion | flops 201981440 | bytes 1187840 | tf_op jit(solution)/shard_map/dot_general | solution.py:46
  57.3 2.9 %collective-permute-done.4 = bf16[256,896]{1,0:T(8,128)(2,1)S(1)} collective-permute-done((bf16[256,896]{1,0:T(8,128)(2,1)}, bf16[256,896]{1,0:T(8,128)(2,1)S(1)}, u32[]{:S(2)}, u32[]{:S(2)}) %collective-permute-start.4) | collective-permute-done | bytes 458784 | tf_op jit(solution)/shard_map/ppermute | solution.py:83
  62.1 5.7 %all-to-all-start.1 = ((f32[128,1,4]{2,1,0:T(1,128)}), f32[128,1,4]{2,1,0:T(1,128)S(1)}, u32[]{:S(2)}, u32[]{:S(2)}) async-start(f32[128,1,4]{2,1,0:T(1,128)} %bitcast.3), calls=%async_computation.1 | async-start | bytes 131072 | tf_op jit(solution)/shard_map/all_to_all | solution.py:90
  67.8 9.8 %all-to-all-done.1 = f32[128,1,4]{2,1,0:T(1,128)S(1)} async-done(((f32[128,1,4]{2,1,0:T(1,128)}), f32[128,1,4]{2,1,0:T(1,128)S(1)}, u32[]{:S(2)}, u32[]{:S(2)}) %all-to-all-start.1) | async-done | bytes 2080 | tf_op jit(solution)/shard_map/all_to_all | solution.py:90
  78.1 0.8 %reduce.31 = f32[128,4]{1,0:T(8,128)S(1)} reduce(f32[128,1,4]{2,1,0:T(1,128)S(1)} %all-to-all-done.1, f32[]{:T(128)} %broadcast.458), dimensions={1}, to_apply=%all_to_all.15.reduce_sub_computation.3 | reduce | bytes 4100 | tf_op jit(solution)/shard_map/all_to_all | solution.py:90
  79.0 0.8 select_reduce_fusion
  (33 shorter events, 6.8 us)
Async XLA Ops:
  36.3 7.8 %collective-permute-start.1 = (bf16[256,896]{1,0:T(8,128)(2,1)S(1)}, bf16[256,896]{1,0:T(8,128)(2,1)S(1)}, u32[]{:S(2)}, u32[]{:S(2)}) collective-permute-start(bf16[256,896]{1,0:T(8,128)(2,1)S(1)} %slice.107), channel_id=1, source_target_pairs={{1,0},{2,1},{3,2},{0,3},{12,4},{13,5},{14,6},{15,7},{9,8},{10,9},{... | collective-permute-start | bytes 1376264 | tf_op jit(solution)/shard_map/ppermute | solution.py:80
  37.4 9.1 %collective-permute-start.2 = (bf16[256,896]{1,0:T(8,128)(2,1)S(1)}, bf16[256,896]{1,0:T(8,128)(2,1)}, u32[]{:S(2)}, u32[]{:S(2)}) collective-permute-start(bf16[256,896]{1,0:T(8,128)(2,1)S(1)} %slice.107), channel_id=1, source_target_pairs={{0,1},{1,2},{2,3},{3,0},{4,12},{5,13},{6,14},{7,15},{8,9},{9,10},{... | collective-permute-start | bytes 1376264 | tf_op jit(solution)/shard_map/ppermute | solution.py:81
  38.0 11.1 %collective-permute-start.3 = (bf16[256,896]{1,0:T(8,128)(2,1)S(1)}, bf16[256,896]{1,0:T(8,128)(2,1)}, u32[]{:S(2)}, u32[]{:S(2)}) collective-permute-start(bf16[256,896]{1,0:T(8,128)(2,1)S(1)} %slice.101), channel_id=1, source_target_pairs={{1,0},{2,1},{3,2},{0,3},{12,4},{13,5},{14,6},{15,7},{9,8},{10,9},{... | collective-permute-start | bytes 1376264 | tf_op jit(solution)/shard_map/ppermute | solution.py:82
  40.2 11.0 %collective-permute-start = (bf16[256,896]{1,0:T(8,128)(2,1)S(1)}, bf16[256,896]{1,0:T(8,128)(2,1)}, u32[]{:S(2)}, u32[]{:S(2)}) collective-permute-start(bf16[256,896]{1,0:T(8,128)(2,1)S(1)} %slice.101), channel_id=1, source_target_pairs={{0,1},{1,2},{2,3},{3,0},{4,12},{5,13},{6,14},{7,15},{8,9},{9,10},{... | collective-permute-start | bytes 1376264 | tf_op jit(solution)/shard_map/ppermute | solution.py:79
  44.1 13.0 %collective-permute-start.5 = (bf16[256,896]{1,0:T(8,128)(2,1)S(1)}, bf16[256,896]{1,0:T(8,128)(2,1)S(1)}, u32[]{:S(2)}, u32[]{:S(2)}) collective-permute-start(bf16[256,896]{1,0:T(8,128)(2,1)S(1)} %collective-permute-done.1), channel_id=1, source_target_pairs={{1,0},{2,1},{3,2},{0,3},{12,4},{13,5},{14,6},{15,7},{9,8},{10,9},{... | collective-permute-start | bytes 1376264 | tf_op jit(solution)/shard_map/ppermute | solution.py:84
  51.2 9.0 %collective-permute-start.4 = (bf16[256,896]{1,0:T(8,128)(2,1)}, bf16[256,896]{1,0:T(8,128)(2,1)S(1)}, u32[]{:S(2)}, u32[]{:S(2)}) collective-permute-start(bf16[256,896]{1,0:T(8,128)(2,1)} %collective-permute-done), channel_id=1, source_target_pairs={{0,1},{1,2},{2,3},{3,0},{4,12},{5,13},{6,14},{7,15},{8,9},{9,10},{... | collective-permute-start | bytes 1376264 | tf_op jit(solution)/shard_map/ppermute | solution.py:83
  60.9 6.9 %copy-start = (s32[256,1]{0,1:T(1,128)S(1)}, s32[256,1]{0,1:T(1,128)}, u32[]{:S(2)}) copy-start(s32[256,1]{0,1:T(1,128)} %param.5) | copy-start | bytes 3076
  62.1 15.5 %all-to-all-start.1 = ((f32[128,1,4]{2,1,0:T(1,128)}), f32[128,1,4]{2,1,0:T(1,128)S(1)}, u32[]{:S(2)}, u32[]{:S(2)}) async-start(f32[128,1,4]{2,1,0:T(1,128)} %bitcast.3), calls=%async_computation.1 | async-start | bytes 131072 | tf_op jit(solution)/shard_map/all_to_all | solution.py:90

commit v4 on v2

v4 whole, which is shorter than its diff:
```python
import numpy as np
import jax
import jax.numpy as jnp
from jax import lax
from jax.sharding import PartitionSpec as P

EXTRA = 128


def normalize(embeddings):
    values = embeddings.astype(jnp.float32)
    scale = lax.rsqrt(jnp.mean(values * values, axis=1, keepdims=True) + 1e-06)
    width = embeddings.shape[1]
    return (values * scale * width ** (-0.5)).astype(jnp.bfloat16)


def ring_of(zs, xs, ys):
    def lin(z, x, c, y):
        return ((z * xs + x) * 2 + c) * ys + y

    nxt = np.zeros(zs * xs * 2 * ys, np.int32)
    ring_pos = np.zeros(zs * xs * 2 * ys, np.int32)
    for z in range(zs):
        for x in range(xs):
            for y in range(ys):
                nxt[lin(z, x, 0, y)] = lin(z, x, 0, (y + 1) % ys)
                nxt[lin(z, x, 1, y)] = lin(z, (x + 1) % xs, 1, y)
                ring_pos[lin(z, x, 0, y)] = y
                ring_pos[lin(z, x, 1, y)] = x
    return nxt, ring_pos


def device_of(group, place, zs, xs, ys):
    first = group * 2 * ys + place
    other = group - zs * xs
    second = ((other // ys * xs + place) * 2 + 1) * ys + other % ys
    return jnp.where(group < zs * xs, first, second)


def split_meta(rows, width):
    cluster = rows[:, width].astype(jnp.float32) - 1.0
    order = rows[:, width + 1].astype(jnp.float32) * 256.0 + rows[:, width + 2].astype(jnp.float32)
    return rows[:, :width], cluster, order


def masks(query, keys):
    query_rows, query_cluster, query_order = query
    key_rows, key_cluster, key_order = keys
    scores = lax.dot_general(
        query_rows, key_rows, (((1,), (1,)), ((), ())), preferred_element_type=jnp.float32
    )
    same = query_cluster[:, None] == key_cluster[None, :]
    return scores, same, key_order[None, :] < query_order[:, None]


def best_over(query, keys):
    scores, same, earlier = masks(query, keys)
    return jnp.max(jnp.where(same & earlier, scores, -2.0), axis=1)


def body(embeddings, point_group, point_cluster, point_order, nxt, ring_pos, dims):
    zs, xs, ys = dims
    devices = nxt.shape[0]
    points, width = embeddings.shape
    slots = devices * 4
    unit = normalize(embeddings)
    group = point_group[:, 0]
    index = jnp.arange(points, dtype=jnp.int32)
    same = (group[:, None] == group[None, :]) & (index[None, :] < index[:, None])
    rank = jnp.sum(same.astype(jnp.int32), axis=1)
    place = rank // 4
    target = device_of(group, place, zs, xs, ys) * 4 + rank % 4
    meta = jnp.stack(
        [point_cluster + 1, point_order // 256, point_order % 256], axis=1
    ).astype(jnp.bfloat16)
    packed = jnp.concatenate(
        [unit, meta, jnp.zeros((points, EXTRA - 3), jnp.bfloat16)], axis=1
    )
    spot = (target[None, :] == jnp.arange(slots, dtype=jnp.int32)[:, None]).astype(jnp.bfloat16)
    send = lax.dot_general(
        spot, packed, (((1,), (0,)), ((), ())), preferred_element_type=jnp.float32
    ).astype(jnp.bfloat16)
    own = lax.all_to_all(send, ("dp", "blk"), split_axis=0, concat_axis=0, tiled=True)
    forward = [(i, int(nxt[i])) for i in range(devices)]
    backward = [(int(nxt[i]), i) for i in range(devices)]
    prev = lax.ppermute(own, ("dp", "blk"), forward)
    next_ = lax.ppermute(own, ("dp", "blk"), backward)
    query = split_meta(own, width)
    best = best_over(query, query)
    best = jnp.maximum(best, best_over(query, split_meta(prev, width)))
    best = jnp.maximum(best, best_over(query, split_meta(next_, width)))
    half = slots // 2
    me = jnp.asarray(ring_pos)[lax.axis_index(("dp", "blk"))]
    inner = (me == 1) | (me == 2)
    rows = jnp.where(inner, prev[:half], next_[half:])
    cols = jnp.where(inner, next_, prev)
    scores, same_c, earlier = masks(split_meta(rows, width), split_meta(cols, width))
    row_part = jnp.max(jnp.where(same_c & earlier, scores, -2.0), axis=1)
    col_order_r = split_meta(rows, width)[2]
    col_order_c = split_meta(cols, width)[2]
    col_ok = same_c & (col_order_r[:, None] < col_order_c[None, :])
    col_part = jnp.max(jnp.where(col_ok, scores, -2.0), axis=0)
    floor = jnp.full((half,), -2.0, jnp.float32)
    side_prev = jnp.where(inner, jnp.concatenate([row_part, floor]), col_part)
    side_next = jnp.where(inner, col_part, jnp.concatenate([floor, row_part]))
    payload = jnp.stack(
        [best.reshape(devices, 4), side_prev.reshape(devices, 4), side_next.reshape(devices, 4)],
        axis=1,
    ).reshape(devices, 12)
    returned = lax.all_to_all(
        payload, ("dp", "blk"), split_axis=0, concat_axis=0, tiled=True
    ).reshape(devices * 12)
    lane = rank % 4
    at_own = device_of(group, place, zs, xs, ys) * 12 + lane
    at_prev = device_of(group, (place + 3) % 4, zs, xs, ys) * 12 + 8 + lane
    at_next = device_of(group, (place + 1) % 4, zs, xs, ys) * 12 + 4 + lane
    entry = jnp.arange(devices * 12, dtype=jnp.int32)[None, :]
    pick = (entry == at_own[:, None]) | (entry == at_prev[:, None]) | (entry == at_next[:, None])
    found = jnp.max(jnp.where(pick, returned[None, :], -2.0), axis=1)
    return jnp.where(found > -1.5, found, -1.0)


def solution(mesh):
    dims = (4, 4, 4)
    nxt, ring_pos = ring_of(*dims)
    in_specs = (P(("dp", "blk"), None), P(("dp", "blk"), None), P(("dp", "blk")), P(("dp", "blk")))
    out_specs = P(("dp", "blk"))

    def run(embeddings, point_group, point_cluster, point_order):
        return body(embeddings, point_group, point_cluster, point_order, nxt, ring_pos, dims)

    return jax.shard_map(run, mesh=mesh, in_specs=in_specs, out_specs=out_specs, check_vma=False)
```

time: 79.8 us -> 72.9 us (0.914)
  waiting for transfers between devices: 26.6 us -> 17.8 us
  local copies, waits for them, and re-layouts: 1.84 us -> 3.52 us
  between operations: 0.16 us -> 1.52 us
    ppermute x4 -> x2, waiting for transfers between devices: 16.8 us -> 8.18 us  [the longest x1 8.18 us: body(): prev = lax.ppermute(own, ('dp', 'blk'), forward)]
    ppermute x4 -> x2, starting transfers between devices: 3.87 us -> 2.74 us  [the longest x1 2.66 us: body(): next_ = lax.ppermute(own, ('dp', 'blk'), backward)]
    dot_general x6 -> x5, matrix products: 3.26 us -> 3.01 us  [the longest x4 2.58 us: masks(): lax.dot_general(query_rows, key_rows, (((1,), (1,)), ((), ())), preferred...]
  transfers between devices with their start and end apart: 5 -> 3, of which waited for: 4 -> 2; matrix products, arithmetic and copies ran while one was open for 4% -> 3% of each run, Pallas kernels for 0% -> 0%
where the time goes in v4:
time: 72.9 us; the launch traced here: 72.6 us
  blocking collectives  29.2 us (40%)
  waiting for transfers between devices  17.8 us (24%)
  starting transfers between devices  9.15 us (13%)
  other arithmetic  8.35 us (11%)
  local copies, waits for them, and re-layouts  3.52 us (5%)
  matrix products  3.01 us (4%)
  between operations  1.52 us (2%)
    all_to_all x1, blocking collectives, body(): lax.all_to_all(send, ('dp', 'blk'), split_axis=0, concat_axis=0, tiled=True)  29.2 us
    all_to_all x1, waiting for transfers between devices, body(): lax.all_to_all(payload, ('dp', 'blk'), split_axis=0, concat_axis=0, tiled...  9.63 us
    ppermute x1, waiting for transfers between devices, body(): prev = lax.ppermute(own, ('dp', 'blk'), forward)  8.18 us
    all_to_all x1, starting transfers between devices, body(): lax.all_to_all(payload, ('dp', 'blk'), split_axis=0, concat_axis=0, tiled...  6.41 us
    ppermute x1, starting transfers between devices, body(): next_ = lax.ppermute(own, ('dp', 'blk'), backward)  2.66 us
    dot_general x4, matrix products, masks(): lax.dot_general(query_rows, key_rows, (((1,), (1,)), ((), ())), preferred...  2.58 us
  transfers between devices with their start and end apart: 3, of which 2 were waited for; matrix products, arithmetic and copies ran while one was open for 3% of the time, Pallas kernels for 0%

profile of v4, /device:TPU:1, one launch (start us, length us, event | category | flops | bytes accessed | tf_op | source)
XLA Modules:
  0.0 72.6 jit_solution(13960368207078946737)
XLA Ops:
  0.0 0.9 %convert_reduce_fusion = s32[256]{0:T(256)S(1)} fusion(s32[256]{0:T(256)} %bitcast.9), kind=kLoop, calls=%fused_computation.42 | loop fusion | flops 327424 | bytes 2048 | tf_op jit(solution)/shard_map/reduce_sum | solution.py:70
  0.9 0.7 fusion.19
  1.6 0.7 fusion.23
  2.5 1.2 %fusion.5 = f32[256]{0:T(256)S(1)} fusion(bf16[256,768]{1,0:T(8,128)(2,1)} %param.5), kind=kLoop, calls=%fused_computation.16 | loop fusion | flops 589568 | bytes 394240 | tf_op jit(solution)/shard_map/reduce_sum | solution.py:12
  3.7 1.2 %fusion.7 = bf16[256,768]{1,0:T(8,128)(2,1)S(1)} fusion(bf16[256,768]{1,0:T(8,128)(2,1)} %param.5, f32[256]{0:T(256)S(1)} %add_rsqrt_fusion), kind=kLoop, calls=%fused_computation.18 | loop fusion | flops 786432 | bytes 787456 | tf_op jit(solution)/shard_map/convert_element_type | solution.py:14
  5.0 0.3 concatenate.10
  5.3 0.4 convolution_convert_fusion
  6.0 29.2 %all_to_all.21 = bf16[128,4,896]{2,1,0:T(4,128)(2,1)S(1)} all-to-all(bf16[128,4,896]{2,1,0:T(4,128)(2,1)S(1)} %all_to_all.14), channel_id=1, replica_groups=mesh['dp'=32,'blk'=4] {'dp','blk'}, dimensions={0} | all-to-all | bytes 1835008 | tf_op jit(solution)/shard_map/all_to_all | solution.py:83
  35.5 2.7 %collective-permute-start.1 = (bf16[512,896]{1,0:T(8,128)(2,1)S(1)}, bf16[512,896]{1,0:T(8,128)(2,1)S(1)}, u32[]{:S(2)}, u32[]{:S(2)}) collective-permute-start(bf16[512,896]{1,0:T(8,128)(2,1)S(1)} %all_to_all.16), channel_id=1, source_target_pairs={{1,0},{2,1},{3,2},{0,3},{12,4},{13,5},{14,6},{15,7},{9,8},{10,9},{... | collective-permute-start | bytes 2752520 | tf_op jit(solution)/shard_map/ppermute | solution.py:87
  38.2 0.6 dynamic_slice.3
  40.1 0.3 add_reduce_fusion.7
  40.4 0.7 fusion.2
  41.1 8.2 %collective-permute-done = bf16[512,896]{1,0:T(8,128)(2,1)S(1)} collective-permute-done((bf16[512,896]{1,0:T(8,128)(2,1)S(1)}, bf16[512,896]{1,0:T(8,128)(2,1)S(1)}, u32[]{:S(2)}, u32[]{:S(2)}) %collective-permute-start) | collective-permute-done | bytes 917536 | tf_op jit(solution)/shard_map/ppermute | solution.py:86
  49.6 0.3 add_reduce_fusion.3
  49.9 0.7 fusion.3
  50.5 0.7 fusion.4
  52.1 0.6 select_reduce_fusion.2
  53.1 0.7 %copy.30 = f32[128,1,12]{2,1,0:T(1,128)} copy(f32[128,1,12]{0,2,1:T(8,128)S(1)} %all_to_all.17) | data formatting | bytes 12288 | tf_op jit(solution)/shard_map/all_to_all | solution.py:110
  53.9 6.4 %all-to-all-start.1 = ((f32[128,1,12]{2,1,0:T(1,128)}), f32[128,1,12]{2,1,0:T(1,128)S(1)}, u32[]{:S(2)}, u32[]{:S(2)}) async-start(f32[128,1,12]{2,1,0:T(1,128)} %copy.30), calls=%async_computation.1 | async-start | bytes 131072 | tf_op jit(solution)/shard_map/all_to_all | solution.py:110
  60.3 9.6 %all-to-all-done.1 = f32[128,1,12]{2,1,0:T(1,128)S(1)} async-done(((f32[128,1,12]{2,1,0:T(1,128)}), f32[128,1,12]{2,1,0:T(1,128)S(1)}, u32[]{:S(2)}, u32[]{:S(2)}) %all-to-all-start.1) | async-done | bytes 6176 | tf_op jit(solution)/shard_map/all_to_all | solution.py:110
  70.0 0.5 broadcast.689
  70.5 0.8 %reduce.23 = f32[128,12]{1,0:T(8,128)S(1)} reduce(f32[128,1,12]{2,1,0:T(1,128)S(1)} %all-to-all-done.1, f32[]{:T(128)} %broadcast.689), dimensions={1}, to_apply=%all_to_all.18.reduce_sub_computation.3 | reduce | bytes 12292 | tf_op jit(solution)/shard_map/all_to_all | solution.py:110
  71.4 0.6 select_reduce_fusion
  72.0 0.6 compare_select_fusion.4
  (34 shorter events, 2.6 us)
Async XLA Ops:
  0.0 4.9 %copy-start.1 = (s32[256]{0:T(256)S(1)}, s32[256]{0:T(256)}, u32[]{:S(2)}) copy-start(s32[256]{0:T(256)} %param.7) | copy-start | bytes 3076
  35.2 3.0 %copy-start.2 = (s32[128]{0:T(128)S(1)}, s32[128]{0:T(128)}, u32[]{:S(2)}) copy-start(s32[128]{0:T(128)} %constant.154.clone) | copy-start | bytes 1540
  35.2 4.9 %copy-start = (s32[256,1]{0,1:T(1,128)S(1)}, s32[256,1]{0,1:T(1,128)}, u32[]{:S(2)}) copy-start(s32[256,1]{0,1:T(1,128)} %param.6) | copy-start | bytes 3076
  35.4 13.8 %collective-permute-start = (bf16[512,896]{1,0:T(8,128)(2,1)S(1)}, bf16[512,896]{1,0:T(8,128)(2,1)S(1)}, u32[]{:S(2)}, u32[]{:S(2)}) collective-permute-start(bf16[512,896]{1,0:T(8,128)(2,1)S(1)} %all_to_all.16), channel_id=1, source_target_pairs={{0,1},{1,2},{2,3},{3,0},{4,12},{5,13},{6,14},{7,15},{8,9},{9,10},{... | collective-permute-start | bytes 2752520 | tf_op jit(solution)/shard_map/ppermute | solution.py:86
  35.5 14.0 %collective-permute-start.1 = (bf16[512,896]{1,0:T(8,128)(2,1)S(1)}, bf16[512,896]{1,0:T(8,128)(2,1)S(1)}, u32[]{:S(2)}, u32[]{:S(2)}) collective-permute-start(bf16[512,896]{1,0:T(8,128)(2,1)S(1)} %all_to_all.16), channel_id=1, source_target_pairs={{1,0},{2,1},{3,2},{0,3},{12,4},{13,5},{14,6},{15,7},{9,8},{10,9},{... | collective-permute-start | bytes 2752520 | tf_op jit(solution)/shard_map/ppermute | solution.py:87
  53.9 16.1 %all-to-all-start.1 = ((f32[128,1,12]{2,1,0:T(1,128)}), f32[128,1,12]{2,1,0:T(1,128)S(1)}, u32[]{:S(2)}, u32[]{:S(2)}) async-start(f32[128,1,12]{2,1,0:T(1,128)} %copy.30), calls=%async_computation.1 | async-start | bytes 131072 | tf_op jit(solution)/shard_map/all_to_all | solution.py:110

commit v5 on v4

--- a/solution.py
+++ b/solution.py
@@ -3,6 +3,7 @@
 import jax.numpy as jnp
 from jax import lax
 from jax.sharding import PartitionSpec as P
+from jax.experimental import pallas as pl
 
 EXTRA = 128
 
@@ -37,6 +38,73 @@
     return jnp.where(group < zs * xs, first, second)
 
 
+def place_of(group, place, zs, xs, ys):
+    first = group * 2 * ys + place
+    other = group - zs * xs
+    second = (((other >> 2) * xs + place) * 2 + 1) * ys + (other & 3)
+    return jnp.where(group < zs * xs, first, second)
+
+
+def prologue(dims):
+    zs, xs, ys = dims
+
+    def kernel(emb_ref, meta_ref, send_ref, idx_ref):
+        x = emb_ref[...].astype(jnp.float32)
+        width = x.shape[1]
+        points = x.shape[0]
+        slots = send_ref.shape[0]
+        scale = lax.rsqrt(jnp.mean(x * x, axis=1, keepdims=True) + 1e-06)
+        unit = (x * scale * width ** (-0.5)).astype(jnp.bfloat16)
+        rows = meta_ref[...]
+        cols = rows.T
+        group_col = cols[:, 3:4]
+        below = lax.broadcasted_iota(jnp.int32, (points, points), 1) < lax.broadcasted_iota(
+            jnp.int32, (points, points), 0
+        )
+        same = (group_col == rows[3:4, :]) & below
+        rank = jnp.sum(same.astype(jnp.float32), axis=1, keepdims=True).astype(jnp.int32)
+        group = group_col.astype(jnp.int32)
+        place = rank >> 2
+        lane = rank & 3
+        dev = place_of(group, place, zs, xs, ys)
+        target = dev * 4 + lane
+        spot = (target == lax.broadcasted_iota(jnp.int32, (points, slots), 1)).astype(jnp.float32)
+        spot = spot.T.astype(jnp.bfloat16)
+        send_ref[:, :width] = jnp.dot(spot, unit, preferred_element_type=jnp.float32).astype(
+            jnp.bfloat16
+        )
+        send_ref[:, width:] = jnp.dot(
+            spot, cols.astype(jnp.bfloat16), preferred_element_type=jnp.float32
+        ).astype(jnp.bfloat16)
+        at_own = dev * 12 + lane
+        at_prev = place_of(group, (place + 3) & 3, zs, xs, ys) * 12 + 8 + lane
+        at_next = place_of(group, (place + 1) & 3, zs, xs, ys) * 12 + 4 + lane
+        which = lax.broadcasted_iota(jnp.int32, idx_ref.shape, 1)
+        idx_ref[...] = jnp.where(which == 0, at_own, jnp.where(which == 1, at_prev, at_next))
+
+    return kernel
+
+
+def build_send(embeddings, group, point_cluster, point_order, slots, dims, interpret=False):
+    points, width = embeddings.shape
+    meta = jnp.concatenate(
+        [
+            jnp.stack([point_cluster + 1, point_order // 256, point_order % 256, group]).astype(
+                jnp.float32
+            ),
+            jnp.zeros((EXTRA - 4, points), jnp.float32),
+        ]
+    )
+    return pl.pallas_call(
+        prologue(dims),
+        out_shape=(
+            jax.ShapeDtypeStruct((slots, width + EXTRA), jnp.bfloat16),
+            jax.ShapeDtypeStruct((points, 128), jnp.int32),
+        ),
+        interpret=interpret,
+    )(embeddings, meta)
+
+
 def split_meta(rows, width):
     cluster = rows[:, width].astype(jnp.float32) - 1.0
     order = rows[:, width + 1].astype(jnp.float32) * 256.0 + rows[:, width + 2].astype(jnp.float32)
@@ -63,23 +131,8 @@
     devices = nxt.shape[0]
     points, width = embeddings.shape
     slots = devices * 4
-    unit = normalize(embeddings)
     group = point_group[:, 0]
-    index = jnp.arange(points, dtype=jnp.int32)
-    same = (group[:, None] == group[None, :]) & (index[None, :] < index[:, None])
-    rank = jnp.sum(same.astype(jnp.int32), axis=1)
-    place = rank // 4
-    target = device_of(group, place, zs, xs, ys) * 4 + rank % 4
-    meta = jnp.stack(
-        [point_cluster + 1, point_order // 256, point_order % 256], axis=1
-    ).astype(jnp.bfloat16)
-    packed = jnp.concatenate(
-        [unit, meta, jnp.zeros((points, EXTRA - 3), jnp.bfloat16)], axis=1
-    )
-    spot = (target[None, :] == jnp.arange(slots, dtype=jnp.int32)[:, None]).astype(jnp.bfloat16)
-    send = lax.dot_general(
-        spot, packed, (((1,), (0,)), ((), ())), preferred_element_type=jnp.float32
-    ).astype(jnp.bfloat16)
+    send, idx = build_send(embeddings, group, point_cluster, point_order, slots, dims)
     own = lax.all_to_all(send, ("dp", "blk"), split_axis=0, concat_axis=0, tiled=True)
     forward = [(i, int(nxt[i])) for i in range(devices)]
     backward = [(int(nxt[i]), i) for i in range(devices)]
@@ -110,10 +163,7 @@
     returned = lax.all_to_all(
         payload, ("dp", "blk"), split_axis=0, concat_axis=0, tiled=True
     ).reshape(devices * 12)
-    lane = rank % 4
-    at_own = device_of(group, place, zs, xs, ys) * 12 + lane
-    at_prev = device_of(group, (place + 3) % 4, zs, xs, ys) * 12 + 8 + lane
-    at_next = device_of(group, (place + 1) % 4, zs, xs, ys) * 12 + 4 + lane
+    at_own, at_prev, at_next = idx[:, 0], idx[:, 1], idx[:, 2]
     entry = jnp.arange(devices * 12, dtype=jnp.int32)[None, :]
     pick = (entry == at_own[:, None]) | (entry == at_prev[:, None]) | (entry == at_next[:, None])
     found = jnp.max(jnp.where(pick, returned[None, :], -2.0), axis=1)

time: 72.9 us -> 73.5 us (level)
  Pallas kernels: 0 us -> 2.89 us
  starting transfers between devices: 9.15 us -> 6.37 us
  other arithmetic: 8.35 us -> 5.7 us
  local copies, waits for them, and re-layouts: 3.52 us -> 5.39 us
  waiting for transfers between devices: 17.8 us -> 19.6 us
    ppermute x1, waiting for transfers between devices: 0.01 us -> 8.23 us  [body(): next_ = lax.ppermute(own, ('dp', 'blk'), backward)]
    ppermute x1, waiting for transfers between devices: 8.18 us -> 1.89 us  [body(): prev = lax.ppermute(own, ('dp', 'blk'), forward)]
    pallas_call x0 -> x1, Pallas kernels: none -> 2.89 us  [build_send(): pl.pallas_call(prologue(dims), out_shape=(jax.ShapeDtypeStruct((slots, wi...]
    reduce_sum x2 -> x0, other arithmetic: 2.08 us -> none  [the longest x1 1.15 us: normalize(): scale = lax.rsqrt(jnp.mean(values * values, axis=1, keepdims=True) + 1e-06)]
    ppermute x1, starting transfers between devices: 2.66 us -> 1.05 us  [body(): next_ = lax.ppermute(own, ('dp', 'blk'), backward)]
    all_to_all x1, starting transfers between devices: 6.41 us -> 4.83 us  [body(): lax.all_to_all(payload, ('dp', 'blk'), split_axis=0, concat_axis=0, tiled...]
    all_to_all x2, local copies, waits for them, and re-layouts: 0.42 us -> 1.99 us  [body(): lax.all_to_all(send, ('dp', 'blk'), split_axis=0, concat_axis=0, tiled=True)]
  transfers between devices with their start and end apart: 3 -> 3, of which waited for: 2 -> 3; matrix products, arithmetic and copies ran while one was open for 3% -> 3% of each run, Pallas kernels for 0% -> 0%
where the time goes in v5:
time: 73.5 us; the launch traced here: 73.2 us
  blocking collectives  29.2 us (40%)
  waiting for transfers between devices  19.6 us (27%)
  starting transfers between devices  6.37 us (9%)
  other arithmetic  5.7 us (8%)
  local copies, waits for them, and re-layouts  5.39 us (7%)
  Pallas kernels  2.89 us (4%)
  matrix products  2.58 us (4%)
  between operations  1.43 us (2%)
    all_to_all x1, blocking collectives, body(): lax.all_to_all(send, ('dp', 'blk'), split_axis=0, concat_axis=0, tiled=True)  29.2 us
    all_to_all x1, waiting for transfers between devices, body(): lax.all_to_all(payload, ('dp', 'blk'), split_axis=0, concat_axis=0, tiled...  9.53 us
    ppermute x1, waiting for transfers between devices, body(): next_ = lax.ppermute(own, ('dp', 'blk'), backward)  8.23 us
    all_to_all x1, starting transfers between devices, body(): lax.all_to_all(payload, ('dp', 'blk'), split_axis=0, concat_axis=0, tiled...  4.83 us
    pallas_call x1, Pallas kernels, build_send(): pl.pallas_call(prologue(dims), out_shape=(jax.ShapeDtypeStruct((slots, wi...  2.89 us
    dot_general x4, matrix products, masks(): lax.dot_general(query_rows, key_rows, (((1,), (1,)), ((), ())), preferred...  2.58 us
    all_to_all x2, local copies, waits for them, and re-layouts, body(): lax.all_to_all(send, ('dp', 'blk'), split_axis=0, concat_axis=0, tiled=True)  1.99 us
    ppermute x1, waiting for transfers between devices, body(): prev = lax.ppermute(own, ('dp', 'blk'), forward)  1.89 us
  transfers between devices with their start and end apart: 3, of which 3 were waited for; matrix products, arithmetic and copies ran while one was open for 3% of the time, Pallas kernels for 0%

profile of v5, /device:TPU:1, one launch (start us, length us, event | category | flops | bytes accessed | tf_op | source)
XLA Modules:
  0.0 73.2 jit_solution(14176769976682717935)
XLA Ops:
  0.0 0.7 broadcast_add_fusion
  0.7 0.7 and_select_fusion.1
  1.4 0.7 add_convert_fusion
  2.1 0.7 concatenate.9.meta_ref
  2.7 2.9 %shard_map.55 = (bf16[512,896]{1,0:T(8,128)(2,1)}, s32[256,128]{1,0:T(8,128)}) custom-call(bf16[256,768]{1,0:T(8,128)(2,1)} %emb_ref.1, f32[128,256]{1,0:T(8,128)} %concatenate.9.meta_ref), custom_call_target="tpu_custom_call" | custom-call | tf_op jit(solution)/shard_map/pallas_call | solution.py:98
  5.6 1.8 %all_to_all.14 = bf16[128,4,896]{2,1,0:T(4,128)(2,1)S(1)} reshape(bf16[512,896]{1,0:T(8,128)(2,1)} %get-tuple-element.8) | data formatting | bytes 1835008 | tf_op jit(solution)/shard_map/all_to_all | solution.py:136
  7.4 29.2 %all_to_all.21 = bf16[128,4,896]{2,1,0:T(4,128)(2,1)S(1)} all-to-all(bf16[128,4,896]{2,1,0:T(4,128)(2,1)S(1)} %all_to_all.14), channel_id=1, replica_groups=mesh['dp'=32,'blk'=4] {'dp','blk'}, dimensions={0} | all-to-all | bytes 1835008 | tf_op jit(solution)/shard_map/all_to_all | solution.py:136
  36.8 1.1 %collective-permute-start.1 = (bf16[512,896]{1,0:T(8,128)(2,1)S(1)}, bf16[512,896]{1,0:T(8,128)(2,1)S(1)}, u32[]{:S(2)}, u32[]{:S(2)}) collective-permute-start(bf16[512,896]{1,0:T(8,128)(2,1)S(1)} %all_to_all.16), channel_id=1, source_target_pairs={{1,0},{2,1},{3,2},{0,3},{12,4},{13,5},{14,6},{15,7},{9,8},{10,9},{... | collective-permute-start | bytes 2752520 | tf_op jit(solution)/shard_map/ppermute | solution.py:140
  37.9 0.5 collective-permute-start
  38.4 0.6 dynamic_slice.3
  40.6 0.7 fusion.2
  41.2 8.2 %collective-permute-done.1 = bf16[512,896]{1,0:T(8,128)(2,1)S(1)} collective-permute-done((bf16[512,896]{1,0:T(8,128)(2,1)S(1)}, bf16[512,896]{1,0:T(8,128)(2,1)S(1)}, u32[]{:S(2)}, u32[]{:S(2)}) %collective-permute-start.1) | collective-permute-done | bytes 917536 | tf_op jit(solution)/shard_map/ppermute | solution.py:140
  49.7 1.9 %collective-permute-done = bf16[512,896]{1,0:T(8,128)(2,1)S(1)} collective-permute-done((bf16[512,896]{1,0:T(8,128)(2,1)S(1)}, bf16[512,896]{1,0:T(8,128)(2,1)S(1)}, u32[]{:S(2)}, u32[]{:S(2)}) %collective-permute-start) | collective-permute-done | bytes 917536 | tf_op jit(solution)/shard_map/ppermute | solution.py:139
  51.9 0.7 fusion.4
  52.6 0.6 fusion.3
  53.9 0.3 add_reduce_fusion.1
  54.2 0.6 select_reduce_fusion.2
  55.2 0.7 %copy.18 = f32[128,1,12]{2,1,0:T(1,128)} copy(f32[128,1,12]{0,2,1:T(8,128)S(1)} %all_to_all.17) | data formatting | bytes 12288 | tf_op jit(solution)/shard_map/all_to_all | solution.py:163
  55.9 4.8 %all-to-all-start.1 = ((f32[128,1,12]{2,1,0:T(1,128)}), f32[128,1,12]{2,1,0:T(1,128)S(1)}, u32[]{:S(2)}, u32[]{:S(2)}) async-start(f32[128,1,12]{2,1,0:T(1,128)} %copy.18), calls=%async_computation.1 | async-start | bytes 131072 | tf_op jit(solution)/shard_map/all_to_all | solution.py:163
  61.1 9.5 %all-to-all-done.1 = f32[128,1,12]{2,1,0:T(1,128)S(1)} async-done(((f32[128,1,12]{2,1,0:T(1,128)}), f32[128,1,12]{2,1,0:T(1,128)S(1)}, u32[]{:S(2)}, u32[]{:S(2)}) %all-to-all-start.1) | async-done | bytes 6176 | tf_op jit(solution)/shard_map/all_to_all | solution.py:163
  70.6 0.5 broadcast.135
  71.1 0.8 %reduce.29 = f32[128,12]{1,0:T(8,128)S(1)} reduce(f32[128,1,12]{2,1,0:T(1,128)S(1)} %all-to-all-done.1, f32[]{:T(128)} %broadcast.135), dimensions={1}, to_apply=%all_to_all.18.reduce_sub_computation.3 | reduce | bytes 12292 | tf_op jit(solution)/shard_map/all_to_all | solution.py:163
  72.0 0.6 select_reduce_fusion
  72.6 0.6 compare_select_fusion
  (23 shorter events, 2.5 us)
Async XLA Ops:
  36.6 1.8 %copy-start.1 = (s32[128]{0:T(128)S(1)}, s32[128]{0:T(128)}, u32[]{:S(2)}) copy-start(s32[128]{0:T(128)} %constant.72.clone) | copy-start | bytes 1540
  36.8 12.6 %collective-permute-start.1 = (bf16[512,896]{1,0:T(8,128)(2,1)S(1)}, bf16[512,896]{1,0:T(8,128)(2,1)S(1)}, u32[]{:S(2)}, u32[]{:S(2)}) collective-permute-start(bf16[512,896]{1,0:T(8,128)(2,1)S(1)} %all_to_all.16), channel_id=1, source_target_pairs={{1,0},{2,1},{3,2},{0,3},{12,4},{13,5},{14,6},{15,7},{9,8},{10,9},{... | collective-permute-start | bytes 2752520 | tf_op jit(solution)/shard_map/ppermute | solution.py:140
  37.9 13.8 %collective-permute-start = (bf16[512,896]{1,0:T(8,128)(2,1)S(1)}, bf16[512,896]{1,0:T(8,128)(2,1)S(1)}, u32[]{:S(2)}, u32[]{:S(2)}) collective-permute-start(bf16[512,896]{1,0:T(8,128)(2,1)S(1)} %all_to_all.16), channel_id=1, source_target_pairs={{0,1},{1,2},{2,3},{3,0},{4,12},{5,13},{6,14},{7,15},{8,9},{9,10},{... | collective-permute-start | bytes 2752520 | tf_op jit(solution)/shard_map/ppermute | solution.py:139
  54.2 6.6 %copy-start = (s32[256,128]{1,0:T(8,128)S(1)}, s32[256,128]{1,0:T(8,128)}, u32[]{:S(2)}) copy-start(s32[256,128]{1,0:T(8,128)} %get-tuple-element.7) | copy-start | bytes 393220
  55.9 14.6 %all-to-all-start.1 = ((f32[128,1,12]{2,1,0:T(1,128)}), f32[128,1,12]{2,1,0:T(1,128)S(1)}, u32[]{:S(2)}, u32[]{:S(2)}) async-start(f32[128,1,12]{2,1,0:T(1,128)} %copy.18), calls=%async_computation.1 | async-start | bytes 131072 | tf_op jit(solution)/shard_map/all_to_all | solution.py:163

commit v6 on v5

--- a/solution.py
+++ b/solution.py
@@ -48,61 +48,68 @@
 def prologue(dims):
     zs, xs, ys = dims
 
-    def kernel(emb_ref, meta_ref, send_ref, idx_ref):
+    def kernel(emb_ref, group_ref, cluster_ref, order_ref, packed_ref, idx_ref):
         x = emb_ref[...].astype(jnp.float32)
-        width = x.shape[1]
-        points = x.shape[0]
-        slots = send_ref.shape[0]
+        points, width = x.shape
         scale = lax.rsqrt(jnp.mean(x * x, axis=1, keepdims=True) + 1e-06)
-        unit = (x * scale * width ** (-0.5)).astype(jnp.bfloat16)
-        rows = meta_ref[...]
+        packed_ref[:, :width] = (x * scale * width ** (-0.5)).astype(jnp.bfloat16)
+        group_row = group_ref[...]
+        order_row = order_ref[...]
+        shape = (packed_ref.shape[1] - width, points)
+        which = lax.broadcasted_iota(jnp.int32, shape, 0)
+        rows = jnp.where(
+            which == 0,
+            cluster_ref[...] + 1,
+            jnp.where(
+                which == 1,
+                order_row >> 8,
+                jnp.where(which == 2, order_row & 255, jnp.where(which == 3, group_row, 0)),
+            ),
+        ).astype(jnp.float32)
         cols = rows.T
+        packed_ref[:, width:] = cols.astype(jnp.bfloat16)
         group_col = cols[:, 3:4]
         below = lax.broadcasted_iota(jnp.int32, (points, points), 1) < lax.broadcasted_iota(
             jnp.int32, (points, points), 0
         )
-        same = (group_col == rows[3:4, :]) & below
+        same = (group_col == group_row.astype(jnp.float32)) & below
         rank = jnp.sum(same.astype(jnp.float32), axis=1, keepdims=True).astype(jnp.int32)
         group = group_col.astype(jnp.int32)
         place = rank >> 2
         lane = rank & 3
         dev = place_of(group, place, zs, xs, ys)
-        target = dev * 4 + lane
-        spot = (target == lax.broadcasted_iota(jnp.int32, (points, slots), 1)).astype(jnp.float32)
-        spot = spot.T.astype(jnp.bfloat16)
-        send_ref[:, :width] = jnp.dot(spot, unit, preferred_element_type=jnp.float32).astype(
-            jnp.bfloat16
-        )
-        send_ref[:, width:] = jnp.dot(
-            spot, cols.astype(jnp.bfloat16), preferred_element_type=jnp.float32
-        ).astype(jnp.bfloat16)
-        at_own = dev * 12 + lane
         at_prev = place_of(group, (place + 3) & 3, zs, xs, ys) * 12 + 8 + lane
         at_next = place_of(group, (place + 1) & 3, zs, xs, ys) * 12 + 4 + lane
-        which = lax.broadcasted_iota(jnp.int32, idx_ref.shape, 1)
-        idx_ref[...] = jnp.where(which == 0, at_own, jnp.where(which == 1, at_prev, at_next))
+        pick = lax.broadcasted_iota(jnp.int32, idx_ref.shape, 1)
+        idx_ref[...] = jnp.where(
+            pick == 0,
+            dev * 4 + lane,
+            jnp.where(pick == 1, dev * 12 + lane, jnp.where(pick == 2, at_prev, at_next)),
+        )
 
     return kernel
 
 
 def build_send(embeddings, group, point_cluster, point_order, slots, dims, interpret=False):
     points, width = embeddings.shape
-    meta = jnp.concatenate(
-        [
-            jnp.stack([point_cluster + 1, point_order // 256, point_order % 256, group]).astype(
-                jnp.float32
-            ),
-            jnp.zeros((EXTRA - 4, points), jnp.float32),
-        ]
-    )
-    return pl.pallas_call(
+    packed, idx = pl.pallas_call(
         prologue(dims),
         out_shape=(
-            jax.ShapeDtypeStruct((slots, width + EXTRA), jnp.bfloat16),
+            jax.ShapeDtypeStruct((points, width + EXTRA), jnp.bfloat16),
             jax.ShapeDtypeStruct((points, 128), jnp.int32),
         ),
         interpret=interpret,
-    )(embeddings, meta)
+    )(
+        embeddings,
+        group.reshape(1, points),
+        point_cluster.reshape(1, points),
+        point_order.reshape(1, points),
+    )
+    spot = (idx[:, 0][None, :] == jnp.arange(slots, dtype=jnp.int32)[:, None]).astype(jnp.bfloat16)
+    send = lax.dot_general(
+        spot, packed, (((1,), (0,)), ((), ())), preferred_element_type=jnp.float32
+    ).astype(jnp.bfloat16)
+    return send, idx[:, 1:4]
 
 
 def split_meta(rows, width):

time: 73.5 us -> 70.2 us (0.955)
  blocking collectives: 29.2 us -> 43.2 us
  waiting for transfers between devices: 19.6 us -> 10.1 us
  starting transfers between devices: 6.37 us -> 1.53 us
  other arithmetic: 5.7 us -> 3.65 us
  local copies, waits for them, and re-layouts: 5.39 us -> 3.74 us
  matrix products: 2.58 us -> 4.03 us
    all_to_all x0 -> x1, blocking collectives: none -> 14 us  [body(): lax.all_to_all(payload, ('dp', 'blk'), split_axis=0, concat_axis=0, tiled...]
    all_to_all x1 -> x0, waiting for transfers between devices: 9.53 us -> none  [body(): lax.all_to_all(payload, ('dp', 'blk'), split_axis=0, concat_axis=0, tiled...]
    all_to_all x1 -> x0, starting transfers between devices: 4.83 us -> none  [body(): lax.all_to_all(payload, ('dp', 'blk'), split_axis=0, concat_axis=0, tiled...]
    all_to_all x2, local copies, waits for them, and re-layouts: 1.99 us -> 0.42 us  [body(): lax.all_to_all(send, ('dp', 'blk'), split_axis=0, concat_axis=0, tiled=True)]
    dot_general x0 -> x1, matrix products: none -> 1.46 us  [build_send(): lax.dot_general(spot, packed, (((1,), (0,)), ((), ())), preferred_element...]
    slice x1, local copies, waits for them, and re-layouts: 0.27 us -> 1.47 us  [body(): at_own, at_prev, at_next = (idx[:, 0], idx[:, 1], idx[:, 2])]
  transfers between devices with their start and end apart: 3 -> 2, of which waited for: 3 -> 2; matrix products, arithmetic and copies ran while one was open for 3% -> 3% of each run, Pallas kernels for 0% -> 0%
where the time goes in v6:
time: 70.2 us; the launch traced here: 70 us
  blocking collectives  43.2 us (62%)
  waiting for transfers between devices  10.1 us (14%)
  matrix products  4.03 us (6%)
  local copies, waits for them, and re-layouts  3.74 us (5%)
  other arithmetic  3.65 us (5%)
  Pallas kernels  2.29 us (3%)
  starting transfers between devices  1.53 us (2%)
  between operations  1.42 us (2%)
    all_to_all x1, blocking collectives, body(): lax.all_to_all(send, ('dp', 'blk'), split_axis=0, concat_axis=0, tiled=True)  29.2 us
    all_to_all x1, blocking collectives, body(): lax.all_to_all(payload, ('dp', 'blk'), split_axis=0, concat_axis=0, tiled...  14 us
    ppermute x1, waiting for transfers between devices, body(): next_ = lax.ppermute(own, ('dp', 'blk'), backward)  8.22 us
    dot_general x4, matrix products, masks(): lax.dot_general(query_rows, key_rows, (((1,), (1,)), ((), ())), preferred...  2.58 us
    pallas_call x1, Pallas kernels, build_send(): pl.pallas_call(prologue(dims), out_shape=(jax.ShapeDtypeStruct((points, w...  2.29 us
    ppermute x1, waiting for transfers between devices, body(): prev = lax.ppermute(own, ('dp', 'blk'), forward)  1.89 us
    slice x1, local copies, waits for them, and re-layouts, body(): at_own, at_prev, at_next = (idx[:, 0], idx[:, 1], idx[:, 2])  1.47 us
    dot_general x1, matrix products, build_send(): lax.dot_general(spot, packed, (((1,), (0,)), ((), ())), preferred_element...  1.46 us
  transfers between devices with their start and end apart: 2, of which 2 were waited for; matrix products, arithmetic and copies ran while one was open for 3% of the time, Pallas kernels for 0%

profile of v6, /device:TPU:1, one launch (start us, length us, event | category | flops | bytes accessed | tf_op | source)
XLA Modules:
  0.0 70.0 jit_solution(12607668474827691556)
XLA Ops:
  0.0 2.3 %shard_map.55 = (bf16[256,896]{1,0:T(8,128)(2,1)}, s32[256,128]{1,0:T(8,128)}) custom-call(bf16[256,768]{1,0:T(8,128)(2,1)} %emb_ref.1, s32[1,256]{1,0:T(1,128)} %bitcast.7, s32[1,256]{1,0:T(1,128)} %bitcast.8, s32[1,256]{1,0:T(1,128)} %bitcast.9), custom_call_target="tpu_custom_call" | custom-call | tf_op jit(solution)/shard_map/pallas_call | solution.py:95
  2.3 1.5 %slice_reduce_fusion.3 = (s32[256]{0:T(256)S(1)}, s32[256]{0:T(256)S(1)}, s32[256]{0:T(256)S(1)}, s32[256]{0:T(256)S(1)}) fusion(s32[256,128]{1,0:T(8,128)} %get-tuple-element.7), kind=kLoop, calls=%fused_computation.42 | loop fusion | bytes 8192 | tf_op jit(solution)/shard_map/slice | solution.py:173
  3.8 1.5 %convolution_convert_fusion = bf16[512,896]{1,0:T(8,128)(2,1)S(1)} fusion(bf16[256,896]{1,0:T(8,128)(2,1)} %get-tuple-element.8, s32[256]{0:T(256)S(1)} %get-tuple-element.22), kind=kOutput, calls=%fused_computation.6 | convolution fusion | flops 235470848 | bytes 1377280 | tf_op jit(solution)/shard_map/dot_general | solution.py:109
  5.2 0.2 all_to_all.14
  5.4 29.2 %all_to_all.21 = bf16[128,4,896]{2,1,0:T(4,128)(2,1)S(1)} all-to-all(bf16[128,4,896]{2,1,0:T(4,128)(2,1)S(1)} %all_to_all.14), channel_id=1, replica_groups=mesh['dp'=32,'blk'=4] {'dp','blk'}, dimensions={0} | all-to-all | bytes 1835008 | tf_op jit(solution)/shard_map/all_to_all | solution.py:143
  34.9 1.1 %collective-permute-start.1 = (bf16[512,896]{1,0:T(8,128)(2,1)S(1)}, bf16[512,896]{1,0:T(8,128)(2,1)S(1)}, u32[]{:S(2)}, u32[]{:S(2)}) collective-permute-start(bf16[512,896]{1,0:T(8,128)(2,1)S(1)} %all_to_all.16), channel_id=1, source_target_pairs={{1,0},{2,1},{3,2},{0,3},{12,4},{13,5},{14,6},{15,7},{9,8},{10,9},{... | collective-permute-start | bytes 2752520 | tf_op jit(solution)/shard_map/ppermute | solution.py:147
  35.9 0.5 collective-permute-start
  36.4 0.6 dynamic_slice.3
  38.3 0.3 add_reduce_fusion.7
  38.6 0.7 fusion.2
  39.3 8.2 %collective-permute-done.1 = bf16[512,896]{1,0:T(8,128)(2,1)S(1)} collective-permute-done((bf16[512,896]{1,0:T(8,128)(2,1)S(1)}, bf16[512,896]{1,0:T(8,128)(2,1)S(1)}, u32[]{:S(2)}, u32[]{:S(2)}) %collective-permute-start.1) | collective-permute-done | bytes 917536 | tf_op jit(solution)/shard_map/ppermute | solution.py:147
  47.5 0.3 add_reduce_fusion.3
  47.8 1.9 %collective-permute-done = bf16[512,896]{1,0:T(8,128)(2,1)S(1)} collective-permute-done((bf16[512,896]{1,0:T(8,128)(2,1)S(1)}, bf16[512,896]{1,0:T(8,128)(2,1)S(1)}, u32[]{:S(2)}, u32[]{:S(2)}) %collective-permute-start) | collective-permute-done | bytes 917536 | tf_op jit(solution)/shard_map/ppermute | solution.py:146
  49.7 0.3 add_reduce_fusion.5
  50.0 0.7 fusion.4
  50.6 0.7 fusion.3
  51.6 0.2 add_reduce_fusion.8
  51.9 0.3 add_reduce_fusion.1
  52.2 0.6 select_reduce_fusion.2
  53.4 14.0 %all_to_all.22 = f32[128,1,12]{2,1,0:T(1,128)S(1)} all-to-all(f32[128,1,12]{2,1,0:T(1,128)S(1)} %copy.18), channel_id=1, replica_groups=mesh['dp'=32,'blk'=4] {'dp','blk'}, dimensions={0} | all-to-all | bytes 12288 | tf_op jit(solution)/shard_map/all_to_all | solution.py:170
  67.3 0.5 broadcast.97
  67.9 0.8 %reduce.31 = f32[128,12]{1,0:T(8,128)S(1)} reduce(f32[128,1,12]{2,1,0:T(1,128)S(1)} %all_to_all.22, f32[]{:T(128)} %broadcast.97), dimensions={1}, to_apply=%all_to_all.18.reduce_sub_computation.3 | reduce | bytes 12292 | tf_op jit(solution)/shard_map/all_to_all | solution.py:170
  68.8 0.6 select_reduce_fusion
  69.4 0.6 compare_select_fusion
  (17 shorter events, 1.2 us)
Async XLA Ops:
  34.7 1.8 %copy-start = (s32[128]{0:T(128)S(1)}, s32[128]{0:T(128)}, u32[]{:S(2)}) copy-start(s32[128]{0:T(128)} %constant.42.clone) | copy-start | bytes 1540
  34.9 12.6 %collective-permute-start.1 = (bf16[512,896]{1,0:T(8,128)(2,1)S(1)}, bf16[512,896]{1,0:T(8,128)(2,1)S(1)}, u32[]{:S(2)}, u32[]{:S(2)}) collective-permute-start(bf16[512,896]{1,0:T(8,128)(2,1)S(1)} %all_to_all.16), channel_id=1, source_target_pairs={{1,0},{2,1},{3,2},{0,3},{12,4},{13,5},{14,6},{15,7},{9,8},{10,9},{... | collective-permute-start | bytes 2752520 | tf_op jit(solution)/shard_map/ppermute | solution.py:147
  35.9 13.8 %collective-permute-start = (bf16[512,896]{1,0:T(8,128)(2,1)S(1)}, bf16[512,896]{1,0:T(8,128)(2,1)S(1)}, u32[]{:S(2)}, u32[]{:S(2)}) collective-permute-start(bf16[512,896]{1,0:T(8,128)(2,1)S(1)} %all_to_all.16), channel_id=1, source_target_pairs={{0,1},{1,2},{2,3},{3,0},{4,12},{5,13},{6,14},{7,15},{8,9},{9,10},{... | collective-permute-start | bytes 2752520 | tf_op jit(solution)/shard_map/ppermute | solution.py:146

commit v7 on v6

--- a/solution.py
+++ b/solution.py
@@ -69,18 +69,18 @@
         cols = rows.T
         packed_ref[:, width:] = cols.astype(jnp.bfloat16)
         group_col = cols[:, 3:4]
-        below = lax.broadcasted_iota(jnp.int32, (points, points), 1) < lax.broadcasted_iota(
-            jnp.int32, (points, points), 0
+        above = lax.broadcasted_iota(jnp.int32, (points, points), 0) < lax.broadcasted_iota(
+            jnp.int32, (points, points), 1
         )
-        same = (group_col == group_row.astype(jnp.float32)) & below
-        rank = jnp.sum(same.astype(jnp.float32), axis=1, keepdims=True).astype(jnp.int32)
-        group = group_col.astype(jnp.int32)
+        same = (group_col == group_row.astype(jnp.float32)) & above
+        rank = jnp.sum(same.astype(jnp.float32), axis=0, keepdims=True).astype(jnp.int32)
+        group = group_row
         place = rank >> 2
         lane = rank & 3
         dev = place_of(group, place, zs, xs, ys)
         at_prev = place_of(group, (place + 3) & 3, zs, xs, ys) * 12 + 8 + lane
         at_next = place_of(group, (place + 1) & 3, zs, xs, ys) * 12 + 4 + lane
-        pick = lax.broadcasted_iota(jnp.int32, idx_ref.shape, 1)
+        pick = lax.broadcasted_iota(jnp.int32, idx_ref.shape, 0)
         idx_ref[...] = jnp.where(
             pick == 0,
             dev * 4 + lane,
@@ -96,7 +96,7 @@
         prologue(dims),
         out_shape=(
             jax.ShapeDtypeStruct((points, width + EXTRA), jnp.bfloat16),
-            jax.ShapeDtypeStruct((points, 128), jnp.int32),
+            jax.ShapeDtypeStruct((8, points), jnp.int32),
         ),
         interpret=interpret,
     )(
@@ -105,11 +105,11 @@
         point_cluster.reshape(1, points),
         point_order.reshape(1, points),
     )
-    spot = (idx[:, 0][None, :] == jnp.arange(slots, dtype=jnp.int32)[:, None]).astype(jnp.bfloat16)
+    spot = (idx[0][None, :] == jnp.arange(slots, dtype=jnp.int32)[:, None]).astype(jnp.bfloat16)
     send = lax.dot_general(
         spot, packed, (((1,), (0,)), ((), ())), preferred_element_type=jnp.float32
     ).astype(jnp.bfloat16)
-    return send, idx[:, 1:4]
+    return send, idx[1:4]
 
 
 def split_meta(rows, width):
@@ -170,7 +170,7 @@
     returned = lax.all_to_all(
         payload, ("dp", "blk"), split_axis=0, concat_axis=0, tiled=True
     ).reshape(devices * 12)
-    at_own, at_prev, at_next = idx[:, 0], idx[:, 1], idx[:, 2]
+    at_own, at_prev, at_next = idx[0], idx[1], idx[2]
     entry = jnp.arange(devices * 12, dtype=jnp.int32)[None, :]
     pick = (entry == at_own[:, None]) | (entry == at_prev[:, None]) | (entry == at_next[:, None])
     found = jnp.max(jnp.where(pick, returned[None, :], -2.0), axis=1)

time: 70.2 us -> 69.4 us (0.989)
  no operation moved by 1% of the time
where the time goes in v7:
time: 69.4 us; the launch traced here: 69.1 us
  blocking collectives  43.2 us (62%)
  waiting for transfers between devices  10.1 us (15%)
  matrix products  4.03 us (6%)
  other arithmetic  3.65 us (5%)
  local copies, waits for them, and re-layouts  3.11 us (4%)
  Pallas kernels  2.05 us (3%)
  starting transfers between devices  1.53 us (2%)
  between operations  1.42 us (2%)
    all_to_all x1, blocking collectives, body(): lax.all_to_all(send, ('dp', 'blk'), split_axis=0, concat_axis=0, tiled=True)  29.2 us
    all_to_all x1, blocking collectives, body(): lax.all_to_all(payload, ('dp', 'blk'), split_axis=0, concat_axis=0, tiled...  14 us
    ppermute x1, waiting for transfers between devices, body(): next_ = lax.ppermute(own, ('dp', 'blk'), backward)  8.22 us
    dot_general x4, matrix products, masks(): lax.dot_general(query_rows, key_rows, (((1,), (1,)), ((), ())), preferred...  2.58 us
    pallas_call x1, Pallas kernels, build_send(): pl.pallas_call(prologue(dims), out_shape=(jax.ShapeDtypeStruct((points, w...  2.05 us
    ppermute x1, waiting for transfers between devices, body(): prev = lax.ppermute(own, ('dp', 'blk'), forward)  1.89 us
    dot_general x1, matrix products, build_send(): lax.dot_general(spot, packed, (((1,), (0,)), ((), ())), preferred_element...  1.45 us
  transfers between devices with their start and end apart: 2, of which 2 were waited for; matrix products, arithmetic and copies ran while one was open for 3% of the time, Pallas kernels for 0%

profile of v7, /device:TPU:1, one launch (start us, length us, event | category | flops | bytes accessed | tf_op | source)
XLA Modules:
  0.0 69.1 jit_solution(17633841663832232742)
XLA Ops:
  0.0 2.1 %shard_map.55 = (bf16[256,896]{1,0:T(8,128)(2,1)}, s32[8,256]{1,0:T(8,128)}) custom-call(bf16[256,768]{1,0:T(8,128)(2,1)} %emb_ref.1, s32[1,256]{1,0:T(1,128)} %bitcast.15, s32[1,256]{1,0:T(1,128)} %bitcast.16, s32[1,256]{1,0:T(1,128)} %bitcast.17), custom_call_target="tpu_custom_call" | custom-call | tf_op jit(solution)/shard_map/pallas_call | solution.py:95
  2.1 0.8 %fusion.14 = (s32[1,256]{1,0:T(1,128)S(1)}, s32[1,256]{1,0:T(1,128)S(1)}, s32[1,256]{1,0:T(1,128)S(1)}, s32[1,256]{1,0:T(1,128)S(1)}) fusion(s32[8,256]{1,0:T(8,128)} %get-tuple-element.7), kind=kLoop, calls=%fused_computation.44 | loop fusion | bytes 8192 | tf_op jit(solution)/shard_map/slice | solution.py:173
  2.9 1.5 %convolution_convert_fusion = bf16[512,896]{1,0:T(8,128)(2,1)S(1)} fusion(bf16[256,896]{1,0:T(8,128)(2,1)} %get-tuple-element.8, s32[256]{0:T(256)S(1)} %bitcast.11), kind=kOutput, calls=%fused_computation.6 | convolution fusion | flops 235470848 | bytes 1377280 | tf_op jit(solution)/shard_map/dot_general | solution.py:109
  4.4 0.2 all_to_all.14
  4.6 29.2 %all_to_all.21 = bf16[128,4,896]{2,1,0:T(4,128)(2,1)S(1)} all-to-all(bf16[128,4,896]{2,1,0:T(4,128)(2,1)S(1)} %all_to_all.14), channel_id=1, replica_groups=mesh['dp'=32,'blk'=4] {'dp','blk'}, dimensions={0} | all-to-all | bytes 1835008 | tf_op jit(solution)/shard_map/all_to_all | solution.py:143
  34.0 1.1 %collective-permute-start.1 = (bf16[512,896]{1,0:T(8,128)(2,1)S(1)}, bf16[512,896]{1,0:T(8,128)(2,1)S(1)}, u32[]{:S(2)}, u32[]{:S(2)}) collective-permute-start(bf16[512,896]{1,0:T(8,128)(2,1)S(1)} %all_to_all.16), channel_id=1, source_target_pairs={{1,0},{2,1},{3,2},{0,3},{12,4},{13,5},{14,6},{15,7},{9,8},{10,9},{... | collective-permute-start | bytes 2752520 | tf_op jit(solution)/shard_map/ppermute | solution.py:147
  35.1 0.5 collective-permute-start
  35.5 0.6 dynamic_slice.3
  37.4 0.3 add_reduce_fusion.7
  37.7 0.7 fusion.2
  38.4 8.2 %collective-permute-done.1 = bf16[512,896]{1,0:T(8,128)(2,1)S(1)} collective-permute-done((bf16[512,896]{1,0:T(8,128)(2,1)S(1)}, bf16[512,896]{1,0:T(8,128)(2,1)S(1)}, u32[]{:S(2)}, u32[]{:S(2)}) %collective-permute-start.1) | collective-permute-done | bytes 917536 | tf_op jit(solution)/shard_map/ppermute | solution.py:147
  46.6 0.3 add_reduce_fusion.3
  46.9 1.9 %collective-permute-done = bf16[512,896]{1,0:T(8,128)(2,1)S(1)} collective-permute-done((bf16[512,896]{1,0:T(8,128)(2,1)S(1)}, bf16[512,896]{1,0:T(8,128)(2,1)S(1)}, u32[]{:S(2)}, u32[]{:S(2)}) %collective-permute-start) | collective-permute-done | bytes 917536 | tf_op jit(solution)/shard_map/ppermute | solution.py:146
  48.8 0.3 add_reduce_fusion.5
  49.1 0.7 fusion.4
  49.8 0.7 fusion.3
  50.7 0.2 add_reduce_fusion.8
  51.0 0.3 add_reduce_fusion.1
  51.3 0.6 select_reduce_fusion.2
  52.5 14.0 %all_to_all.22 = f32[128,1,12]{2,1,0:T(1,128)S(1)} all-to-all(f32[128,1,12]{2,1,0:T(1,128)S(1)} %copy.18), channel_id=1, replica_groups=mesh['dp'=32,'blk'=4] {'dp','blk'}, dimensions={0} | all-to-all | bytes 12288 | tf_op jit(solution)/shard_map/all_to_all | solution.py:170
  66.5 0.5 broadcast.93
  67.0 0.8 %reduce.23 = f32[128,12]{1,0:T(8,128)S(1)} reduce(f32[128,1,12]{2,1,0:T(1,128)S(1)} %all_to_all.22, f32[]{:T(128)} %broadcast.93), dimensions={1}, to_apply=%all_to_all.18.reduce_sub_computation.3 | reduce | bytes 12292 | tf_op jit(solution)/shard_map/all_to_all | solution.py:170
  67.9 0.6 select_reduce_fusion
  68.5 0.6 compare_select_fusion
  (17 shorter events, 1.2 us)
Async XLA Ops:
  33.8 1.8 %copy-start = (s32[128]{0:T(128)S(1)}, s32[128]{0:T(128)}, u32[]{:S(2)}) copy-start(s32[128]{0:T(128)} %constant.42.clone) | copy-start | bytes 1540
  34.0 12.6 %collective-permute-start.1 = (bf16[512,896]{1,0:T(8,128)(2,1)S(1)}, bf16[512,896]{1,0:T(8,128)(2,1)S(1)}, u32[]{:S(2)}, u32[]{:S(2)}) collective-permute-start(bf16[512,896]{1,0:T(8,128)(2,1)S(1)} %all_to_all.16), channel_id=1, source_target_pairs={{1,0},{2,1},{3,2},{0,3},{12,4},{13,5},{14,6},{15,7},{9,8},{10,9},{... | collective-permute-start | bytes 2752520 | tf_op jit(solution)/shard_map/ppermute | solution.py:147
  35.1 13.8 %collective-permute-start = (bf16[512,896]{1,0:T(8,128)(2,1)S(1)}, bf16[512,896]{1,0:T(8,128)(2,1)S(1)}, u32[]{:S(2)}, u32[]{:S(2)}) collective-permute-start(bf16[512,896]{1,0:T(8,128)(2,1)S(1)} %all_to_all.16), channel_id=1, source_target_pairs={{0,1},{1,2},{2,3},{3,0},{4,12},{5,13},{6,14},{7,15},{8,9},{9,10},{... | collective-permute-start | bytes 2752520 | tf_op jit(solution)/shard_map/ppermute | solution.py:146

commit v8 on v7

--- a/solution.py
+++ b/solution.py
@@ -143,22 +143,26 @@
     own = lax.all_to_all(send, ("dp", "blk"), split_axis=0, concat_axis=0, tiled=True)
     forward = [(i, int(nxt[i])) for i in range(devices)]
     backward = [(int(nxt[i]), i) for i in range(devices)]
-    prev = lax.ppermute(own, ("dp", "blk"), forward)
-    next_ = lax.ppermute(own, ("dp", "blk"), backward)
     query = split_meta(own, width)
+    data = query[0]
+    labels = jnp.stack([query[1], query[2]])
+    prev_data = lax.ppermute(data, ("dp", "blk"), forward)
+    next_data = lax.ppermute(data, ("dp", "blk"), backward)
+    prev_labels = lax.ppermute(labels, ("dp", "blk"), forward)
+    next_labels = lax.ppermute(labels, ("dp", "blk"), backward)
+    prev = (prev_data, prev_labels[0], prev_labels[1])
+    next_ = (next_data, next_labels[0], next_labels[1])
     best = best_over(query, query)
-    best = jnp.maximum(best, best_over(query, split_meta(prev, width)))
-    best = jnp.maximum(best, best_over(query, split_meta(next_, width)))
+    best = jnp.maximum(best, best_over(query, prev))
+    best = jnp.maximum(best, best_over(query, next_))
     half = slots // 2
     me = jnp.asarray(ring_pos)[lax.axis_index(("dp", "blk"))]
     inner = (me == 1) | (me == 2)
-    rows = jnp.where(inner, prev[:half], next_[half:])
-    cols = jnp.where(inner, next_, prev)
-    scores, same_c, earlier = masks(split_meta(rows, width), split_meta(cols, width))
+    rows = tuple(jnp.where(inner, p[:half], n[half:]) for p, n in zip(prev, next_))
+    cols = tuple(jnp.where(inner, n, p) for p, n in zip(prev, next_))
+    scores, same_c, earlier = masks(rows, cols)
     row_part = jnp.max(jnp.where(same_c & earlier, scores, -2.0), axis=1)
-    col_order_r = split_meta(rows, width)[2]
-    col_order_c = split_meta(cols, width)[2]
-    col_ok = same_c & (col_order_r[:, None] < col_order_c[None, :])
+    col_ok = same_c & (rows[2][:, None] < cols[2][None, :])
     col_part = jnp.max(jnp.where(col_ok, scores, -2.0), axis=0)
     floor = jnp.full((half,), -2.0, jnp.float32)
     side_prev = jnp.where(inner, jnp.concatenate([row_part, floor]), col_part)

time: 69.4 us -> 68.6 us (0.988)
  blocking collectives: 43.2 us -> 14 us
  waiting for transfers between devices: 10.1 us -> 25 us
  starting transfers between devices: 1.53 us -> 15.3 us
  other arithmetic: 3.65 us -> 2.35 us
  local copies, waits for them, and re-layouts: 3.11 us -> 4.09 us
    all_to_all x1 -> x0, blocking collectives: 29.2 us -> none  [body(): lax.all_to_all(send, ('dp', 'blk'), split_axis=0, concat_axis=0, tiled=True)]
    all_to_all x0 -> x1, waiting for transfers between devices: none -> 16 us  [body(): lax.all_to_all(send, ('dp', 'blk'), split_axis=0, concat_axis=0, tiled=True)]
    all_to_all x0 -> x1, starting transfers between devices: none -> 11.5 us  [body(): lax.all_to_all(send, ('dp', 'blk'), split_axis=0, concat_axis=0, tiled=True)]
    ppermute x2 -> x4, starting transfers between devices: 1.53 us -> 3.79 us  [the longest x1 2.26 us: body(): next_labels = lax.ppermute(labels, ('dp', 'blk'), backward)]
    ppermute x2 -> x4, waiting for transfers between devices: 10.1 us -> 8.99 us  [the longest x1 6.79 us: body(): next_labels = lax.ppermute(labels, ('dp', 'blk'), backward)]
    all_to_all x2, local copies, waits for them, and re-layouts: 0.42 us -> 1.35 us  [body(): lax.all_to_all(send, ('dp', 'blk'), split_axis=0, concat_axis=0, tiled=True)]
    sub x4 -> x1, other arithmetic: 1.22 us -> 0.31 us  [split_meta(): cluster = rows[:, width].astype(jnp.float32) - 1.0]
  transfers between devices with their start and end apart: 2 -> 5, of which waited for: 2 -> 3; matrix products, arithmetic and copies ran while one was open for 3% -> 2% of each run, Pallas kernels for 0% -> 0%
where the time goes in v8:
time: 68.6 us; the launch traced here: 68.3 us
  waiting for transfers between devices  25 us (36%)
  starting transfers between devices  15.3 us (22%)
  blocking collectives  14 us (20%)
  local copies, waits for them, and re-layouts  4.09 us (6%)
  matrix products  4.07 us (6%)
  other arithmetic  2.35 us (3%)
  Pallas kernels  2.05 us (3%)
  between operations  1.45 us (2%)
    all_to_all x1, waiting for transfers between devices, body(): lax.all_to_all(send, ('dp', 'blk'), split_axis=0, concat_axis=0, tiled=True)  16 us
    all_to_all x1, blocking collectives, body(): lax.all_to_all(payload, ('dp', 'blk'), split_axis=0, concat_axis=0, tiled...  14 us
    all_to_all x1, starting transfers between devices, body(): lax.all_to_all(send, ('dp', 'blk'), split_axis=0, concat_axis=0, tiled=True)  11.5 us
    ppermute x1, waiting for transfers between devices, body(): next_labels = lax.ppermute(labels, ('dp', 'blk'), backward)  6.79 us
    dot_general x4, matrix products, masks(): lax.dot_general(query_rows, key_rows, (((1,), (1,)), ((), ())), preferred...  2.61 us
    ppermute x1, starting transfers between devices, body(): next_labels = lax.ppermute(labels, ('dp', 'blk'), backward)  2.26 us
    ppermute x1, waiting for transfers between devices, body(): prev_labels = lax.ppermute(labels, ('dp', 'blk'), forward)  2.19 us
    pallas_call x1, Pallas kernels, build_send(): pl.pallas_call(prologue(dims), out_shape=(jax.ShapeDtypeStruct((points, w...  2.05 us
  transfers between devices with their start and end apart: 5, of which 3 were waited for; matrix products, arithmetic and copies ran while one was open for 2% of the time, Pallas kernels for 0%

profile of v8, /device:TPU:1, one launch (start us, length us, event | category | flops | bytes accessed | tf_op | source)
XLA Modules:
  0.0 68.3 jit_solution(2640368024458557165)
XLA Ops:
  0.0 2.1 %shard_map.55 = (bf16[256,896]{1,0:T(8,128)(2,1)}, s32[8,256]{1,0:T(8,128)}) custom-call(bf16[256,768]{1,0:T(8,128)(2,1)} %emb_ref.1, s32[1,256]{1,0:T(1,128)} %bitcast.35, s32[1,256]{1,0:T(1,128)} %bitcast.36, s32[1,256]{1,0:T(1,128)} %bitcast.37), custom_call_target="tpu_custom_call" | custom-call | tf_op jit(solution)/shard_map/pallas_call | solution.py:95
  2.1 0.8 %fusion.18 = (s32[1,256]{1,0:T(1,128)S(1)}, s32[1,256]{1,0:T(1,128)S(1)}, s32[1,256]{1,0:T(1,128)S(1)}, s32[1,256]{1,0:T(1,128)S(1)}) fusion(s32[8,256]{1,0:T(8,128)} %get-tuple-element.7), kind=kLoop, calls=%fused_computation.40 | loop fusion | bytes 8192 | tf_op jit(solution)/shard_map/slice | solution.py:177
  2.9 1.5 %convolution_convert_fusion = bf16[512,896]{1,0:T(8,128)(2,1)S(1)} fusion(bf16[256,896]{1,0:T(8,128)(2,1)} %get-tuple-element.8, s32[256]{0:T(256)S(1)} %bitcast.25), kind=kOutput, calls=%fused_computation.6 | convolution fusion | flops 235470848 | bytes 1377280 | tf_op jit(solution)/shard_map/dot_general | solution.py:109
  4.4 1.1 %all_to_all.14 = bf16[128,4,896]{2,1,0:T(4,128)(2,1)} reshape(bf16[512,896]{1,0:T(8,128)(2,1)S(1)} %convolution_convert_fusion) | data formatting | bytes 1835008 | tf_op jit(solution)/shard_map/all_to_all | solution.py:143
  5.5 11.5 %all-to-all-start = ((bf16[128,4,896]{2,1,0:T(4,128)(2,1)}), bf16[128,4,896]{2,1,0:T(4,128)(2,1)S(1)}, u32[]{:S(2)}, u32[]{:S(2)}) async-start(bf16[128,4,896]{2,1,0:T(4,128)(2,1)} %all_to_all.14), calls=%async_computation | async-start | bytes 1835008 | tf_op jit(solution)/shard_map/all_to_all | solution.py:143
  17.0 0.6 dynamic_slice.3
  18.9 16.0 %all-to-all-done = bf16[128,4,896]{2,1,0:T(4,128)(2,1)S(1)} async-done(((bf16[128,4,896]{2,1,0:T(4,128)(2,1)}), bf16[128,4,896]{2,1,0:T(4,128)(2,1)S(1)}, u32[]{:S(2)}, u32[]{:S(2)}) %all-to-all-start) | async-done | bytes 917536 | tf_op jit(solution)/shard_map/all_to_all | solution.py:143
  34.9 0.2 all_to_all.16
  35.1 0.3 add_reduce_fusion.1
  35.5 1.1 %collective-permute-start.3 = (bf16[512,768]{1,0:T(8,128)(2,1)S(1)}, bf16[512,768]{1,0:T(8,128)(2,1)S(1)}, u32[]{:S(2)}, u32[]{:S(2)}) collective-permute-start(bf16[512,768]{1,0:T(8,128)(2,1)S(1)} %slice.87), channel_id=1, source_target_pairs={{1,0},{2,1},{3,2},{0,3},{12,4},{13,5},{14,6},{15,7},{9,8},{10,9},{... | collective-permute-start | bytes 2359304 | tf_op jit(solution)/shard_map/ppermute | solution.py:150
  36.5 0.5 collective-permute-start.1
  37.0 2.3 %collective-permute-start.2 = (f32[2,512]{1,0:T(2,128)S(1)}, f32[2,512]{1,0:T(2,128)S(1)}, u32[]{:S(2)}, u32[]{:S(2)}) collective-permute-start(f32[2,512]{1,0:T(2,128)S(1)} %pad_maximum_fusion.1), channel_id=1, source_target_pairs={{1,0},{2,1},{3,2},{0,3},{12,4},{13,5},{14,6},{15,7},{9,8},{10,9},{... | collective-permute-start | bytes 12296 | tf_op jit(solution)/shard_map/ppermute | solution.py:152
  39.3 0.6 fusion.2
  40.0 6.8 %collective-permute-done.2 = f32[2,512]{1,0:T(2,128)S(1)} collective-permute-done((f32[2,512]{1,0:T(2,128)S(1)}, f32[2,512]{1,0:T(2,128)S(1)}, u32[]{:S(2)}, u32[]{:S(2)}) %collective-permute-start.2) | collective-permute-done | bytes 4128 | tf_op jit(solution)/shard_map/ppermute | solution.py:152
  46.7 2.2 %collective-permute-done = f32[2,512]{1,0:T(2,128)S(1)} collective-permute-done((f32[2,512]{1,0:T(2,128)S(1)}, f32[2,512]{1,0:T(2,128)S(1)}, u32[]{:S(2)}, u32[]{:S(2)}) %collective-permute-start) | collective-permute-done | bytes 4128 | tf_op jit(solution)/shard_map/ppermute | solution.py:151
  49.0 0.6 select_reduce_fusion.4
  49.8 0.1 stack_reshape.7
  50.0 0.7 select_reduce_fusion.1
  50.7 0.7 select_reduce_fusion.2
  51.7 14.0 %all_to_all.21 = f32[128,1,12]{2,1,0:T(1,128)S(1)} all-to-all(f32[128,1,12]{2,1,0:T(1,128)S(1)} %copy.18), channel_id=1, replica_groups=mesh['dp'=32,'blk'=4] {'dp','blk'}, dimensions={0} | all-to-all | bytes 12288 | tf_op jit(solution)/shard_map/all_to_all | solution.py:174
  65.7 0.5 broadcast.55
  66.2 0.8 %reduce.9 = f32[128,12]{1,0:T(8,128)S(1)} reduce(f32[128,1,12]{2,1,0:T(1,128)S(1)} %all_to_all.21, f32[]{:T(128)} %broadcast.55), dimensions={1}, to_apply=%all_to_all.18.reduce_sub_computation.3 | reduce | bytes 12292 | tf_op jit(solution)/shard_map/all_to_all | solution.py:174
  67.1 0.6 select_reduce_fusion
  67.7 0.6 compare_select_fusion
  (20 shorter events, 0.7 us)
Async XLA Ops:
  5.5 11.5 %copy-start = (s32[128]{0:T(128)S(1)}, s32[128]{0:T(128)}, u32[]{:S(2)}) copy-start(s32[128]{0:T(128)} %constant.36.clone) | copy-start | bytes 1540
  5.5 29.4 %all-to-all-start = ((bf16[128,4,896]{2,1,0:T(4,128)(2,1)}), bf16[128,4,896]{2,1,0:T(4,128)(2,1)S(1)}, u32[]{:S(2)}, u32[]{:S(2)}) async-start(bf16[128,4,896]{2,1,0:T(4,128)(2,1)} %all_to_all.14), calls=%async_computation | async-start | bytes 1835008 | tf_op jit(solution)/shard_map/all_to_all | solution.py:143
  35.5 13.5 %collective-permute-start.3 = (bf16[512,768]{1,0:T(8,128)(2,1)S(1)}, bf16[512,768]{1,0:T(8,128)(2,1)S(1)}, u32[]{:S(2)}, u32[]{:S(2)}) collective-permute-start(bf16[512,768]{1,0:T(8,128)(2,1)S(1)} %slice.87), channel_id=1, source_target_pairs={{1,0},{2,1},{3,2},{0,3},{12,4},{13,5},{14,6},{15,7},{9,8},{10,9},{... | collective-permute-start | bytes 2359304 | tf_op jit(solution)/shard_map/ppermute | solution.py:150
  36.5 12.4 %collective-permute-start.1 = (bf16[512,768]{1,0:T(8,128)(2,1)S(1)}, bf16[512,768]{1,0:T(8,128)(2,1)S(1)}, u32[]{:S(2)}, u32[]{:S(2)}) collective-permute-start(bf16[512,768]{1,0:T(8,128)(2,1)S(1)} %slice.87), channel_id=1, source_target_pairs={{0,1},{1,2},{2,3},{3,0},{4,12},{5,13},{6,14},{7,15},{8,9},{9,10},{... | collective-permute-start | bytes 2359304 | tf_op jit(solution)/shard_map/ppermute | solution.py:149
  37.0 9.7 %collective-permute-start.2 = (f32[2,512]{1,0:T(2,128)S(1)}, f32[2,512]{1,0:T(2,128)S(1)}, u32[]{:S(2)}, u32[]{:S(2)}) collective-permute-start(f32[2,512]{1,0:T(2,128)S(1)} %pad_maximum_fusion.1), channel_id=1, source_target_pairs={{1,0},{2,1},{3,2},{0,3},{12,4},{13,5},{14,6},{15,7},{9,8},{10,9},{... | collective-permute-start | bytes 12296 | tf_op jit(solution)/shard_map/ppermute | solution.py:152
  39.3 9.6 %collective-permute-start = (f32[2,512]{1,0:T(2,128)S(1)}, f32[2,512]{1,0:T(2,128)S(1)}, u32[]{:S(2)}, u32[]{:S(2)}) collective-permute-start(f32[2,512]{1,0:T(2,128)S(1)} %pad_maximum_fusion.1), channel_id=1, source_target_pairs={{0,1},{1,2},{2,3},{3,0},{4,12},{5,13},{6,14},{7,15},{8,9},{9,10},{... | collective-permute-start | bytes 12296 | tf_op jit(solution)/shard_map/ppermute | solution.py:151

commit v9 on v8

--- a/solution.py
+++ b/solution.py
@@ -48,7 +48,7 @@
 def prologue(dims):
     zs, xs, ys = dims
 
-    def kernel(emb_ref, group_ref, cluster_ref, order_ref, packed_ref, idx_ref):
+    def kernel(emb_ref, group_ref, cluster_ref, order_ref, packed_ref, target_ref, own_ref, prev_ref, next_ref):
         x = emb_ref[...].astype(jnp.float32)
         points, width = x.shape
         scale = lax.rsqrt(jnp.mean(x * x, axis=1, keepdims=True) + 1e-06)
@@ -80,24 +80,20 @@
         dev = place_of(group, place, zs, xs, ys)
         at_prev = place_of(group, (place + 3) & 3, zs, xs, ys) * 12 + 8 + lane
         at_next = place_of(group, (place + 1) & 3, zs, xs, ys) * 12 + 4 + lane
-        pick = lax.broadcasted_iota(jnp.int32, idx_ref.shape, 0)
-        idx_ref[...] = jnp.where(
-            pick == 0,
-            dev * 4 + lane,
-            jnp.where(pick == 1, dev * 12 + lane, jnp.where(pick == 2, at_prev, at_next)),
-        )
+        target_ref[...] = dev * 4 + lane
+        own_ref[...] = dev * 12 + lane
+        prev_ref[...] = at_prev
+        next_ref[...] = at_next
 
     return kernel
 
 
 def build_send(embeddings, group, point_cluster, point_order, slots, dims, interpret=False):
     points, width = embeddings.shape
-    packed, idx = pl.pallas_call(
+    packed, target, at_own, at_prev, at_next = pl.pallas_call(
         prologue(dims),
-        out_shape=(
-            jax.ShapeDtypeStruct((points, width + EXTRA), jnp.bfloat16),
-            jax.ShapeDtypeStruct((8, points), jnp.int32),
-        ),
+        out_shape=(jax.ShapeDtypeStruct((points, width + EXTRA), jnp.bfloat16),)
+        + tuple(jax.ShapeDtypeStruct((1, points), jnp.int32) for _ in range(4)),
         interpret=interpret,
     )(
         embeddings,
@@ -105,11 +101,11 @@
         point_cluster.reshape(1, points),
         point_order.reshape(1, points),
     )
-    spot = (idx[0][None, :] == jnp.arange(slots, dtype=jnp.int32)[:, None]).astype(jnp.bfloat16)
+    spot = (target.reshape(points)[None, :] == jnp.arange(slots, dtype=jnp.int32)[:, None]).astype(jnp.bfloat16)
     send = lax.dot_general(
         spot, packed, (((1,), (0,)), ((), ())), preferred_element_type=jnp.float32
     ).astype(jnp.bfloat16)
-    return send, idx[1:4]
+    return send, tuple(a.reshape(points) for a in (at_own, at_prev, at_next))
 
 
 def split_meta(rows, width):
@@ -167,12 +163,11 @@
     floor = jnp.full((half,), -2.0, jnp.float32)
     side_prev = jnp.where(inner, jnp.concatenate([row_part, floor]), col_part)
     side_next = jnp.where(inner, col_part, jnp.concatenate([floor, row_part]))
-    payload = jnp.stack(
-        [best.reshape(devices, 4), side_prev.reshape(devices, 4), side_next.reshape(devices, 4)],
-        axis=1,
-    ).reshape(devices, 12)
+    payload = jnp.concatenate(
+        [v.reshape(devices, 1, 4) for v in (best, side_prev, side_next)], axis=2
+    )
     returned = lax.all_to_all(
-        payload, ("dp", "blk"), split_axis=0, concat_axis=0, tiled=True
+        payload, ("dp", "blk"), split_axis=0, concat_axis=0, tiled=False
     ).reshape(devices * 12)
     at_own, at_prev, at_next = idx[0], idx[1], idx[2]
     entry = jnp.arange(devices * 12, dtype=jnp.int32)[None, :]

time: 68.6 us -> 67.5 us (0.984)
  local copies, waits for them, and re-layouts: 4.09 us -> 2.93 us
    slice x1 -> x0, local copies, waits for them, and re-layouts: 0.85 us -> none  [body(): at_own, at_prev, at_next = (idx[0], idx[1], idx[2])]
where the time goes in v9:
time: 67.5 us; the launch traced here: 67.2 us
  waiting for transfers between devices  25 us (37%)
  starting transfers between devices  15.3 us (23%)
  blocking collectives  14 us (21%)
  matrix products  4.06 us (6%)
  local copies, waits for them, and re-layouts  2.93 us (4%)
  other arithmetic  2.44 us (4%)
  Pallas kernels  2.05 us (3%)
  between operations  1.49 us (2%)
    all_to_all x1, waiting for transfers between devices, body(): lax.all_to_all(send, ('dp', 'blk'), split_axis=0, concat_axis=0, tiled=True)  16 us
    all_to_all x1, blocking collectives, body(): lax.all_to_all(payload, ('dp', 'blk'), split_axis=0, concat_axis=0, tiled...  14 us
    all_to_all x1, starting transfers between devices, body(): lax.all_to_all(send, ('dp', 'blk'), split_axis=0, concat_axis=0, tiled=True)  11.5 us
    ppermute x1, waiting for transfers between devices, body(): next_labels = lax.ppermute(labels, ('dp', 'blk'), backward)  6.79 us
    dot_general x4, matrix products, masks(): lax.dot_general(query_rows, key_rows, (((1,), (1,)), ((), ())), preferred...  2.59 us
    ppermute x1, starting transfers between devices, body(): next_labels = lax.ppermute(labels, ('dp', 'blk'), backward)  2.26 us
    ppermute x1, waiting for transfers between devices, body(): prev_labels = lax.ppermute(labels, ('dp', 'blk'), forward)  2.19 us
    pallas_call x1, Pallas kernels, build_send(): pl.pallas_call(prologue(dims), out_shape=(jax.ShapeDtypeStruct((points, w...  2.05 us
  transfers between devices with their start and end apart: 5, of which 3 were waited for; matrix products, arithmetic and copies ran while one was open for 2% of the time, Pallas kernels for 0%

profile of v9, /device:TPU:1, one launch (start us, length us, event | category | flops | bytes accessed | tf_op | source)
XLA Modules:
  0.0 67.2 jit_solution(18436905481226840497)
XLA Ops:
  0.0 2.1 %shard_map.55 = (bf16[256,896]{1,0:T(8,128)(2,1)}, s32[1,256]{1,0:T(1,128)}, s32[1,256]{1,0:T(1,128)}, s32[1,256]{1,0:T(1,128)}, s32[1,256]{1,0:T(1,128)}) custom-call(bf16[256,768]{1,0:T(8,128)(2,1)} %emb_ref.1, s32[1,256]{1,0:T(1,128)} %bitcast.31, s32[1,256]{1,0:T(1,128)} %bitcast.32, s32[1,256]{1,0:T(1,128)} %bitcast.33), custom_call_target="tpu_custom_call" | custom-call | tf_op jit(solution)/shard_map/pallas_call | solution.py:93
  2.1 1.5 %convolution_convert_fusion = bf16[512,896]{1,0:T(8,128)(2,1)S(1)} fusion(bf16[256,896]{1,0:T(8,128)(2,1)} %get-tuple-element.14, s32[256]{0:T(256)} %bitcast.34), kind=kOutput, calls=%fused_computation.6 | convolution fusion | flops 235470848 | bytes 1377280 | tf_op jit(solution)/shard_map/dot_general | solution.py:105
  3.5 1.1 %all_to_all.11 = bf16[128,4,896]{2,1,0:T(4,128)(2,1)} reshape(bf16[512,896]{1,0:T(8,128)(2,1)S(1)} %convolution_convert_fusion) | data formatting | bytes 1835008 | tf_op jit(solution)/shard_map/all_to_all | solution.py:139
  4.7 11.5 %all-to-all-start = ((bf16[128,4,896]{2,1,0:T(4,128)(2,1)}), bf16[128,4,896]{2,1,0:T(4,128)(2,1)S(1)}, u32[]{:S(2)}, u32[]{:S(2)}) async-start(bf16[128,4,896]{2,1,0:T(4,128)(2,1)} %all_to_all.11), calls=%async_computation | async-start | bytes 1835008 | tf_op jit(solution)/shard_map/all_to_all | solution.py:139
  16.2 0.6 dynamic_slice.3
  18.1 16.0 %all-to-all-done = bf16[128,4,896]{2,1,0:T(4,128)(2,1)S(1)} async-done(((bf16[128,4,896]{2,1,0:T(4,128)(2,1)}), bf16[128,4,896]{2,1,0:T(4,128)(2,1)S(1)}, u32[]{:S(2)}, u32[]{:S(2)}) %all-to-all-start) | async-done | bytes 917536 | tf_op jit(solution)/shard_map/all_to_all | solution.py:139
  34.1 0.2 all_to_all.13
  34.3 0.3 add_reduce_fusion.1
  34.7 1.1 %collective-permute-start.3 = (bf16[512,768]{1,0:T(8,128)(2,1)S(1)}, bf16[512,768]{1,0:T(8,128)(2,1)S(1)}, u32[]{:S(2)}, u32[]{:S(2)}) collective-permute-start(bf16[512,768]{1,0:T(8,128)(2,1)S(1)} %slice.67), channel_id=1, source_target_pairs={{1,0},{2,1},{3,2},{0,3},{12,4},{13,5},{14,6},{15,7},{9,8},{10,9},{... | collective-permute-start | bytes 2359304 | tf_op jit(solution)/shard_map/ppermute | solution.py:146
  35.7 0.5 collective-permute-start.1
  36.2 2.3 %collective-permute-start.2 = (f32[2,512]{1,0:T(2,128)S(1)}, f32[2,512]{1,0:T(2,128)S(1)}, u32[]{:S(2)}, u32[]{:S(2)}) collective-permute-start(f32[2,512]{1,0:T(2,128)S(1)} %pad_maximum_fusion.1), channel_id=1, source_target_pairs={{1,0},{2,1},{3,2},{0,3},{12,4},{13,5},{14,6},{15,7},{9,8},{10,9},{... | collective-permute-start | bytes 12296 | tf_op jit(solution)/shard_map/ppermute | solution.py:148
  38.5 0.6 fusion.2
  39.1 6.8 %collective-permute-done.2 = f32[2,512]{1,0:T(2,128)S(1)} collective-permute-done((f32[2,512]{1,0:T(2,128)S(1)}, f32[2,512]{1,0:T(2,128)S(1)}, u32[]{:S(2)}, u32[]{:S(2)}) %collective-permute-start.2) | collective-permute-done | bytes 4128 | tf_op jit(solution)/shard_map/ppermute | solution.py:148
  45.9 2.2 %collective-permute-done = f32[2,512]{1,0:T(2,128)S(1)} collective-permute-done((f32[2,512]{1,0:T(2,128)S(1)}, f32[2,512]{1,0:T(2,128)S(1)}, u32[]{:S(2)}, u32[]{:S(2)}) %collective-permute-start) | collective-permute-done | bytes 4128 | tf_op jit(solution)/shard_map/ppermute | solution.py:147
  48.1 0.6 select_reduce_fusion.4
  48.8 0.1 reshape.140
  48.9 0.1 reshape.139
  49.0 0.7 select_reduce_fusion.1
  49.7 0.7 select_reduce_fusion.2
  50.6 14.0 %all_to_all.17 = f32[128,1,12]{2,1,0:T(1,128)S(1)} all-to-all(f32[128,1,12]{2,1,0:T(1,128)S(1)} %bitcast.22), channel_id=1, replica_groups=mesh['dp'=32,'blk'=4] {'dp','blk'}, dimensions={0} | all-to-all | bytes 12288 | tf_op jit(solution)/shard_map/all_to_all | solution.py:169
  64.6 0.5 broadcast.55
  65.1 0.8 %reduce.9 = f32[128,12]{1,0:T(8,128)S(1)} reduce(f32[128,1,12]{2,1,0:T(1,128)S(1)} %all_to_all.17, f32[]{:T(128)} %broadcast.55), dimensions={1}, to_apply=%all_to_all.14.reduce_sub_computation.3 | reduce | bytes 12292 | tf_op jit(solution)/shard_map/all_to_all | solution.py:169
  66.1 0.6 select_reduce_fusion
  66.7 0.6 compare_select_fusion
  (20 shorter events, 0.4 us)
Async XLA Ops:
  4.7 11.5 %copy-start.3 = (s32[128]{0:T(128)S(1)}, s32[128]{0:T(128)}, u32[]{:S(2)}) copy-start(s32[128]{0:T(128)} %constant.36.clone) | copy-start | bytes 1540
  4.7 29.4 %all-to-all-start = ((bf16[128,4,896]{2,1,0:T(4,128)(2,1)}), bf16[128,4,896]{2,1,0:T(4,128)(2,1)S(1)}, u32[]{:S(2)}, u32[]{:S(2)}) async-start(bf16[128,4,896]{2,1,0:T(4,128)(2,1)} %all_to_all.11), calls=%async_computation | async-start | bytes 1835008 | tf_op jit(solution)/shard_map/all_to_all | solution.py:139
  34.7 13.5 %collective-permute-start.3 = (bf16[512,768]{1,0:T(8,128)(2,1)S(1)}, bf16[512,768]{1,0:T(8,128)(2,1)S(1)}, u32[]{:S(2)}, u32[]{:S(2)}) collective-permute-start(bf16[512,768]{1,0:T(8,128)(2,1)S(1)} %slice.67), channel_id=1, source_target_pairs={{1,0},{2,1},{3,2},{0,3},{12,4},{13,5},{14,6},{15,7},{9,8},{10,9},{... | collective-permute-start | bytes 2359304 | tf_op jit(solution)/shard_map/ppermute | solution.py:146
  35.7 12.4 %collective-permute-start.1 = (bf16[512,768]{1,0:T(8,128)(2,1)S(1)}, bf16[512,768]{1,0:T(8,128)(2,1)S(1)}, u32[]{:S(2)}, u32[]{:S(2)}) collective-permute-start(bf16[512,768]{1,0:T(8,128)(2,1)S(1)} %slice.67), channel_id=1, source_target_pairs={{0,1},{1,2},{2,3},{3,0},{4,12},{5,13},{6,14},{7,15},{8,9},{9,10},{... | collective-permute-start | bytes 2359304 | tf_op jit(solution)/shard_map/ppermute | solution.py:145
  36.2 9.7 %collective-permute-start.2 = (f32[2,512]{1,0:T(2,128)S(1)}, f32[2,512]{1,0:T(2,128)S(1)}, u32[]{:S(2)}, u32[]{:S(2)}) collective-permute-start(f32[2,512]{1,0:T(2,128)S(1)} %pad_maximum_fusion.1), channel_id=1, source_target_pairs={{1,0},{2,1},{3,2},{0,3},{12,4},{13,5},{14,6},{15,7},{9,8},{10,9},{... | collective-permute-start | bytes 12296 | tf_op jit(solution)/shard_map/ppermute | solution.py:148
  38.5 9.6 %collective-permute-start = (f32[2,512]{1,0:T(2,128)S(1)}, f32[2,512]{1,0:T(2,128)S(1)}, u32[]{:S(2)}, u32[]{:S(2)}) collective-permute-start(f32[2,512]{1,0:T(2,128)S(1)} %pad_maximum_fusion.1), channel_id=1, source_target_pairs={{0,1},{1,2},{2,3},{3,0},{4,12},{5,13},{6,14},{7,15},{8,9},{9,10},{... | collective-permute-start | bytes 12296 | tf_op jit(solution)/shard_map/ppermute | solution.py:147
  49.7 16.3 %copy-start = (s32[1,256]{1,0:T(1,128)S(1)}, s32[1,256]{1,0:T(1,128)}, u32[]{:S(2)}) copy-start(s32[1,256]{1,0:T(1,128)} %get-tuple-element.10) | copy-start | bytes 3076
  49.7 16.3 %copy-start.1 = (s32[1,256]{1,0:T(1,128)S(1)}, s32[1,256]{1,0:T(1,128)}, u32[]{:S(2)}) copy-start(s32[1,256]{1,0:T(1,128)} %get-tuple-element.11) | copy-start | bytes 3076
  49.7 16.3 %copy-start.2 = (s32[1,256]{1,0:T(1,128)S(1)}, s32[1,256]{1,0:T(1,128)}, u32[]{:S(2)}) copy-start(s32[1,256]{1,0:T(1,128)} %get-tuple-element.12) | copy-start | bytes 3076

commit v10 on v9

--- a/solution.py
+++ b/solution.py
@@ -114,6 +114,13 @@
     return rows[:, :width], cluster, order
 
 
+def unpack(ring, slots):
+    marks = ring[slots:].reshape(-1).astype(jnp.float32)
+    cluster = marks[:slots] - 1.0
+    order = marks[slots : 2 * slots] * 256.0 + marks[2 * slots : 3 * slots]
+    return ring[:slots], cluster, order
+
+
 def masks(query, keys):
     query_rows, query_cluster, query_order = query
     key_rows, key_cluster, key_order = keys
@@ -140,14 +147,10 @@
     forward = [(i, int(nxt[i])) for i in range(devices)]
     backward = [(int(nxt[i]), i) for i in range(devices)]
     query = split_meta(own, width)
-    data = query[0]
-    labels = jnp.stack([query[1], query[2]])
-    prev_data = lax.ppermute(data, ("dp", "blk"), forward)
-    next_data = lax.ppermute(data, ("dp", "blk"), backward)
-    prev_labels = lax.ppermute(labels, ("dp", "blk"), forward)
-    next_labels = lax.ppermute(labels, ("dp", "blk"), backward)
-    prev = (prev_data, prev_labels[0], prev_labels[1])
-    next_ = (next_data, next_labels[0], next_labels[1])
+    marks = jnp.concatenate([own[:, width + k] for k in range(3)]).reshape(-1, width)
+    ring = jnp.concatenate([query[0], marks], axis=0)
+    prev = unpack(lax.ppermute(ring, ("dp", "blk"), forward), slots)
+    next_ = unpack(lax.ppermute(ring, ("dp", "blk"), backward), slots)
     best = best_over(query, query)
     best = jnp.maximum(best, best_over(query, prev))
     best = jnp.maximum(best, best_over(query, next_))

time: 67.5 us -> 73 us (1.081)
  blocking collectives: 14 us -> 46.2 us
  waiting for transfers between devices: 25 us -> 8.19 us
  starting transfers between devices: 15.3 us -> 2.34 us
  matrix products: 4.06 us -> 6.46 us
  other arithmetic: 2.44 us -> 3.21 us
    all_to_all x0 -> x1, blocking collectives: none -> 29.2 us  [body(): lax.all_to_all(send, ('dp', 'blk'), split_axis=0, concat_axis=0, tiled=True)]
    all_to_all x1 -> x0, waiting for transfers between devices: 16 us -> none  [body(): lax.all_to_all(send, ('dp', 'blk'), split_axis=0, concat_axis=0, tiled=True)]
    all_to_all x1 -> x0, starting transfers between devices: 11.5 us -> none  [body(): lax.all_to_all(send, ('dp', 'blk'), split_axis=0, concat_axis=0, tiled=True)]
    all_to_all x1, blocking collectives: 14 us -> 16.9 us  [body(): lax.all_to_all(payload, ('dp', 'blk'), split_axis=0, concat_axis=0, tiled...]
    dot_general x4, matrix products: 2.59 us -> 4.99 us  [masks(): lax.dot_general(query_rows, key_rows, (((1,), (1,)), ((), ())), preferred...]
    ppermute x4 -> x2, starting transfers between devices: 3.79 us -> 2.34 us  [the longest x1 2.27 us: body(): next_ = unpack(lax.ppermute(ring, ('dp', 'blk'), backward), slots)]
    all_to_all x2, local copies, waits for them, and re-layouts: 1.35 us -> 0.42 us  [body(): lax.all_to_all(send, ('dp', 'blk'), split_axis=0, concat_axis=0, tiled=True)]
    ppermute x4 -> x2, waiting for transfers between devices: 8.99 us -> 8.19 us  [the longest x1 6.87 us: body(): prev = unpack(lax.ppermute(ring, ('dp', 'blk'), forward), slots)]
  transfers between devices with their start and end apart: 5 -> 2, of which waited for: 3 -> 2; matrix products, arithmetic and copies ran while one was open for 2% -> 2% of each run, Pallas kernels for 0% -> 0%
where the time goes in v10:
time: 73 us; the launch traced here: 72.7 us
  blocking collectives  46.2 us (63%)
  waiting for transfers between devices  8.19 us (11%)
  matrix products  6.46 us (9%)
  other arithmetic  3.21 us (4%)
  local copies, waits for them, and re-layouts  2.78 us (4%)
  starting transfers between devices  2.34 us (3%)
  Pallas kernels  2.05 us (3%)
  between operations  1.51 us (2%)
    all_to_all x1, blocking collectives, body(): lax.all_to_all(send, ('dp', 'blk'), split_axis=0, concat_axis=0, tiled=True)  29.2 us
    all_to_all x1, blocking collectives, body(): lax.all_to_all(payload, ('dp', 'blk'), split_axis=0, concat_axis=0, tiled...  16.9 us
    ppermute x1, waiting for transfers between devices, body(): prev = unpack(lax.ppermute(ring, ('dp', 'blk'), forward), slots)  6.87 us
    dot_general x4, matrix products, masks(): lax.dot_general(query_rows, key_rows, (((1,), (1,)), ((), ())), preferred...  4.99 us
    ppermute x1, starting transfers between devices, body(): next_ = unpack(lax.ppermute(ring, ('dp', 'blk'), backward), slots)  2.27 us
    pallas_call x1, Pallas kernels, build_send(): pl.pallas_call(prologue(dims), out_shape=(jax.ShapeDtypeStruct((points, w...  2.05 us
    dot_general x1, matrix products, build_send(): lax.dot_general(spot, packed, (((1,), (0,)), ((), ())), preferred_element...  1.47 us
  transfers between devices with their start and end apart: 2, of which 2 were waited for; matrix products, arithmetic and copies ran while one was open for 2% of the time, Pallas kernels for 0%

profile of v10, /device:TPU:1, one launch (start us, length us, event | category | flops | bytes accessed | tf_op | source)
XLA Modules:
  0.0 72.7 jit_solution(15127018230138431485)
XLA Ops:
  0.0 2.1 %shard_map.55 = (bf16[256,896]{1,0:T(8,128)(2,1)}, s32[1,256]{1,0:T(1,128)}, s32[1,256]{1,0:T(1,128)}, s32[1,256]{1,0:T(1,128)}, s32[1,256]{1,0:T(1,128)}) custom-call(bf16[256,768]{1,0:T(8,128)(2,1)} %emb_ref.1, s32[1,256]{1,0:T(1,128)} %bitcast.11, s32[1,256]{1,0:T(1,128)} %bitcast.12, s32[1,256]{1,0:T(1,128)} %bitcast.13), custom_call_target="tpu_custom_call" | custom-call | tf_op jit(solution)/shard_map/pallas_call | solution.py:93
  2.1 1.5 %convolution_convert_fusion = bf16[512,896]{1,0:T(8,128)(2,1)S(1)} fusion(bf16[256,896]{1,0:T(8,128)(2,1)} %get-tuple-element.14, s32[256]{0:T(256)} %bitcast.14), kind=kOutput, calls=%fused_computation.6 | convolution fusion | flops 235470848 | bytes 1377280 | tf_op jit(solution)/shard_map/dot_general | solution.py:105
  3.5 0.2 all_to_all.11
  3.7 29.2 %all_to_all.17 = bf16[128,4,896]{2,1,0:T(4,128)(2,1)S(1)} all-to-all(bf16[128,4,896]{2,1,0:T(4,128)(2,1)S(1)} %all_to_all.11), channel_id=1, replica_groups=mesh['dp'=32,'blk'=4] {'dp','blk'}, dimensions={0} | all-to-all | bytes 1835008 | tf_op jit(solution)/shard_map/all_to_all | solution.py:146
  33.0 0.2 all_to_all.13
  33.2 0.3 slice_reduce_fusion.2
  33.7 0.5 copy-done.3
  34.2 0.6 dynamic_slice.3
  36.1 2.3 %collective-permute-start.1 = (bf16[514,768]{1,0:T(8,128)(2,1)S(1)}, bf16[514,768]{1,0:T(8,128)(2,1)}, u32[]{:S(2)}, u32[]{:S(2)}) collective-permute-start(bf16[514,768]{1,0:T(8,128)(2,1)S(1)} %pad_maximum_fusion), channel_id=1, source_target_pairs={{1,0},{2,1},{3,2},{0,3},{12,4},{13,5},{14,6},{15,7},{9,8},{10,9},{... | collective-permute-start | bytes 2368520 | tf_op jit(solution)/shard_map/ppermute | solution.py:153
  38.3 0.3 add_reduce_fusion.1
  38.6 0.7 fusion.2
  39.3 6.9 %collective-permute-done = bf16[514,768]{1,0:T(8,128)(2,1)S(1)} collective-permute-done((bf16[514,768]{1,0:T(8,128)(2,1)S(1)}, bf16[514,768]{1,0:T(8,128)(2,1)S(1)}, u32[]{:S(2)}, u32[]{:S(2)}) %collective-permute-start) | collective-permute-done | bytes 789536 | tf_op jit(solution)/shard_map/ppermute | solution.py:152
  46.2 1.3 %collective-permute-done.1 = bf16[514,768]{1,0:T(8,128)(2,1)} collective-permute-done((bf16[514,768]{1,0:T(8,128)(2,1)S(1)}, bf16[514,768]{1,0:T(8,128)(2,1)}, u32[]{:S(2)}, u32[]{:S(2)}) %collective-permute-start.1) | collective-permute-done | bytes 789536 | tf_op jit(solution)/shard_map/ppermute | solution.py:153
  47.5 0.7 slice_convert_fusion
  48.2 0.7 fusion.3
  48.9 1.8 %fusion.4 = f32[512]{0:T(512)S(1)} fusion(bf16[514,768]{1,0:T(8,128)(2,1)} %collective-permute-done.1, f32[512]{0:T(512)S(1)} %get-tuple-element.16, f32[512]{0:T(512)S(1)} %get-tuple-element.15, f32[512]{0:T(512)S(1)} %get-tuple-element.24, f32[512]{0:T(512)S(1)} %get-tuple-element.27, bf16[512,896]{1,0:T(8,128)(2,1)S(1)} %all_to_all.13), kind=kOutput, calls=%fused_computation.12 | convolution fusion | flops 403963392 | bytes 1583104 | tf_op jit(solution)/shard_map/dot_general | solution.py:127
  50.7 0.1 max.26
  50.8 1.9 %select_reduce_fusion.2 = (f32[256]{0:T(256)S(1)}, f32[512]{0:T(512)S(1)}) fusion(f32[512]{0:T(512)S(1)} %get-tuple-element.22, f32[512]{0:T(512)S(1)} %get-tuple-element.25, f32[256]{0:T(256)S(1)} %get-tuple-element.31, f32[256]{0:T(256)S(1)} %get-tuple-element.30, pred[]{:T(512)} %bitcast.7, bf16[514,768]{1,0:T(8,128)(2,1)} %collective-permute-done.1, ...), kind=kOutput, calls=%fused_computation.24 | convolution fusion | flops 203095296 | bytes 2369536 | tf_op jit(solution)/shard_map/dot_general | solution.py:127
  52.8 0.1 reshape.91
  53.1 16.9 %all_to_all.18 = f32[128,1,12]{2,1,0:T(1,128)S(1)} all-to-all(f32[128,1,12]{2,1,0:T(1,128)S(1)} %bitcast.10), channel_id=1, replica_groups=mesh['dp'=32,'blk'=4] {'dp','blk'}, dimensions={0} | all-to-all | bytes 12288 | tf_op jit(solution)/shard_map/all_to_all | solution.py:172
  70.0 0.5 broadcast.59
  70.6 0.8 %reduce.13 = f32[128,12]{1,0:T(8,128)S(1)} reduce(f32[128,1,12]{2,1,0:T(1,128)S(1)} %all_to_all.18, f32[]{:T(128)} %broadcast.59), dimensions={1}, to_apply=%all_to_all.14.reduce_sub_computation.3 | reduce | bytes 12292 | tf_op jit(solution)/shard_map/all_to_all | solution.py:172
  71.5 0.6 select_reduce_fusion
  72.1 0.6 compare_select_fusion
  (23 shorter events, 0.6 us)
Async XLA Ops:
  33.5 0.7 copy-start.3
  33.6 12.5 %collective-permute-start = (bf16[514,768]{1,0:T(8,128)(2,1)S(1)}, bf16[514,768]{1,0:T(8,128)(2,1)S(1)}, u32[]{:S(2)}, u32[]{:S(2)}) collective-permute-start(bf16[514,768]{1,0:T(8,128)(2,1)S(1)} %pad_maximum_fusion), channel_id=1, source_target_pairs={{0,1},{1,2},{2,3},{3,0},{4,12},{5,13},{6,14},{7,15},{8,9},{9,10},{... | collective-permute-start | bytes 2368520 | tf_op jit(solution)/shard_map/ppermute | solution.py:152
  36.1 11.4 %collective-permute-start.1 = (bf16[514,768]{1,0:T(8,128)(2,1)S(1)}, bf16[514,768]{1,0:T(8,128)(2,1)}, u32[]{:S(2)}, u32[]{:S(2)}) collective-permute-start(bf16[514,768]{1,0:T(8,128)(2,1)S(1)} %pad_maximum_fusion), channel_id=1, source_target_pairs={{1,0},{2,1},{3,2},{0,3},{12,4},{13,5},{14,6},{15,7},{9,8},{10,9},{... | collective-permute-start | bytes 2368520 | tf_op jit(solution)/shard_map/ppermute | solution.py:153
  50.8 20.7 %copy-start = (s32[1,256]{1,0:T(1,128)S(1)}, s32[1,256]{1,0:T(1,128)}, u32[]{:S(2)}) copy-start(s32[1,256]{1,0:T(1,128)} %get-tuple-element.10) | copy-start | bytes 3076
  50.8 20.7 %copy-start.1 = (s32[1,256]{1,0:T(1,128)S(1)}, s32[1,256]{1,0:T(1,128)}, u32[]{:S(2)}) copy-start(s32[1,256]{1,0:T(1,128)} %get-tuple-element.11) | copy-start | bytes 3076
  50.8 20.7 %copy-start.2 = (s32[1,256]{1,0:T(1,128)S(1)}, s32[1,256]{1,0:T(1,128)}, u32[]{:S(2)}) copy-start(s32[1,256]{1,0:T(1,128)} %get-tuple-element.12) | copy-start | bytes 3076

commit v11 on v9

--- a/solution.py
+++ b/solution.py
@@ -6,13 +6,6 @@
 from jax.experimental import pallas as pl
 
 EXTRA = 128
-
-
-def normalize(embeddings):
-    values = embeddings.astype(jnp.float32)
-    scale = lax.rsqrt(jnp.mean(values * values, axis=1, keepdims=True) + 1e-06)
-    width = embeddings.shape[1]
-    return (values * scale * width ** (-0.5)).astype(jnp.bfloat16)
 
 
 def ring_of(zs, xs, ys):
@@ -29,13 +22,6 @@
                 ring_pos[lin(z, x, 0, y)] = y
                 ring_pos[lin(z, x, 1, y)] = x
     return nxt, ring_pos
-
-
-def device_of(group, place, zs, xs, ys):
-    first = group * 2 * ys + place
-    other = group - zs * xs
-    second = ((other // ys * xs + place) * 2 + 1) * ys + other % ys
-    return jnp.where(group < zs * xs, first, second)
 
 
 def place_of(group, place, zs, xs, ys):
@@ -130,9 +116,8 @@
 
 
 def body(embeddings, point_group, point_cluster, point_order, nxt, ring_pos, dims):
-    zs, xs, ys = dims
     devices = nxt.shape[0]
-    points, width = embeddings.shape
+    _, width = embeddings.shape
     slots = devices * 4
     group = point_group[:, 0]
     send, idx = build_send(embeddings, group, point_cluster, point_order, slots, dims)
@@ -142,10 +127,10 @@
     query = split_meta(own, width)
     data = query[0]
     labels = jnp.stack([query[1], query[2]])
+    prev_labels = lax.ppermute(labels, ("dp", "blk"), forward)
+    next_labels = lax.ppermute(labels, ("dp", "blk"), backward)
     prev_data = lax.ppermute(data, ("dp", "blk"), forward)
     next_data = lax.ppermute(data, ("dp", "blk"), backward)
-    prev_labels = lax.ppermute(labels, ("dp", "blk"), forward)
-    next_labels = lax.ppermute(labels, ("dp", "blk"), backward)
     prev = (prev_data, prev_labels[0], prev_labels[1])
     next_ = (next_data, next_labels[0], next_labels[1])
     best = best_over(query, query)

time: 67.5 us -> 67.5 us (level)
  no operation moved by 1% of the time
where the time goes in v11:
time: 67.5 us; the launch traced here: 67.2 us
  waiting for transfers between devices  25 us (37%)
  starting transfers between devices  15.3 us (23%)
  blocking collectives  14 us (21%)
  matrix products  4.06 us (6%)
  local copies, waits for them, and re-layouts  2.93 us (4%)
  other arithmetic  2.44 us (4%)
  Pallas kernels  2.05 us (3%)
  between operations  1.49 us (2%)
    all_to_all x1, waiting for transfers between devices, body(): lax.all_to_all(send, ('dp', 'blk'), split_axis=0, concat_axis=0, tiled=True)  16 us
    all_to_all x1, blocking collectives, body(): lax.all_to_all(payload, ('dp', 'blk'), split_axis=0, concat_axis=0, tiled...  14 us
    all_to_all x1, starting transfers between devices, body(): lax.all_to_all(send, ('dp', 'blk'), split_axis=0, concat_axis=0, tiled=True)  11.5 us
    ppermute x1, waiting for transfers between devices, body(): next_labels = lax.ppermute(labels, ('dp', 'blk'), backward)  6.79 us
    dot_general x4, matrix products, masks(): lax.dot_general(query_rows, key_rows, (((1,), (1,)), ((), ())), preferred...  2.59 us
    ppermute x1, starting transfers between devices, body(): next_labels = lax.ppermute(labels, ('dp', 'blk'), backward)  2.26 us
    ppermute x1, waiting for transfers between devices, body(): prev_labels = lax.ppermute(labels, ('dp', 'blk'), forward)  2.19 us
    pallas_call x1, Pallas kernels, build_send(): pl.pallas_call(prologue(dims), out_shape=(jax.ShapeDtypeStruct((points, w...  2.05 us
  transfers between devices with their start and end apart: 5, of which 3 were waited for; matrix products, arithmetic and copies ran while one was open for 2% of the time, Pallas kernels for 0%

profile of v11, /device:TPU:1, one launch (start us, length us, event | category | flops | bytes accessed | tf_op | source)
XLA Modules:
  0.0 67.2 jit_solution(18436905481226840497)
XLA Ops:
  0.0 2.1 %shard_map.55 = (bf16[256,896]{1,0:T(8,128)(2,1)}, s32[1,256]{1,0:T(1,128)}, s32[1,256]{1,0:T(1,128)}, s32[1,256]{1,0:T(1,128)}, s32[1,256]{1,0:T(1,128)}) custom-call(bf16[256,768]{1,0:T(8,128)(2,1)} %emb_ref.1, s32[1,256]{1,0:T(1,128)} %bitcast.31, s32[1,256]{1,0:T(1,128)} %bitcast.32, s32[1,256]{1,0:T(1,128)} %bitcast.33), custom_call_target="tpu_custom_call" | custom-call | tf_op jit(solution)/shard_map/pallas_call | solution.py:79
  2.1 1.5 %convolution_convert_fusion = bf16[512,896]{1,0:T(8,128)(2,1)S(1)} fusion(bf16[256,896]{1,0:T(8,128)(2,1)} %get-tuple-element.14, s32[256]{0:T(256)} %bitcast.34), kind=kOutput, calls=%fused_computation.6 | convolution fusion | flops 235470848 | bytes 1377280 | tf_op jit(solution)/shard_map/dot_general | solution.py:91
  3.5 1.1 %all_to_all.11 = bf16[128,4,896]{2,1,0:T(4,128)(2,1)} reshape(bf16[512,896]{1,0:T(8,128)(2,1)S(1)} %convolution_convert_fusion) | data formatting | bytes 1835008 | tf_op jit(solution)/shard_map/all_to_all | solution.py:124
  4.7 11.5 %all-to-all-start = ((bf16[128,4,896]{2,1,0:T(4,128)(2,1)}), bf16[128,4,896]{2,1,0:T(4,128)(2,1)S(1)}, u32[]{:S(2)}, u32[]{:S(2)}) async-start(bf16[128,4,896]{2,1,0:T(4,128)(2,1)} %all_to_all.11), calls=%async_computation | async-start | bytes 1835008 | tf_op jit(solution)/shard_map/all_to_all | solution.py:124
  16.2 0.6 dynamic_slice.3
  18.1 16.0 %all-to-all-done = bf16[128,4,896]{2,1,0:T(4,128)(2,1)S(1)} async-done(((bf16[128,4,896]{2,1,0:T(4,128)(2,1)}), bf16[128,4,896]{2,1,0:T(4,128)(2,1)S(1)}, u32[]{:S(2)}, u32[]{:S(2)}) %all-to-all-start) | async-done | bytes 917536 | tf_op jit(solution)/shard_map/all_to_all | solution.py:124
  34.1 0.2 all_to_all.13
  34.3 0.3 add_reduce_fusion.1
  34.7 1.1 %collective-permute-start.3 = (bf16[512,768]{1,0:T(8,128)(2,1)S(1)}, bf16[512,768]{1,0:T(8,128)(2,1)S(1)}, u32[]{:S(2)}, u32[]{:S(2)}) collective-permute-start(bf16[512,768]{1,0:T(8,128)(2,1)S(1)} %slice.67), channel_id=1, source_target_pairs={{1,0},{2,1},{3,2},{0,3},{12,4},{13,5},{14,6},{15,7},{9,8},{10,9},{... | collective-permute-start | bytes 2359304 | tf_op jit(solution)/shard_map/ppermute | solution.py:133
  35.7 0.5 collective-permute-start.1
  36.2 2.3 %collective-permute-start.2 = (f32[2,512]{1,0:T(2,128)S(1)}, f32[2,512]{1,0:T(2,128)S(1)}, u32[]{:S(2)}, u32[]{:S(2)}) collective-permute-start(f32[2,512]{1,0:T(2,128)S(1)} %pad_maximum_fusion.1), channel_id=1, source_target_pairs={{1,0},{2,1},{3,2},{0,3},{12,4},{13,5},{14,6},{15,7},{9,8},{10,9},{... | collective-permute-start | bytes 12296 | tf_op jit(solution)/shard_map/ppermute | solution.py:131
  38.5 0.6 fusion.2
  39.1 6.8 %collective-permute-done.2 = f32[2,512]{1,0:T(2,128)S(1)} collective-permute-done((f32[2,512]{1,0:T(2,128)S(1)}, f32[2,512]{1,0:T(2,128)S(1)}, u32[]{:S(2)}, u32[]{:S(2)}) %collective-permute-start.2) | collective-permute-done | bytes 4128 | tf_op jit(solution)/shard_map/ppermute | solution.py:131
  45.9 2.2 %collective-permute-done = f32[2,512]{1,0:T(2,128)S(1)} collective-permute-done((f32[2,512]{1,0:T(2,128)S(1)}, f32[2,512]{1,0:T(2,128)S(1)}, u32[]{:S(2)}, u32[]{:S(2)}) %collective-permute-start) | collective-permute-done | bytes 4128 | tf_op jit(solution)/shard_map/ppermute | solution.py:130
  48.1 0.6 select_reduce_fusion.4
  48.8 0.1 reshape.140
  48.9 0.1 reshape.139
  49.0 0.7 select_reduce_fusion.1
  49.7 0.7 select_reduce_fusion.2
  50.6 14.0 %all_to_all.17 = f32[128,1,12]{2,1,0:T(1,128)S(1)} all-to-all(f32[128,1,12]{2,1,0:T(1,128)S(1)} %bitcast.22), channel_id=1, replica_groups=mesh['dp'=32,'blk'=4] {'dp','blk'}, dimensions={0} | all-to-all | bytes 12288 | tf_op jit(solution)/shard_map/all_to_all | solution.py:154
  64.6 0.5 broadcast.55
  65.1 0.8 %reduce.9 = f32[128,12]{1,0:T(8,128)S(1)} reduce(f32[128,1,12]{2,1,0:T(1,128)S(1)} %all_to_all.17, f32[]{:T(128)} %broadcast.55), dimensions={1}, to_apply=%all_to_all.14.reduce_sub_computation.3 | reduce | bytes 12292 | tf_op jit(solution)/shard_map/all_to_all | solution.py:154
  66.1 0.6 select_reduce_fusion
  66.7 0.6 compare_select_fusion
  (20 shorter events, 0.4 us)
Async XLA Ops:
  4.7 11.5 %copy-start.3 = (s32[128]{0:T(128)S(1)}, s32[128]{0:T(128)}, u32[]{:S(2)}) copy-start(s32[128]{0:T(128)} %constant.36.clone) | copy-start | bytes 1540
  4.7 29.4 %all-to-all-start = ((bf16[128,4,896]{2,1,0:T(4,128)(2,1)}), bf16[128,4,896]{2,1,0:T(4,128)(2,1)S(1)}, u32[]{:S(2)}, u32[]{:S(2)}) async-start(bf16[128,4,896]{2,1,0:T(4,128)(2,1)} %all_to_all.11), calls=%async_computation | async-start | bytes 1835008 | tf_op jit(solution)/shard_map/all_to_all | solution.py:124
  34.7 13.5 %collective-permute-start.3 = (bf16[512,768]{1,0:T(8,128)(2,1)S(1)}, bf16[512,768]{1,0:T(8,128)(2,1)S(1)}, u32[]{:S(2)}, u32[]{:S(2)}) collective-permute-start(bf16[512,768]{1,0:T(8,128)(2,1)S(1)} %slice.67), channel_id=1, source_target_pairs={{1,0},{2,1},{3,2},{0,3},{12,4},{13,5},{14,6},{15,7},{9,8},{10,9},{... | collective-permute-start | bytes 2359304 | tf_op jit(solution)/shard_map/ppermute | solution.py:133
  35.7 12.4 %collective-permute-start.1 = (bf16[512,768]{1,0:T(8,128)(2,1)S(1)}, bf16[512,768]{1,0:T(8,128)(2,1)S(1)}, u32[]{:S(2)}, u32[]{:S(2)}) collective-permute-start(bf16[512,768]{1,0:T(8,128)(2,1)S(1)} %slice.67), channel_id=1, source_target_pairs={{0,1},{1,2},{2,3},{3,0},{4,12},{5,13},{6,14},{7,15},{8,9},{9,10},{... | collective-permute-start | bytes 2359304 | tf_op jit(solution)/shard_map/ppermute | solution.py:132
  36.2 9.7 %collective-permute-start.2 = (f32[2,512]{1,0:T(2,128)S(1)}, f32[2,512]{1,0:T(2,128)S(1)}, u32[]{:S(2)}, u32[]{:S(2)}) collective-permute-start(f32[2,512]{1,0:T(2,128)S(1)} %pad_maximum_fusion.1), channel_id=1, source_target_pairs={{1,0},{2,1},{3,2},{0,3},{12,4},{13,5},{14,6},{15,7},{9,8},{10,9},{... | collective-permute-start | bytes 12296 | tf_op jit(solution)/shard_map/ppermute | solution.py:131
  38.5 9.6 %collective-permute-start = (f32[2,512]{1,0:T(2,128)S(1)}, f32[2,512]{1,0:T(2,128)S(1)}, u32[]{:S(2)}, u32[]{:S(2)}) collective-permute-start(f32[2,512]{1,0:T(2,128)S(1)} %pad_maximum_fusion.1), channel_id=1, source_target_pairs={{0,1},{1,2},{2,3},{3,0},{4,12},{5,13},{6,14},{7,15},{8,9},{9,10},{... | collective-permute-start | bytes 12296 | tf_op jit(solution)/shard_map/ppermute | solution.py:130
  49.7 16.3 %copy-start = (s32[1,256]{1,0:T(1,128)S(1)}, s32[1,256]{1,0:T(1,128)}, u32[]{:S(2)}) copy-start(s32[1,256]{1,0:T(1,128)} %get-tuple-element.10) | copy-start | bytes 3076
  49.7 16.3 %copy-start.1 = (s32[1,256]{1,0:T(1,128)S(1)}, s32[1,256]{1,0:T(1,128)}, u32[]{:S(2)}) copy-start(s32[1,256]{1,0:T(1,128)} %get-tuple-element.11) | copy-start | bytes 3076
  49.7 16.3 %copy-start.2 = (s32[1,256]{1,0:T(1,128)S(1)}, s32[1,256]{1,0:T(1,128)}, u32[]{:S(2)}) copy-start(s32[1,256]{1,0:T(1,128)} %get-tuple-element.12) | copy-start | bytes 3076

commit v12 on v11

--- a/solution.py
+++ b/solution.py
@@ -115,7 +115,8 @@
     return jnp.max(jnp.where(same & earlier, scores, -2.0), axis=1)
 
 
-def body(embeddings, point_group, point_cluster, point_order, nxt, ring_pos, dims):
+def body(embeddings, point_group, point_cluster, point_order, nxt, dims):
+    _, xs, ys = dims
     devices = nxt.shape[0]
     _, width = embeddings.shape
     slots = devices * 4
@@ -127,17 +128,18 @@
     query = split_meta(own, width)
     data = query[0]
     labels = jnp.stack([query[1], query[2]])
+    prev_data = lax.ppermute(data, ("dp", "blk"), forward)
+    next_data = lax.ppermute(data, ("dp", "blk"), backward)
     prev_labels = lax.ppermute(labels, ("dp", "blk"), forward)
     next_labels = lax.ppermute(labels, ("dp", "blk"), backward)
-    prev_data = lax.ppermute(data, ("dp", "blk"), forward)
-    next_data = lax.ppermute(data, ("dp", "blk"), backward)
     prev = (prev_data, prev_labels[0], prev_labels[1])
     next_ = (next_data, next_labels[0], next_labels[1])
     best = best_over(query, query)
     best = jnp.maximum(best, best_over(query, prev))
     best = jnp.maximum(best, best_over(query, next_))
     half = slots // 2
-    me = jnp.asarray(ring_pos)[lax.axis_index(("dp", "blk"))]
+    here = lax.axis_index(("dp", "blk"))
+    me = jnp.where((here // ys) % 2 == 0, here % ys, (here // (2 * ys)) % xs)
     inner = (me == 1) | (me == 2)
     rows = tuple(jnp.where(inner, p[:half], n[half:]) for p, n in zip(prev, next_))
     cols = tuple(jnp.where(inner, n, p) for p, n in zip(prev, next_))
@@ -163,11 +165,11 @@
 
 def solution(mesh):
     dims = (4, 4, 4)
-    nxt, ring_pos = ring_of(*dims)
+    nxt, _ = ring_of(*dims)
     in_specs = (P(("dp", "blk"), None), P(("dp", "blk"), None), P(("dp", "blk")), P(("dp", "blk")))
     out_specs = P(("dp", "blk"))
 
     def run(embeddings, point_group, point_cluster, point_order):
-        return body(embeddings, point_group, point_cluster, point_order, nxt, ring_pos, dims)
+        return body(embeddings, point_group, point_cluster, point_order, nxt, dims)
 
     return jax.shard_map(run, mesh=mesh, in_specs=in_specs, out_specs=out_specs, check_vma=False)

time: 67.5 us -> 67.5 us (level)
  waiting for transfers between devices: 25 us -> 26.8 us
  between operations: 1.49 us -> 0.24 us
    all_to_all x1, waiting for transfers between devices: 16 us -> 17.9 us  [body(): lax.all_to_all(send, ('dp', 'blk'), split_axis=0, concat_axis=0, tiled=True)]
  transfers between devices with their start and end apart: 5 -> 5, of which waited for: 3 -> 3; matrix products, arithmetic and copies ran while one was open for 2% -> 1% of each run, Pallas kernels for 0% -> 0%
where the time goes in v12:
time: 67.5 us; the launch traced here: 67.2 us
  waiting for transfers between devices  26.8 us (40%)
  starting transfers between devices  15.3 us (23%)
  blocking collectives  14 us (21%)
  matrix products  4.07 us (6%)
  other arithmetic  2.44 us (4%)
  local copies, waits for them, and re-layouts  2.34 us (3%)
  Pallas kernels  2.05 us (3%)
    all_to_all x1, waiting for transfers between devices, body(): lax.all_to_all(send, ('dp', 'blk'), split_axis=0, concat_axis=0, tiled=True)  17.9 us
    all_to_all x1, blocking collectives, body(): lax.all_to_all(payload, ('dp', 'blk'), split_axis=0, concat_axis=0, tiled...  14 us
    all_to_all x1, starting transfers between devices, body(): lax.all_to_all(send, ('dp', 'blk'), split_axis=0, concat_axis=0, tiled=True)  11.5 us
    ppermute x1, waiting for transfers between devices, body(): next_labels = lax.ppermute(labels, ('dp', 'blk'), backward)  6.79 us
    dot_general x4, matrix products, masks(): lax.dot_general(query_rows, key_rows, (((1,), (1,)), ((), ())), preferred...  2.6 us
    ppermute x1, starting transfers between devices, body(): next_labels = lax.ppermute(labels, ('dp', 'blk'), backward)  2.26 us
    ppermute x1, waiting for transfers between devices, body(): prev_labels = lax.ppermute(labels, ('dp', 'blk'), forward)  2.19 us
    pallas_call x1, Pallas kernels, build_send(): pl.pallas_call(prologue(dims), out_shape=(jax.ShapeDtypeStruct((points, w...  2.05 us
  transfers between devices with their start and end apart: 5, of which 3 were waited for; matrix products, arithmetic and copies ran while one was open for 1% of the time, Pallas kernels for 0%

profile of v12, /device:TPU:1, one launch (start us, length us, event | category | flops | bytes accessed | tf_op | source)
XLA Modules:
  0.0 67.2 jit_solution(1478520087119246162)
XLA Ops:
  0.0 2.1 %shard_map.46 = (bf16[256,896]{1,0:T(8,128)(2,1)}, s32[1,256]{1,0:T(1,128)}, s32[1,256]{1,0:T(1,128)}, s32[1,256]{1,0:T(1,128)}, s32[1,256]{1,0:T(1,128)}) custom-call(bf16[256,768]{1,0:T(8,128)(2,1)} %emb_ref.1, s32[1,256]{1,0:T(1,128)} %bitcast.30, s32[1,256]{1,0:T(1,128)} %bitcast.31, s32[1,256]{1,0:T(1,128)} %bitcast.32), custom_call_target="tpu_custom_call" | custom-call | tf_op jit(solution)/shard_map/pallas_call | solution.py:79
  2.1 1.5 %convolution_convert_fusion = bf16[512,896]{1,0:T(8,128)(2,1)S(1)} fusion(bf16[256,896]{1,0:T(8,128)(2,1)} %get-tuple-element.14, s32[256]{0:T(256)} %bitcast.33), kind=kOutput, calls=%fused_computation.6 | convolution fusion | flops 235470848 | bytes 1377280 | tf_op jit(solution)/shard_map/dot_general | solution.py:91
  3.5 1.1 %all_to_all.11 = bf16[128,4,896]{2,1,0:T(4,128)(2,1)} reshape(bf16[512,896]{1,0:T(8,128)(2,1)S(1)} %convolution_convert_fusion) | data formatting | bytes 1835008 | tf_op jit(solution)/shard_map/all_to_all | solution.py:125
  4.7 11.5 %all-to-all-start = ((bf16[128,4,896]{2,1,0:T(4,128)(2,1)}), bf16[128,4,896]{2,1,0:T(4,128)(2,1)S(1)}, u32[]{:S(2)}, u32[]{:S(2)}) async-start(bf16[128,4,896]{2,1,0:T(4,128)(2,1)} %all_to_all.11), calls=%async_computation | async-start | bytes 1835008 | tf_op jit(solution)/shard_map/all_to_all | solution.py:125
  16.2 17.9 %all-to-all-done = bf16[128,4,896]{2,1,0:T(4,128)(2,1)S(1)} async-done(((bf16[128,4,896]{2,1,0:T(4,128)(2,1)}), bf16[128,4,896]{2,1,0:T(4,128)(2,1)S(1)}, u32[]{:S(2)}, u32[]{:S(2)}) %all-to-all-start) | async-done | bytes 917536 | tf_op jit(solution)/shard_map/all_to_all | solution.py:125
  34.1 0.2 all_to_all.13
  34.3 0.3 add_reduce_fusion.1
  34.7 1.1 %collective-permute-start.3 = (bf16[512,768]{1,0:T(8,128)(2,1)S(1)}, bf16[512,768]{1,0:T(8,128)(2,1)S(1)}, u32[]{:S(2)}, u32[]{:S(2)}) collective-permute-start(bf16[512,768]{1,0:T(8,128)(2,1)S(1)} %slice.67), channel_id=1, source_target_pairs={{1,0},{2,1},{3,2},{0,3},{12,4},{13,5},{14,6},{15,7},{9,8},{10,9},{... | collective-permute-start | bytes 2359304 | tf_op jit(solution)/shard_map/ppermute | solution.py:132
  35.7 0.5 collective-permute-start.1
  36.2 2.3 %collective-permute-start.2 = (f32[2,512]{1,0:T(2,128)S(1)}, f32[2,512]{1,0:T(2,128)S(1)}, u32[]{:S(2)}, u32[]{:S(2)}) collective-permute-start(f32[2,512]{1,0:T(2,128)S(1)} %pad_maximum_fusion.1), channel_id=1, source_target_pairs={{1,0},{2,1},{3,2},{0,3},{12,4},{13,5},{14,6},{15,7},{9,8},{10,9},{... | collective-permute-start | bytes 12296 | tf_op jit(solution)/shard_map/ppermute | solution.py:134
  38.5 0.7 fusion.2
  39.1 6.8 %collective-permute-done.2 = f32[2,512]{1,0:T(2,128)S(1)} collective-permute-done((f32[2,512]{1,0:T(2,128)S(1)}, f32[2,512]{1,0:T(2,128)S(1)}, u32[]{:S(2)}, u32[]{:S(2)}) %collective-permute-start.2) | collective-permute-done | bytes 4128 | tf_op jit(solution)/shard_map/ppermute | solution.py:134
  45.9 2.2 %collective-permute-done = f32[2,512]{1,0:T(2,128)S(1)} collective-permute-done((f32[2,512]{1,0:T(2,128)S(1)}, f32[2,512]{1,0:T(2,128)S(1)}, u32[]{:S(2)}, u32[]{:S(2)}) %collective-permute-start) | collective-permute-done | bytes 4128 | tf_op jit(solution)/shard_map/ppermute | solution.py:133
  48.1 0.6 select_reduce_fusion.4
  48.8 0.1 reshape.135
  48.9 0.1 reshape.134
  49.0 0.7 select_reduce_fusion.1
  49.7 0.7 select_reduce_fusion.2
  50.4 0.1 max.26
  50.6 14.0 %all_to_all.17 = f32[128,1,12]{2,1,0:T(1,128)S(1)} all-to-all(f32[128,1,12]{2,1,0:T(1,128)S(1)} %bitcast.21), channel_id=1, replica_groups=mesh['dp'=32,'blk'=4] {'dp','blk'}, dimensions={0} | all-to-all | bytes 12288 | tf_op jit(solution)/shard_map/all_to_all | solution.py:156
  64.6 0.5 broadcast.60
  65.1 0.8 %reduce.9 = f32[128,12]{1,0:T(8,128)S(1)} reduce(f32[128,1,12]{2,1,0:T(1,128)S(1)} %all_to_all.17, f32[]{:T(128)} %broadcast.60), dimensions={1}, to_apply=%all_to_all.14.reduce_sub_computation.3 | reduce | bytes 12292 | tf_op jit(solution)/shard_map/all_to_all | solution.py:156
  66.0 0.6 select_reduce_fusion
  66.7 0.6 compare_select_fusion
  (17 shorter events, 0.3 us)
Async XLA Ops:
  4.7 29.4 %all-to-all-start = ((bf16[128,4,896]{2,1,0:T(4,128)(2,1)}), bf16[128,4,896]{2,1,0:T(4,128)(2,1)S(1)}, u32[]{:S(2)}, u32[]{:S(2)}) async-start(bf16[128,4,896]{2,1,0:T(4,128)(2,1)} %all_to_all.11), calls=%async_computation | async-start | bytes 1835008 | tf_op jit(solution)/shard_map/all_to_all | solution.py:125
  34.7 13.5 %collective-permute-start.3 = (bf16[512,768]{1,0:T(8,128)(2,1)S(1)}, bf16[512,768]{1,0:T(8,128)(2,1)S(1)}, u32[]{:S(2)}, u32[]{:S(2)}) collective-permute-start(bf16[512,768]{1,0:T(8,128)(2,1)S(1)} %slice.67), channel_id=1, source_target_pairs={{1,0},{2,1},{3,2},{0,3},{12,4},{13,5},{14,6},{15,7},{9,8},{10,9},{... | collective-permute-start | bytes 2359304 | tf_op jit(solution)/shard_map/ppermute | solution.py:132
  35.7 12.4 %collective-permute-start.1 = (bf16[512,768]{1,0:T(8,128)(2,1)S(1)}, bf16[512,768]{1,0:T(8,128)(2,1)S(1)}, u32[]{:S(2)}, u32[]{:S(2)}) collective-permute-start(bf16[512,768]{1,0:T(8,128)(2,1)S(1)} %slice.67), channel_id=1, source_target_pairs={{0,1},{1,2},{2,3},{3,0},{4,12},{5,13},{6,14},{7,15},{8,9},{9,10},{... | collective-permute-start | bytes 2359304 | tf_op jit(solution)/shard_map/ppermute | solution.py:131
  36.2 9.7 %collective-permute-start.2 = (f32[2,512]{1,0:T(2,128)S(1)}, f32[2,512]{1,0:T(2,128)S(1)}, u32[]{:S(2)}, u32[]{:S(2)}) collective-permute-start(f32[2,512]{1,0:T(2,128)S(1)} %pad_maximum_fusion.1), channel_id=1, source_target_pairs={{1,0},{2,1},{3,2},{0,3},{12,4},{13,5},{14,6},{15,7},{9,8},{10,9},{... | collective-permute-start | bytes 12296 | tf_op jit(solution)/shard_map/ppermute | solution.py:134
  38.5 9.6 %collective-permute-start = (f32[2,512]{1,0:T(2,128)S(1)}, f32[2,512]{1,0:T(2,128)S(1)}, u32[]{:S(2)}, u32[]{:S(2)}) collective-permute-start(f32[2,512]{1,0:T(2,128)S(1)} %pad_maximum_fusion.1), channel_id=1, source_target_pairs={{0,1},{1,2},{2,3},{3,0},{4,12},{5,13},{6,14},{7,15},{8,9},{9,10},{... | collective-permute-start | bytes 12296 | tf_op jit(solution)/shard_map/ppermute | solution.py:133
  49.7 16.3 %copy-start = (s32[1,256]{1,0:T(1,128)S(1)}, s32[1,256]{1,0:T(1,128)}, u32[]{:S(2)}) copy-start(s32[1,256]{1,0:T(1,128)} %get-tuple-element.10) | copy-start | bytes 3076
  49.7 16.3 %copy-start.1 = (s32[1,256]{1,0:T(1,128)S(1)}, s32[1,256]{1,0:T(1,128)}, u32[]{:S(2)}) copy-start(s32[1,256]{1,0:T(1,128)} %get-tuple-element.11) | copy-start | bytes 3076
  49.7 16.3 %copy-start.2 = (s32[1,256]{1,0:T(1,128)S(1)}, s32[1,256]{1,0:T(1,128)}, u32[]{:S(2)}) copy-start(s32[1,256]{1,0:T(1,128)} %get-tuple-element.12) | copy-start | bytes 3076

commit v13 on v12

--- a/solution.py
+++ b/solution.py
@@ -135,14 +135,16 @@
     prev = (prev_data, prev_labels[0], prev_labels[1])
     next_ = (next_data, next_labels[0], next_labels[1])
     best = best_over(query, query)
-    best = jnp.maximum(best, best_over(query, prev))
+    near = best_over(query, prev)
+    best = jnp.maximum(best, near)
     best = jnp.maximum(best, best_over(query, next_))
     half = slots // 2
     here = lax.axis_index(("dp", "blk"))
     me = jnp.where((here // ys) % 2 == 0, here % ys, (here // (2 * ys)) % xs)
     inner = (me == 1) | (me == 2)
-    rows = tuple(jnp.where(inner, p[:half], n[half:]) for p, n in zip(prev, next_))
-    cols = tuple(jnp.where(inner, n, p) for p, n in zip(prev, next_))
+    far_prev = (prev[0],) + lax.optimization_barrier(prev[1:])
+    rows = tuple(jnp.where(inner, p[:half], n[half:]) for p, n in zip(far_prev, next_))
+    cols = tuple(jnp.where(inner, n, p) for p, n in zip(far_prev, next_))
     scores, same_c, earlier = masks(rows, cols)
     row_part = jnp.max(jnp.where(same_c & earlier, scores, -2.0), axis=1)
     col_ok = same_c & (rows[2][:, None] < cols[2][None, :])

time: 67.5 us -> 70 us (1.037)
  waiting for transfers between devices: 26.8 us -> 28.8 us
    ppermute x1, waiting for transfers between devices: 0.01 us -> 7.88 us  [body(): next_data = lax.ppermute(data, ('dp', 'blk'), backward)]
    ppermute x1, waiting for transfers between devices: 6.79 us -> 0.01 us  [body(): next_labels = lax.ppermute(labels, ('dp', 'blk'), backward)]
    ppermute x1, waiting for transfers between devices: 0.01 us -> 2.75 us  [body(): prev_data = lax.ppermute(data, ('dp', 'blk'), forward)]
    ppermute x1, waiting for transfers between devices: 2.19 us -> 0.34 us  [body(): prev_labels = lax.ppermute(labels, ('dp', 'blk'), forward)]
    ppermute x1, starting transfers between devices: 2.26 us -> 1.05 us  [body(): next_labels = lax.ppermute(labels, ('dp', 'blk'), backward)]
    ppermute x1, starting transfers between devices: 1.05 us -> 2.19 us  [body(): next_data = lax.ppermute(data, ('dp', 'blk'), backward)]
  transfers between devices with their start and end apart: 5 -> 5, of which waited for: 3 -> 4; matrix products, arithmetic and copies ran while one was open for 1% -> 2% of each run, Pallas kernels for 0% -> 0%
where the time goes in v13:
time: 70 us; the launch traced here: 69.8 us
  waiting for transfers between devices  28.8 us (41%)
  starting transfers between devices  15.2 us (22%)
  blocking collectives  14.6 us (21%)
  matrix products  4.05 us (6%)
  other arithmetic  2.44 us (3%)
  local copies, waits for them, and re-layouts  2.35 us (3%)
  Pallas kernels  2.05 us (3%)
    all_to_all x1, waiting for transfers between devices, body(): lax.all_to_all(send, ('dp', 'blk'), split_axis=0, concat_axis=0, tiled=True)  17.9 us
    all_to_all x1, blocking collectives, body(): lax.all_to_all(payload, ('dp', 'blk'), split_axis=0, concat_axis=0, tiled...  14.6 us
    all_to_all x1, starting transfers between devices, body(): lax.all_to_all(send, ('dp', 'blk'), split_axis=0, concat_axis=0, tiled=True)  11.5 us
    ppermute x1, waiting for transfers between devices, body(): next_data = lax.ppermute(data, ('dp', 'blk'), backward)  7.88 us
    ppermute x1, waiting for transfers between devices, body(): prev_data = lax.ppermute(data, ('dp', 'blk'), forward)  2.75 us
    dot_general x4, matrix products, masks(): lax.dot_general(query_rows, key_rows, (((1,), (1,)), ((), ())), preferred...  2.58 us
    ppermute x1, starting transfers between devices, body(): next_data = lax.ppermute(data, ('dp', 'blk'), backward)  2.19 us
    pallas_call x1, Pallas kernels, build_send(): pl.pallas_call(prologue(dims), out_shape=(jax.ShapeDtypeStruct((points, w...  2.05 us
  transfers between devices with their start and end apart: 5, of which 4 were waited for; matrix products, arithmetic and copies ran while one was open for 2% of the time, Pallas kernels for 0%

profile of v13, /device:TPU:1, one launch (start us, length us, event | category | flops | bytes accessed | tf_op | source)
XLA Modules:
  0.0 69.8 jit_solution(12576150256746361359)
XLA Ops:
  0.0 2.1 %shard_map.46 = (bf16[256,896]{1,0:T(8,128)(2,1)}, s32[1,256]{1,0:T(1,128)}, s32[1,256]{1,0:T(1,128)}, s32[1,256]{1,0:T(1,128)}, s32[1,256]{1,0:T(1,128)}) custom-call(bf16[256,768]{1,0:T(8,128)(2,1)} %emb_ref.1, s32[1,256]{1,0:T(1,128)} %bitcast.34, s32[1,256]{1,0:T(1,128)} %bitcast.35, s32[1,256]{1,0:T(1,128)} %bitcast.36), custom_call_target="tpu_custom_call" | custom-call | tf_op jit(solution)/shard_map/pallas_call | solution.py:79
  2.1 1.5 %convolution_convert_fusion = bf16[512,896]{1,0:T(8,128)(2,1)S(1)} fusion(bf16[256,896]{1,0:T(8,128)(2,1)} %get-tuple-element.16, s32[256]{0:T(256)} %bitcast.37), kind=kOutput, calls=%fused_computation.6 | convolution fusion | flops 235470848 | bytes 1377280 | tf_op jit(solution)/shard_map/dot_general | solution.py:91
  3.5 1.1 %all_to_all.11 = bf16[128,4,896]{2,1,0:T(4,128)(2,1)} reshape(bf16[512,896]{1,0:T(8,128)(2,1)S(1)} %convolution_convert_fusion) | data formatting | bytes 1835008 | tf_op jit(solution)/shard_map/all_to_all | solution.py:125
  4.7 11.5 %all-to-all-start = ((bf16[128,4,896]{2,1,0:T(4,128)(2,1)}), bf16[128,4,896]{2,1,0:T(4,128)(2,1)S(1)}, u32[]{:S(2)}, u32[]{:S(2)}) async-start(bf16[128,4,896]{2,1,0:T(4,128)(2,1)} %all_to_all.11), calls=%async_computation | async-start | bytes 1835008 | tf_op jit(solution)/shard_map/all_to_all | solution.py:125
  16.2 17.9 %all-to-all-done = bf16[128,4,896]{2,1,0:T(4,128)(2,1)S(1)} async-done(((bf16[128,4,896]{2,1,0:T(4,128)(2,1)}), bf16[128,4,896]{2,1,0:T(4,128)(2,1)S(1)}, u32[]{:S(2)}, u32[]{:S(2)}) %all-to-all-start) | async-done | bytes 917536 | tf_op jit(solution)/shard_map/all_to_all | solution.py:125
  34.1 0.2 all_to_all.13
  34.3 0.3 add_reduce_fusion.1
  34.7 1.1 %collective-permute-start.2 = (f32[2,512]{1,0:T(2,128)S(1)}, f32[2,512]{1,0:T(2,128)S(1)}, u32[]{:S(2)}, u32[]{:S(2)}) collective-permute-start(f32[2,512]{1,0:T(2,128)S(1)} %pad_maximum_fusion.1), channel_id=1, source_target_pairs={{1,0},{2,1},{3,2},{0,3},{12,4},{13,5},{14,6},{15,7},{9,8},{10,9},{... | collective-permute-start | bytes 12296 | tf_op jit(solution)/shard_map/ppermute | solution.py:134
  35.7 0.5 collective-permute-start
  36.2 2.2 %collective-permute-start.3 = (bf16[512,768]{1,0:T(8,128)(2,1)S(1)}, bf16[512,768]{1,0:T(8,128)(2,1)S(1)}, u32[]{:S(2)}, u32[]{:S(2)}) collective-permute-start(bf16[512,768]{1,0:T(8,128)(2,1)S(1)} %slice.69), channel_id=1, source_target_pairs={{1,0},{2,1},{3,2},{0,3},{12,4},{13,5},{14,6},{15,7},{9,8},{10,9},{... | collective-permute-start | bytes 2359304 | tf_op jit(solution)/shard_map/ppermute | solution.py:132
  38.4 0.6 fusion.2
  39.1 0.3 collective-permute-done
  39.5 7.9 %collective-permute-done.3 = bf16[512,768]{1,0:T(8,128)(2,1)S(1)} collective-permute-done((bf16[512,768]{1,0:T(8,128)(2,1)S(1)}, bf16[512,768]{1,0:T(8,128)(2,1)S(1)}, u32[]{:S(2)}, u32[]{:S(2)}) %collective-permute-start.3) | collective-permute-done | bytes 786464 | tf_op jit(solution)/shard_map/ppermute | solution.py:132
  47.4 0.6 select_reduce_fusion.1
  48.0 2.8 %collective-permute-done.1 = bf16[512,768]{1,0:T(8,128)(2,1)S(1)} collective-permute-done((bf16[512,768]{1,0:T(8,128)(2,1)S(1)}, bf16[512,768]{1,0:T(8,128)(2,1)S(1)}, u32[]{:S(2)}, u32[]{:S(2)}) %collective-permute-start.1) | collective-permute-done | bytes 786464 | tf_op jit(solution)/shard_map/ppermute | solution.py:131
  50.8 0.7 select_reduce_fusion.2
  51.4 0.1 max.26
  51.6 0.6 select_reduce_fusion.4
  52.2 0.1 reshape.114
  52.5 14.6 %all_to_all.17 = f32[128,1,12]{2,1,0:T(1,128)S(1)} all-to-all(f32[128,1,12]{2,1,0:T(1,128)S(1)} %bitcast.19), channel_id=1, replica_groups=mesh['dp'=32,'blk'=4] {'dp','blk'}, dimensions={0} | all-to-all | bytes 12288 | tf_op jit(solution)/shard_map/all_to_all | solution.py:158
  67.1 0.5 broadcast.51
  67.6 0.8 %reduce.9 = f32[128,12]{1,0:T(8,128)S(1)} reduce(f32[128,1,12]{2,1,0:T(1,128)S(1)} %all_to_all.17, f32[]{:T(128)} %broadcast.51), dimensions={1}, to_apply=%all_to_all.14.reduce_sub_computation.3 | reduce | bytes 12292 | tf_op jit(solution)/shard_map/all_to_all | solution.py:158
  68.6 0.6 select_reduce_fusion
  69.2 0.6 compare_select_fusion
  (20 shorter events, 0.4 us)
Async XLA Ops:
  4.7 29.4 %all-to-all-start = ((bf16[128,4,896]{2,1,0:T(4,128)(2,1)}), bf16[128,4,896]{2,1,0:T(4,128)(2,1)S(1)}, u32[]{:S(2)}, u32[]{:S(2)}) async-start(bf16[128,4,896]{2,1,0:T(4,128)(2,1)} %all_to_all.11), calls=%async_computation | async-start | bytes 1835008 | tf_op jit(solution)/shard_map/all_to_all | solution.py:125
  34.7 4.7 %collective-permute-start.2 = (f32[2,512]{1,0:T(2,128)S(1)}, f32[2,512]{1,0:T(2,128)S(1)}, u32[]{:S(2)}, u32[]{:S(2)}) collective-permute-start(f32[2,512]{1,0:T(2,128)S(1)} %pad_maximum_fusion.1), channel_id=1, source_target_pairs={{1,0},{2,1},{3,2},{0,3},{12,4},{13,5},{14,6},{15,7},{9,8},{10,9},{... | collective-permute-start | bytes 12296 | tf_op jit(solution)/shard_map/ppermute | solution.py:134
  35.7 3.7 %collective-permute-start = (f32[2,512]{1,0:T(2,128)S(1)}, f32[2,512]{1,0:T(2,128)S(1)}, u32[]{:S(2)}, u32[]{:S(2)}) collective-permute-start(f32[2,512]{1,0:T(2,128)S(1)} %pad_maximum_fusion.1), channel_id=1, source_target_pairs={{0,1},{1,2},{2,3},{3,0},{4,12},{5,13},{6,14},{7,15},{8,9},{9,10},{... | collective-permute-start | bytes 12296 | tf_op jit(solution)/shard_map/ppermute | solution.py:133
  36.2 11.1 %collective-permute-start.3 = (bf16[512,768]{1,0:T(8,128)(2,1)S(1)}, bf16[512,768]{1,0:T(8,128)(2,1)S(1)}, u32[]{:S(2)}, u32[]{:S(2)}) collective-permute-start(bf16[512,768]{1,0:T(8,128)(2,1)S(1)} %slice.69), channel_id=1, source_target_pairs={{1,0},{2,1},{3,2},{0,3},{12,4},{13,5},{14,6},{15,7},{9,8},{10,9},{... | collective-permute-start | bytes 2359304 | tf_op jit(solution)/shard_map/ppermute | solution.py:132
  38.4 12.3 %collective-permute-start.1 = (bf16[512,768]{1,0:T(8,128)(2,1)S(1)}, bf16[512,768]{1,0:T(8,128)(2,1)S(1)}, u32[]{:S(2)}, u32[]{:S(2)}) collective-permute-start(bf16[512,768]{1,0:T(8,128)(2,1)S(1)} %slice.69), channel_id=1, source_target_pairs={{0,1},{1,2},{2,3},{3,0},{4,12},{5,13},{6,14},{7,15},{8,9},{9,10},{... | collective-permute-start | bytes 2359304 | tf_op jit(solution)/shard_map/ppermute | solution.py:131
  51.5 17.0 %copy-start = (s32[1,256]{1,0:T(1,128)S(1)}, s32[1,256]{1,0:T(1,128)}, u32[]{:S(2)}) copy-start(s32[1,256]{1,0:T(1,128)} %get-tuple-element.12) | copy-start | bytes 3076
  51.5 17.0 %copy-start.1 = (s32[1,256]{1,0:T(1,128)S(1)}, s32[1,256]{1,0:T(1,128)}, u32[]{:S(2)}) copy-start(s32[1,256]{1,0:T(1,128)} %get-tuple-element.13) | copy-start | bytes 3076
  51.6 17.0 %copy-start.2 = (s32[1,256]{1,0:T(1,128)S(1)}, s32[1,256]{1,0:T(1,128)}, u32[]{:S(2)}) copy-start(s32[1,256]{1,0:T(1,128)} %get-tuple-element.14) | copy-start | bytes 3076

commit v14 on v12

--- a/solution.py
+++ b/solution.py
@@ -63,9 +63,13 @@
         group = group_row
         place = rank >> 2
         lane = rank & 3
-        dev = place_of(group, place, zs, xs, ys)
-        at_prev = place_of(group, (place + 3) & 3, zs, xs, ys) * 12 + 8 + lane
-        at_next = place_of(group, (place + 1) & 3, zs, xs, ys) * 12 + 4 + lane
+
+        def order_of(lin):
+            return (lin & 3) * (2 * zs * xs) + (lin >> 2)
+
+        dev = order_of(place_of(group, place, zs, xs, ys))
+        at_prev = order_of(place_of(group, (place + 3) & 3, zs, xs, ys)) * 12 + 8 + lane
+        at_next = order_of(place_of(group, (place + 1) & 3, zs, xs, ys)) * 12 + 4 + lane
         target_ref[...] = dev * 4 + lane
         own_ref[...] = dev * 12 + lane
         prev_ref[...] = at_prev
@@ -122,7 +126,7 @@
     slots = devices * 4
     group = point_group[:, 0]
     send, idx = build_send(embeddings, group, point_cluster, point_order, slots, dims)
-    own = lax.all_to_all(send, ("dp", "blk"), split_axis=0, concat_axis=0, tiled=True)
+    own = lax.all_to_all(send, ("blk", "dp"), split_axis=0, concat_axis=0, tiled=True)
     forward = [(i, int(nxt[i])) for i in range(devices)]
     backward = [(int(nxt[i]), i) for i in range(devices)]
     query = split_meta(own, width)
@@ -154,7 +158,7 @@
         [v.reshape(devices, 1, 4) for v in (best, side_prev, side_next)], axis=2
     )
     returned = lax.all_to_all(
-        payload, ("dp", "blk"), split_axis=0, concat_axis=0, tiled=False
+        payload, ("blk", "dp"), split_axis=0, concat_axis=0, tiled=False
     ).reshape(devices * 12)
     at_own, at_prev, at_next = idx[0], idx[1], idx[2]
     entry = jnp.arange(devices * 12, dtype=jnp.int32)[None, :]

time: 67.5 us -> 67.6 us (level)
  no operation moved by 1% of the time
where the time goes in v14:
time: 67.6 us; the launch traced here: 67.4 us
  waiting for transfers between devices  26.7 us (39%)
  starting transfers between devices  15 us (22%)
  blocking collectives  14.5 us (21%)
  matrix products  4.07 us (6%)
  other arithmetic  2.44 us (4%)
  local copies, waits for them, and re-layouts  2.34 us (3%)
  Pallas kernels  2.05 us (3%)
    all_to_all x1, waiting for transfers between devices, body(): lax.all_to_all(send, ('blk', 'dp'), split_axis=0, concat_axis=0, tiled=True)  17.8 us
    all_to_all x1, blocking collectives, body(): lax.all_to_all(payload, ('blk', 'dp'), split_axis=0, concat_axis=0, tiled...  14.5 us
    all_to_all x1, starting transfers between devices, body(): lax.all_to_all(send, ('blk', 'dp'), split_axis=0, concat_axis=0, tiled=True)  11.5 us
    ppermute x1, waiting for transfers between devices, body(): next_labels = lax.ppermute(labels, ('dp', 'blk'), backward)  7.06 us
    dot_general x4, matrix products, masks(): lax.dot_general(query_rows, key_rows, (((1,), (1,)), ((), ())), preferred...  2.6 us
    pallas_call x1, Pallas kernels, build_send(): pl.pallas_call(prologue(dims), out_shape=(jax.ShapeDtypeStruct((points, w...  2.05 us
    ppermute x1, starting transfers between devices, body(): next_labels = lax.ppermute(labels, ('dp', 'blk'), backward)  1.98 us
    ppermute x1, waiting for transfers between devices, body(): prev_labels = lax.ppermute(labels, ('dp', 'blk'), forward)  1.92 us
  transfers between devices with their start and end apart: 5, of which 3 were waited for; matrix products, arithmetic and copies ran while one was open for 1% of the time, Pallas kernels for 0%

profile of v14, /device:TPU:1, one launch (start us, length us, event | category | flops | bytes accessed | tf_op | source)
XLA Modules:
  0.0 67.4 jit_solution(17388709454910026244)
XLA Ops:
  0.0 2.1 %shard_map.46 = (bf16[256,896]{1,0:T(8,128)(2,1)}, s32[1,256]{1,0:T(1,128)}, s32[1,256]{1,0:T(1,128)}, s32[1,256]{1,0:T(1,128)}, s32[1,256]{1,0:T(1,128)}) custom-call(bf16[256,768]{1,0:T(8,128)(2,1)} %emb_ref.1, s32[1,256]{1,0:T(1,128)} %bitcast.30, s32[1,256]{1,0:T(1,128)} %bitcast.31, s32[1,256]{1,0:T(1,128)} %bitcast.32), custom_call_target="tpu_custom_call" | custom-call | tf_op jit(solution)/shard_map/pallas_call | solution.py:83
  2.1 1.5 %convolution_convert_fusion = bf16[512,896]{1,0:T(8,128)(2,1)S(1)} fusion(bf16[256,896]{1,0:T(8,128)(2,1)} %get-tuple-element.14, s32[256]{0:T(256)} %bitcast.33), kind=kOutput, calls=%fused_computation.6 | convolution fusion | flops 235470848 | bytes 1377280 | tf_op jit(solution)/shard_map/dot_general | solution.py:95
  3.5 1.1 %all_to_all.11 = bf16[128,4,896]{2,1,0:T(4,128)(2,1)} reshape(bf16[512,896]{1,0:T(8,128)(2,1)S(1)} %convolution_convert_fusion) | data formatting | bytes 1835008 | tf_op jit(solution)/shard_map/all_to_all | solution.py:129
  4.7 11.5 %all-to-all-start = ((bf16[128,4,896]{2,1,0:T(4,128)(2,1)}), bf16[128,4,896]{2,1,0:T(4,128)(2,1)S(1)}, u32[]{:S(2)}, u32[]{:S(2)}) async-start(bf16[128,4,896]{2,1,0:T(4,128)(2,1)} %all_to_all.11), calls=%async_computation | async-start | bytes 1835008 | tf_op jit(solution)/shard_map/all_to_all | solution.py:129
  16.2 17.8 %all-to-all-done = bf16[128,4,896]{2,1,0:T(4,128)(2,1)S(1)} async-done(((bf16[128,4,896]{2,1,0:T(4,128)(2,1)}), bf16[128,4,896]{2,1,0:T(4,128)(2,1)S(1)}, u32[]{:S(2)}, u32[]{:S(2)}) %all-to-all-start) | async-done | bytes 917536 | tf_op jit(solution)/shard_map/all_to_all | solution.py:129
  34.0 0.2 all_to_all.13
  34.2 0.3 add_reduce_fusion.1
  34.6 0.8 %collective-permute-start.3 = (bf16[512,768]{1,0:T(8,128)(2,1)S(1)}, bf16[512,768]{1,0:T(8,128)(2,1)S(1)}, u32[]{:S(2)}, u32[]{:S(2)}) collective-permute-start(bf16[512,768]{1,0:T(8,128)(2,1)S(1)} %slice.67), channel_id=1, source_target_pairs={{1,0},{2,1},{3,2},{0,3},{12,4},{13,5},{14,6},{15,7},{9,8},{10,9},{... | collective-permute-start | bytes 2359304 | tf_op jit(solution)/shard_map/ppermute | solution.py:136
  35.3 0.8 %collective-permute-start.1 = (bf16[512,768]{1,0:T(8,128)(2,1)S(1)}, bf16[512,768]{1,0:T(8,128)(2,1)S(1)}, u32[]{:S(2)}, u32[]{:S(2)}) collective-permute-start(bf16[512,768]{1,0:T(8,128)(2,1)S(1)} %slice.67), channel_id=1, source_target_pairs={{0,1},{1,2},{2,3},{3,0},{4,12},{5,13},{6,14},{7,15},{8,9},{9,10},{... | collective-permute-start | bytes 2359304 | tf_op jit(solution)/shard_map/ppermute | solution.py:135
  36.1 2.0 %collective-permute-start.2 = (f32[2,512]{1,0:T(2,128)S(1)}, f32[2,512]{1,0:T(2,128)S(1)}, u32[]{:S(2)}, u32[]{:S(2)}) collective-permute-start(f32[2,512]{1,0:T(2,128)S(1)} %pad_maximum_fusion.1), channel_id=1, source_target_pairs={{1,0},{2,1},{3,2},{0,3},{12,4},{13,5},{14,6},{15,7},{9,8},{10,9},{... | collective-permute-start | bytes 12296 | tf_op jit(solution)/shard_map/ppermute | solution.py:138
  38.1 0.7 fusion.2
  38.8 7.1 %collective-permute-done.2 = f32[2,512]{1,0:T(2,128)S(1)} collective-permute-done((f32[2,512]{1,0:T(2,128)S(1)}, f32[2,512]{1,0:T(2,128)S(1)}, u32[]{:S(2)}, u32[]{:S(2)}) %collective-permute-start.2) | collective-permute-done | bytes 4128 | tf_op jit(solution)/shard_map/ppermute | solution.py:138
  45.8 1.9 %collective-permute-done = f32[2,512]{1,0:T(2,128)S(1)} collective-permute-done((f32[2,512]{1,0:T(2,128)S(1)}, f32[2,512]{1,0:T(2,128)S(1)}, u32[]{:S(2)}, u32[]{:S(2)}) %collective-permute-start) | collective-permute-done | bytes 4128 | tf_op jit(solution)/shard_map/ppermute | solution.py:137
  47.8 0.6 select_reduce_fusion.4
  48.4 0.1 reshape.135
  48.5 0.1 reshape.134
  48.7 0.7 select_reduce_fusion.1
  49.3 0.7 select_reduce_fusion.2
  50.0 0.1 max.26
  50.2 14.5 %all_to_all.17 = f32[128,1,12]{2,1,0:T(1,128)S(1)} all-to-all(f32[128,1,12]{2,1,0:T(1,128)S(1)} %bitcast.21), channel_id=1, replica_groups=mesh['dp'=32,'blk'=4] {'blk','dp'}, dimensions={0} | all-to-all | bytes 12288 | tf_op jit(solution)/shard_map/all_to_all | solution.py:160
  64.7 0.5 broadcast.60
  65.2 0.8 %reduce.9 = f32[128,12]{1,0:T(8,128)S(1)} reduce(f32[128,1,12]{2,1,0:T(1,128)S(1)} %all_to_all.17, f32[]{:T(128)} %broadcast.60), dimensions={1}, to_apply=%all_to_all.14.reduce_sub_computation.3 | reduce | bytes 12292 | tf_op jit(solution)/shard_map/all_to_all | solution.py:160
  66.2 0.6 select_reduce_fusion
  66.8 0.6 compare_select_fusion
  (17 shorter events, 0.3 us)
Async XLA Ops:
  4.7 29.3 %all-to-all-start = ((bf16[128,4,896]{2,1,0:T(4,128)(2,1)}), bf16[128,4,896]{2,1,0:T(4,128)(2,1)S(1)}, u32[]{:S(2)}, u32[]{:S(2)}) async-start(bf16[128,4,896]{2,1,0:T(4,128)(2,1)} %all_to_all.11), calls=%async_computation | async-start | bytes 1835008 | tf_op jit(solution)/shard_map/all_to_all | solution.py:129
  34.6 13.2 %collective-permute-start.3 = (bf16[512,768]{1,0:T(8,128)(2,1)S(1)}, bf16[512,768]{1,0:T(8,128)(2,1)S(1)}, u32[]{:S(2)}, u32[]{:S(2)}) collective-permute-start(bf16[512,768]{1,0:T(8,128)(2,1)S(1)} %slice.67), channel_id=1, source_target_pairs={{1,0},{2,1},{3,2},{0,3},{12,4},{13,5},{14,6},{15,7},{9,8},{10,9},{... | collective-permute-start | bytes 2359304 | tf_op jit(solution)/shard_map/ppermute | solution.py:136
  35.3 12.4 %collective-permute-start.1 = (bf16[512,768]{1,0:T(8,128)(2,1)S(1)}, bf16[512,768]{1,0:T(8,128)(2,1)S(1)}, u32[]{:S(2)}, u32[]{:S(2)}) collective-permute-start(bf16[512,768]{1,0:T(8,128)(2,1)S(1)} %slice.67), channel_id=1, source_target_pairs={{0,1},{1,2},{2,3},{3,0},{4,12},{5,13},{6,14},{7,15},{8,9},{9,10},{... | collective-permute-start | bytes 2359304 | tf_op jit(solution)/shard_map/ppermute | solution.py:135
  36.1 9.7 %collective-permute-start.2 = (f32[2,512]{1,0:T(2,128)S(1)}, f32[2,512]{1,0:T(2,128)S(1)}, u32[]{:S(2)}, u32[]{:S(2)}) collective-permute-start(f32[2,512]{1,0:T(2,128)S(1)} %pad_maximum_fusion.1), channel_id=1, source_target_pairs={{1,0},{2,1},{3,2},{0,3},{12,4},{13,5},{14,6},{15,7},{9,8},{10,9},{... | collective-permute-start | bytes 12296 | tf_op jit(solution)/shard_map/ppermute | solution.py:138
  38.1 9.6 %collective-permute-start = (f32[2,512]{1,0:T(2,128)S(1)}, f32[2,512]{1,0:T(2,128)S(1)}, u32[]{:S(2)}, u32[]{:S(2)}) collective-permute-start(f32[2,512]{1,0:T(2,128)S(1)} %pad_maximum_fusion.1), channel_id=1, source_target_pairs={{0,1},{1,2},{2,3},{3,0},{4,12},{5,13},{6,14},{7,15},{8,9},{9,10},{... | collective-permute-start | bytes 12296 | tf_op jit(solution)/shard_map/ppermute | solution.py:137
  49.3 16.8 %copy-start = (s32[1,256]{1,0:T(1,128)S(1)}, s32[1,256]{1,0:T(1,128)}, u32[]{:S(2)}) copy-start(s32[1,256]{1,0:T(1,128)} %get-tuple-element.10) | copy-start | bytes 3076
  49.3 16.8 %copy-start.1 = (s32[1,256]{1,0:T(1,128)S(1)}, s32[1,256]{1,0:T(1,128)}, u32[]{:S(2)}) copy-start(s32[1,256]{1,0:T(1,128)} %get-tuple-element.11) | copy-start | bytes 3076
  49.3 16.8 %copy-start.2 = (s32[1,256]{1,0:T(1,128)S(1)}, s32[1,256]{1,0:T(1,128)}, u32[]{:S(2)}) copy-start(s32[1,256]{1,0:T(1,128)} %get-tuple-element.12) | copy-start | bytes 3076

commit v15 on v12

--- a/solution.py
+++ b/solution.py
@@ -118,7 +118,7 @@
 def body(embeddings, point_group, point_cluster, point_order, nxt, dims):
     _, xs, ys = dims
     devices = nxt.shape[0]
-    _, width = embeddings.shape
+    points, width = embeddings.shape
     slots = devices * 4
     group = point_group[:, 0]
     send, idx = build_send(embeddings, group, point_cluster, point_order, slots, dims)
@@ -150,16 +150,27 @@
     floor = jnp.full((half,), -2.0, jnp.float32)
     side_prev = jnp.where(inner, jnp.concatenate([row_part, floor]), col_part)
     side_next = jnp.where(inner, col_part, jnp.concatenate([floor, row_part]))
+    lanes = 128
     payload = jnp.concatenate(
-        [v.reshape(devices, 1, 4) for v in (best, side_prev, side_next)], axis=2
+        [v.reshape(devices, 1, 4) for v in (best, side_prev, side_next)]
+        + [jnp.broadcast_to(jnp.minimum(best[0], -2.0), (devices, 1, lanes - 12))],
+        axis=2,
     )
     returned = lax.all_to_all(
         payload, ("dp", "blk"), split_axis=0, concat_axis=0, tiled=False
-    ).reshape(devices * 12)
-    at_own, at_prev, at_next = idx[0], idx[1], idx[2]
-    entry = jnp.arange(devices * 12, dtype=jnp.int32)[None, :]
-    pick = (entry == at_own[:, None]) | (entry == at_prev[:, None]) | (entry == at_next[:, None])
-    found = jnp.max(jnp.where(pick, returned[None, :], -2.0), axis=1)
+    ).reshape(devices, lanes)
+    at = jnp.concatenate(idx)
+    sender = (at // 12)[:, None] == jnp.arange(devices, dtype=jnp.int32)[None, :]
+    rows = lax.dot_general(
+        sender.astype(jnp.float32),
+        returned,
+        (((1,), (0,)), ((), ())),
+        precision=lax.Precision.HIGHEST,
+        preferred_element_type=jnp.float32,
+    )
+    column = (at % 12)[:, None] == jnp.arange(lanes, dtype=jnp.int32)[None, :]
+    found = jnp.max(jnp.where(column, rows, -2.0), axis=1).reshape(3, points)
+    found = jnp.max(found, axis=0)
     return jnp.where(found > -1.5, found, -1.0)
 
 

time: 67.5 us -> 70 us (1.037)
  blocking collectives: 14 us -> 0 us
  waiting for transfers between devices: 26.8 us -> 38.1 us
  starting transfers between devices: 15.3 us -> 19.9 us
    all_to_all x1 -> x0, blocking collectives: 14 us -> none  [body(): lax.all_to_all(payload, ('dp', 'blk'), split_axis=0, concat_axis=0, tiled...]
    all_to_all x0 -> x1, waiting for transfers between devices: none -> 9.75 us  [body(): lax.all_to_all(payload, ('dp', 'blk'), split_axis=0, concat_axis=0, tiled...]
    all_to_all x0 -> x1, starting transfers between devices: none -> 5.38 us  [body(): lax.all_to_all(payload, ('dp', 'blk'), split_axis=0, concat_axis=0, tiled...]
    ppermute x1, waiting for transfers between devices: 0.01 us -> 2.99 us  [body(): prev_data = lax.ppermute(data, ('dp', 'blk'), forward)]
    ppermute x1, waiting for transfers between devices: 2.19 us -> 0.01 us  [body(): prev_labels = lax.ppermute(labels, ('dp', 'blk'), forward)]
    ppermute x1, starting transfers between devices: 2.26 us -> 0.31 us  [body(): next_labels = lax.ppermute(labels, ('dp', 'blk'), backward)]
    ppermute x1, starting transfers between devices: 0.01 us -> 1.22 us  [body(): prev_labels = lax.ppermute(labels, ('dp', 'blk'), forward)]
    concatenate x1, other arithmetic: 0.1 us -> 0.96 us  [body(): jnp.concatenate([v.reshape(devices, 1, 4) for v in (best, side_prev, side...]
  transfers between devices with their start and end apart: 5 -> 6, of which waited for: 3 -> 4; matrix products, arithmetic and copies ran while one was open for 1% -> 2% of each run, Pallas kernels for 0% -> 0%
where the time goes in v15:
time: 70 us; the launch traced here: 69.8 us
  waiting for transfers between devices  38.1 us (54%)
  starting transfers between devices  19.9 us (28%)
  matrix products  4.54 us (6%)
  local copies, waits for them, and re-layouts  2.33 us (3%)
  Pallas kernels  2.05 us (3%)
  other arithmetic  1.91 us (3%)
  between operations  0.87 us (1%)
    all_to_all x1, waiting for transfers between devices, body(): lax.all_to_all(send, ('dp', 'blk'), split_axis=0, concat_axis=0, tiled=True)  17.9 us
    all_to_all x1, starting transfers between devices, body(): lax.all_to_all(send, ('dp', 'blk'), split_axis=0, concat_axis=0, tiled=True)  11.5 us
    all_to_all x1, waiting for transfers between devices, body(): lax.all_to_all(payload, ('dp', 'blk'), split_axis=0, concat_axis=0, tiled...  9.75 us
    ppermute x1, waiting for transfers between devices, body(): next_labels = lax.ppermute(labels, ('dp', 'blk'), backward)  7.52 us
    all_to_all x1, starting transfers between devices, body(): lax.all_to_all(payload, ('dp', 'blk'), split_axis=0, concat_axis=0, tiled...  5.38 us
    ppermute x1, waiting for transfers between devices, body(): prev_data = lax.ppermute(data, ('dp', 'blk'), forward)  2.99 us
    dot_general x4, matrix products, masks(): lax.dot_general(query_rows, key_rows, (((1,), (1,)), ((), ())), preferred...  2.59 us
    pallas_call x1, Pallas kernels, build_send(): pl.pallas_call(prologue(dims), out_shape=(jax.ShapeDtypeStruct((points, w...  2.05 us
  transfers between devices with their start and end apart: 6, of which 4 were waited for; matrix products, arithmetic and copies ran while one was open for 2% of the time, Pallas kernels for 0%

profile of v15, /device:TPU:1, one launch (start us, length us, event | category | flops | bytes accessed | tf_op | source)
XLA Modules:
  0.0 69.8 jit_solution(12230095818121024025)
XLA Ops:
  0.0 2.1 %shard_map.46 = (bf16[256,896]{1,0:T(8,128)(2,1)}, s32[1,256]{1,0:T(1,128)}, s32[1,256]{1,0:T(1,128)}, s32[1,256]{1,0:T(1,128)}, s32[1,256]{1,0:T(1,128)}) custom-call(bf16[256,768]{1,0:T(8,128)(2,1)} %emb_ref.1, s32[1,256]{1,0:T(1,128)} %bitcast.38, s32[1,256]{1,0:T(1,128)} %bitcast.39, s32[1,256]{1,0:T(1,128)} %bitcast.40), custom_call_target="tpu_custom_call" | custom-call | tf_op jit(solution)/shard_map/pallas_call | solution.py:79
  2.1 1.5 %convolution_convert_fusion = bf16[512,896]{1,0:T(8,128)(2,1)S(1)} fusion(bf16[256,896]{1,0:T(8,128)(2,1)} %get-tuple-element.14, s32[256]{0:T(256)} %bitcast.41), kind=kOutput, calls=%fused_computation | convolution fusion | flops 235470848 | bytes 1377280 | tf_op jit(solution)/shard_map/dot_general | solution.py:91
  3.5 1.1 %all_to_all.11 = bf16[128,4,896]{2,1,0:T(4,128)(2,1)} reshape(bf16[512,896]{1,0:T(8,128)(2,1)S(1)} %convolution_convert_fusion) | data formatting | bytes 1835008 | tf_op jit(solution)/shard_map/all_to_all | solution.py:125
  4.7 11.5 %all-to-all-start = ((bf16[128,4,896]{2,1,0:T(4,128)(2,1)}), bf16[128,4,896]{2,1,0:T(4,128)(2,1)S(1)}, u32[]{:S(2)}, u32[]{:S(2)}) async-start(bf16[128,4,896]{2,1,0:T(4,128)(2,1)} %all_to_all.11), calls=%async_computation | async-start | bytes 1835008 | tf_op jit(solution)/shard_map/all_to_all | solution.py:125
  16.2 17.9 %all-to-all-done = bf16[128,4,896]{2,1,0:T(4,128)(2,1)S(1)} async-done(((bf16[128,4,896]{2,1,0:T(4,128)(2,1)}), bf16[128,4,896]{2,1,0:T(4,128)(2,1)S(1)}, u32[]{:S(2)}, u32[]{:S(2)}) %all-to-all-start) | async-done | bytes 917536 | tf_op jit(solution)/shard_map/all_to_all | solution.py:125
  34.1 0.2 all_to_all.13
  34.3 0.3 add_reduce_fusion.1
  34.7 1.1 %collective-permute-start.3 = (bf16[512,768]{1,0:T(8,128)(2,1)S(1)}, bf16[512,768]{1,0:T(8,128)(2,1)S(1)}, u32[]{:S(2)}, u32[]{:S(2)}) collective-permute-start(bf16[512,768]{1,0:T(8,128)(2,1)S(1)} %slice.71), channel_id=1, source_target_pairs={{1,0},{2,1},{3,2},{0,3},{12,4},{13,5},{14,6},{15,7},{9,8},{10,9},{... | collective-permute-start | bytes 2359304 | tf_op jit(solution)/shard_map/ppermute | solution.py:132
  35.7 0.3 collective-permute-start.2
  36.0 1.2 %collective-permute-start = (f32[2,512]{1,0:T(2,128)S(1)}, f32[2,512]{1,0:T(2,128)S(1)}, u32[]{:S(2)}, u32[]{:S(2)}) collective-permute-start(f32[2,512]{1,0:T(2,128)S(1)} %pad_maximum_fusion), channel_id=1, source_target_pairs={{0,1},{1,2},{2,3},{3,0},{4,12},{5,13},{6,14},{7,15},{8,9},{9,10},{... | collective-permute-start | bytes 12296 | tf_op jit(solution)/shard_map/ppermute | solution.py:133
  37.3 0.5 collective-permute-start.1
  37.7 0.6 fusion
  38.4 7.5 %collective-permute-done.2 = f32[2,512]{1,0:T(2,128)S(1)} collective-permute-done((f32[2,512]{1,0:T(2,128)S(1)}, f32[2,512]{1,0:T(2,128)S(1)}, u32[]{:S(2)}, u32[]{:S(2)}) %collective-permute-start.2) | collective-permute-done | bytes 4128 | tf_op jit(solution)/shard_map/ppermute | solution.py:134
  46.0 0.7 select_reduce_fusion
  46.6 3.0 %collective-permute-done.1 = bf16[512,768]{1,0:T(8,128)(2,1)S(1)} collective-permute-done((bf16[512,768]{1,0:T(8,128)(2,1)S(1)}, bf16[512,768]{1,0:T(8,128)(2,1)S(1)}, u32[]{:S(2)}, u32[]{:S(2)}) %collective-permute-start.1) | collective-permute-done | bytes 786464 | tf_op jit(solution)/shard_map/ppermute | solution.py:131
  49.6 0.7 select_reduce_fusion.1
  50.4 0.5 slice.67
  50.9 0.6 select_reduce_fusion.3
  51.5 0.1 reshape.232
  52.5 1.0 %maximum_maximum_fusion = f32[128,1,128]{2,1,0:T(1,128)} fusion(f32[128,1,4]{2,1,0:T(1,128)S(1)} %bitcast.27, f32[128,1,4]{2,1,0:T(1,128)S(1)} %bitcast.28, f32[128,1,4]{2,1,0:T(1,128)S(1)} %bitcast.26, f32[128]{0:T(128)S(1)} %pad.5.clone), kind=kLoop, calls=%fused_computation.24 | loop fusion | flops 49152 | bytes 72192 | tf_op jit(solution)/shard_map/concatenate | solution.py:154
  53.5 5.4 %all-to-all-start.1 = ((f32[128,1,128]{2,1,0:T(1,128)}), f32[128,1,128]{2,1,0:T(1,128)S(1)}, u32[]{:S(2)}, u32[]{:S(2)}) async-start(f32[128,1,128]{2,1,0:T(1,128)} %maximum_maximum_fusion), calls=%async_computation.1 | async-start | bytes 131072 | tf_op jit(solution)/shard_map/all_to_all | solution.py:159
  58.9 9.8 %all-to-all-done.1 = f32[128,1,128]{2,1,0:T(1,128)S(1)} async-done(((f32[128,1,128]{2,1,0:T(1,128)}), f32[128,1,128]{2,1,0:T(1,128)S(1)}, u32[]{:S(2)}, u32[]{:S(2)}) %all-to-all-start.1) | async-done | bytes 65568 | tf_op jit(solution)/shard_map/all_to_all | solution.py:159
  68.7 0.5 fusion.1
  69.2 0.6 compare_select_fusion
  (21 shorter events, 0.4 us)
Async XLA Ops:
  4.7 29.4 %all-to-all-start = ((bf16[128,4,896]{2,1,0:T(4,128)(2,1)}), bf16[128,4,896]{2,1,0:T(4,128)(2,1)S(1)}, u32[]{:S(2)}, u32[]{:S(2)}) async-start(bf16[128,4,896]{2,1,0:T(4,128)(2,1)} %all_to_all.11), calls=%async_computation | async-start | bytes 1835008 | tf_op jit(solution)/shard_map/all_to_all | solution.py:125
  34.7 11.3 %collective-permute-start.3 = (bf16[512,768]{1,0:T(8,128)(2,1)S(1)}, bf16[512,768]{1,0:T(8,128)(2,1)S(1)}, u32[]{:S(2)}, u32[]{:S(2)}) collective-permute-start(bf16[512,768]{1,0:T(8,128)(2,1)S(1)} %slice.71), channel_id=1, source_target_pairs={{1,0},{2,1},{3,2},{0,3},{12,4},{13,5},{14,6},{15,7},{9,8},{10,9},{... | collective-permute-start | bytes 2359304 | tf_op jit(solution)/shard_map/ppermute | solution.py:132
  35.7 10.2 %collective-permute-start.2 = (f32[2,512]{1,0:T(2,128)S(1)}, f32[2,512]{1,0:T(2,128)S(1)}, u32[]{:S(2)}, u32[]{:S(2)}) collective-permute-start(f32[2,512]{1,0:T(2,128)S(1)} %pad_maximum_fusion), channel_id=1, source_target_pairs={{1,0},{2,1},{3,2},{0,3},{12,4},{13,5},{14,6},{15,7},{9,8},{10,9},{... | collective-permute-start | bytes 12296 | tf_op jit(solution)/shard_map/ppermute | solution.py:134
  36.0 9.9 %collective-permute-start = (f32[2,512]{1,0:T(2,128)S(1)}, f32[2,512]{1,0:T(2,128)S(1)}, u32[]{:S(2)}, u32[]{:S(2)}) collective-permute-start(f32[2,512]{1,0:T(2,128)S(1)} %pad_maximum_fusion), channel_id=1, source_target_pairs={{0,1},{1,2},{2,3},{3,0},{4,12},{5,13},{6,14},{7,15},{8,9},{9,10},{... | collective-permute-start | bytes 12296 | tf_op jit(solution)/shard_map/ppermute | solution.py:133
  37.3 12.3 %collective-permute-start.1 = (bf16[512,768]{1,0:T(8,128)(2,1)S(1)}, bf16[512,768]{1,0:T(8,128)(2,1)S(1)}, u32[]{:S(2)}, u32[]{:S(2)}) collective-permute-start(bf16[512,768]{1,0:T(8,128)(2,1)S(1)} %slice.71), channel_id=1, source_target_pairs={{0,1},{1,2},{2,3},{3,0},{4,12},{5,13},{6,14},{7,15},{8,9},{9,10},{... | collective-permute-start | bytes 2359304 | tf_op jit(solution)/shard_map/ppermute | solution.py:131
  50.9 8.0 %copy-start = (s32[1,256]{1,0:T(1,128)S(1)}, s32[1,256]{1,0:T(1,128)}, u32[]{:S(2)}) copy-start(s32[1,256]{1,0:T(1,128)} %get-tuple-element.10) | copy-start | bytes 3076
  50.9 8.0 %copy-start.1 = (s32[1,256]{1,0:T(1,128)S(1)}, s32[1,256]{1,0:T(1,128)}, u32[]{:S(2)}) copy-start(s32[1,256]{1,0:T(1,128)} %get-tuple-element.11) | copy-start | bytes 3076
  50.9 8.0 %copy-start.2 = (s32[1,256]{1,0:T(1,128)S(1)}, s32[1,256]{1,0:T(1,128)}, u32[]{:S(2)}) copy-start(s32[1,256]{1,0:T(1,128)} %get-tuple-element.12) | copy-start | bytes 3076
  53.5 15.2 %all-to-all-start.1 = ((f32[128,1,128]{2,1,0:T(1,128)}), f32[128,1,128]{2,1,0:T(1,128)S(1)}, u32[]{:S(2)}, u32[]{:S(2)}) async-start(f32[128,1,128]{2,1,0:T(1,128)} %maximum_maximum_fusion), calls=%async_computation.1 | async-start | bytes 131072 | tf_op jit(solution)/shard_map/all_to_all | solution.py:159

commit v16 on v15

--- a/solution.py
+++ b/solution.py
@@ -153,14 +153,15 @@
     lanes = 128
     payload = jnp.concatenate(
         [v.reshape(devices, 1, 4) for v in (best, side_prev, side_next)]
-        + [jnp.broadcast_to(jnp.minimum(best[0], -2.0), (devices, 1, lanes - 12))],
+        + [jnp.broadcast_to(best.reshape(devices, 1, 4)[:, :, :1] * 0.0 - 2.0, (devices, 1, lanes - 12))],
         axis=2,
     )
     returned = lax.all_to_all(
         payload, ("dp", "blk"), split_axis=0, concat_axis=0, tiled=False
     ).reshape(devices, lanes)
     at = jnp.concatenate(idx)
-    sender = (at // 12)[:, None] == jnp.arange(devices, dtype=jnp.int32)[None, :]
+    sender = lax.div(at, 12)[:, None] == jnp.arange(devices, dtype=jnp.int32)[None, :]
+    spot = lax.rem(at, 12)
     rows = lax.dot_general(
         sender.astype(jnp.float32),
         returned,
@@ -168,7 +169,7 @@
         precision=lax.Precision.HIGHEST,
         preferred_element_type=jnp.float32,
     )
-    column = (at % 12)[:, None] == jnp.arange(lanes, dtype=jnp.int32)[None, :]
+    column = spot[:, None] == jnp.arange(lanes, dtype=jnp.int32)[None, :]
     found = jnp.max(jnp.where(column, rows, -2.0), axis=1).reshape(3, points)
     found = jnp.max(found, axis=0)
     return jnp.where(found > -1.5, found, -1.0)

time: 70 us -> 68.6 us (0.980)
  waiting for transfers between devices: 38.1 us -> 33.8 us
  starting transfers between devices: 19.9 us -> 23.7 us
    ppermute x1, waiting for transfers between devices: 7.52 us -> 0.01 us  [body(): next_labels = lax.ppermute(labels, ('dp', 'blk'), backward)]
    ppermute x1, waiting for transfers between devices: 0.01 us -> 6.31 us  [body(): prev_labels = lax.ppermute(labels, ('dp', 'blk'), forward)]
    ppermute x1, waiting for transfers between devices: 2.99 us -> 0.01 us  [body(): prev_data = lax.ppermute(data, ('dp', 'blk'), forward)]
    ppermute x1, starting transfers between devices: 0.31 us -> 2.66 us  [body(): next_labels = lax.ppermute(labels, ('dp', 'blk'), backward)]
    ppermute x1, starting transfers between devices: 1.05 us -> 2.66 us  [body(): next_data = lax.ppermute(data, ('dp', 'blk'), backward)]
    all_to_all x1, starting transfers between devices: 5.38 us -> 6.7 us  [body(): lax.all_to_all(payload, ('dp', 'blk'), split_axis=0, concat_axis=0, tiled...]
    ppermute x1, starting transfers between devices: 1.22 us -> 0.07 us  [body(): prev_labels = lax.ppermute(labels, ('dp', 'blk'), forward)]
  transfers between devices with their start and end apart: 6 -> 6, of which waited for: 4 -> 3; matrix products, arithmetic and copies ran while one was open for 2% -> 1% of each run, Pallas kernels for 0% -> 0%
where the time goes in v16:
time: 68.6 us; the launch traced here: 68.4 us
  waiting for transfers between devices  33.8 us (49%)
  starting transfers between devices  23.7 us (35%)
  matrix products  4.55 us (7%)
  other arithmetic  2.15 us (3%)
  Pallas kernels  2.05 us (3%)
  local copies, waits for them, and re-layouts  1.94 us (3%)
    all_to_all x1, waiting for transfers between devices, body(): lax.all_to_all(send, ('dp', 'blk'), split_axis=0, concat_axis=0, tiled=True)  17.9 us
    all_to_all x1, starting transfers between devices, body(): lax.all_to_all(send, ('dp', 'blk'), split_axis=0, concat_axis=0, tiled=True)  11.5 us
    all_to_all x1, waiting for transfers between devices, body(): lax.all_to_all(payload, ('dp', 'blk'), split_axis=0, concat_axis=0, tiled...  9.62 us
    all_to_all x1, starting transfers between devices, body(): lax.all_to_all(payload, ('dp', 'blk'), split_axis=0, concat_axis=0, tiled...  6.7 us
    ppermute x1, waiting for transfers between devices, body(): prev_labels = lax.ppermute(labels, ('dp', 'blk'), forward)  6.31 us
    ppermute x1, starting transfers between devices, body(): next_data = lax.ppermute(data, ('dp', 'blk'), backward)  2.66 us
    ppermute x1, starting transfers between devices, body(): next_labels = lax.ppermute(labels, ('dp', 'blk'), backward)  2.66 us
    dot_general x4, matrix products, masks(): lax.dot_general(query_rows, key_rows, (((1,), (1,)), ((), ())), preferred...  2.6 us
  transfers between devices with their start and end apart: 6, of which 3 were waited for; matrix products, arithmetic and copies ran while one was open for 1% of the time, Pallas kernels for 0%

profile of v16, /device:TPU:1, one launch (start us, length us, event | category | flops | bytes accessed | tf_op | source)
XLA Modules:
  0.0 68.4 jit_solution(8441534458908219228)
XLA Ops:
  0.0 2.1 %shard_map.46 = (bf16[256,896]{1,0:T(8,128)(2,1)}, s32[1,256]{1,0:T(1,128)}, s32[1,256]{1,0:T(1,128)}, s32[1,256]{1,0:T(1,128)}, s32[1,256]{1,0:T(1,128)}) custom-call(bf16[256,768]{1,0:T(8,128)(2,1)} %emb_ref.1, s32[1,256]{1,0:T(1,128)} %bitcast.37, s32[1,256]{1,0:T(1,128)} %bitcast.38, s32[1,256]{1,0:T(1,128)} %bitcast.39), custom_call_target="tpu_custom_call" | custom-call | tf_op jit(solution)/shard_map/pallas_call | solution.py:79
  2.1 1.5 %convolution_convert_fusion = bf16[512,896]{1,0:T(8,128)(2,1)S(1)} fusion(bf16[256,896]{1,0:T(8,128)(2,1)} %get-tuple-element.14, s32[256]{0:T(256)} %bitcast.40), kind=kOutput, calls=%fused_computation | convolution fusion | flops 235470848 | bytes 1377280 | tf_op jit(solution)/shard_map/dot_general | solution.py:91
  3.5 1.1 %all_to_all.11 = bf16[128,4,896]{2,1,0:T(4,128)(2,1)} reshape(bf16[512,896]{1,0:T(8,128)(2,1)S(1)} %convolution_convert_fusion) | data formatting | bytes 1835008 | tf_op jit(solution)/shard_map/all_to_all | solution.py:125
  4.7 11.5 %all-to-all-start = ((bf16[128,4,896]{2,1,0:T(4,128)(2,1)}), bf16[128,4,896]{2,1,0:T(4,128)(2,1)S(1)}, u32[]{:S(2)}, u32[]{:S(2)}) async-start(bf16[128,4,896]{2,1,0:T(4,128)(2,1)} %all_to_all.11), calls=%async_computation | async-start | bytes 1835008 | tf_op jit(solution)/shard_map/all_to_all | solution.py:125
  16.2 17.9 %all-to-all-done = bf16[128,4,896]{2,1,0:T(4,128)(2,1)S(1)} async-done(((bf16[128,4,896]{2,1,0:T(4,128)(2,1)}), bf16[128,4,896]{2,1,0:T(4,128)(2,1)S(1)}, u32[]{:S(2)}, u32[]{:S(2)}) %all-to-all-start) | async-done | bytes 917536 | tf_op jit(solution)/shard_map/all_to_all | solution.py:125
  34.1 0.2 all_to_all.13
  34.3 0.3 add_reduce_fusion.1
  34.7 2.7 %collective-permute-start.3 = (bf16[512,768]{1,0:T(8,128)(2,1)S(1)}, bf16[512,768]{1,0:T(8,128)(2,1)S(1)}, u32[]{:S(2)}, u32[]{:S(2)}) collective-permute-start(bf16[512,768]{1,0:T(8,128)(2,1)S(1)} %slice.71), channel_id=1, source_target_pairs={{1,0},{2,1},{3,2},{0,3},{12,4},{13,5},{14,6},{15,7},{9,8},{10,9},{... | collective-permute-start | bytes 2359304 | tf_op jit(solution)/shard_map/ppermute | solution.py:132
  37.5 2.7 %collective-permute-start.2 = (f32[2,512]{1,0:T(2,128)S(1)}, f32[2,512]{1,0:T(2,128)S(1)}, u32[]{:S(2)}, u32[]{:S(2)}) collective-permute-start(f32[2,512]{1,0:T(2,128)S(1)} %pad_maximum_fusion.1), channel_id=1, source_target_pairs={{1,0},{2,1},{3,2},{0,3},{12,4},{13,5},{14,6},{15,7},{9,8},{10,9},{... | collective-permute-start | bytes 12296 | tf_op jit(solution)/shard_map/ppermute | solution.py:134
  40.2 0.6 fusion
  40.8 6.3 %collective-permute-done = f32[2,512]{1,0:T(2,128)S(1)} collective-permute-done((f32[2,512]{1,0:T(2,128)S(1)}, f32[2,512]{1,0:T(2,128)S(1)}, u32[]{:S(2)}, u32[]{:S(2)}) %collective-permute-start) | collective-permute-done | bytes 4128 | tf_op jit(solution)/shard_map/ppermute | solution.py:133
  47.2 0.6 select_reduce_fusion.3
  47.8 0.1 reshape.192
  47.9 0.1 reshape.193
  48.1 0.7 select_reduce_fusion.1
  48.7 0.7 select_reduce_fusion
  49.4 0.1 max.26
  49.5 0.1 fusion.10
  49.6 0.2 broadcast_in_dim.24
  49.8 1.1 %pad_maximum_fusion = f32[128,1,128]{2,1,0:T(1,128)} fusion(f32[128,1,116]{2,1,0:T(1,128)S(1)} %broadcast_in_dim.24, f32[128,1,4]{2,1,0:T(1,128)S(1)} %bitcast.27, f32[128,1,4]{2,1,0:T(1,128)S(1)} %bitcast.26, f32[128,1,4]{2,1,0:T(1,128)S(1)} %bitcast.25), kind=kLoop, calls=%fused_computation.27 | loop fusion | flops 49152 | bytes 131072 | tf_op jit(solution)/shard_map/concatenate | solution.py:154
  50.9 6.7 %all-to-all-start.1 = ((f32[128,1,128]{2,1,0:T(1,128)}), f32[128,1,128]{2,1,0:T(1,128)S(1)}, u32[]{:S(2)}, u32[]{:S(2)}) async-start(f32[128,1,128]{2,1,0:T(1,128)} %pad_maximum_fusion), calls=%async_computation.1 | async-start | bytes 131072 | tf_op jit(solution)/shard_map/all_to_all | solution.py:159
  57.7 9.6 %all-to-all-done.1 = f32[128,1,128]{2,1,0:T(1,128)S(1)} async-done(((f32[128,1,128]{2,1,0:T(1,128)}), f32[128,1,128]{2,1,0:T(1,128)S(1)}, u32[]{:S(2)}, u32[]{:S(2)}) %all-to-all-start.1) | async-done | bytes 65568 | tf_op jit(solution)/shard_map/all_to_all | solution.py:159
  67.3 0.5 fusion.1
  67.8 0.6 compare_select_fusion
  (20 shorter events, 0.3 us)
Async XLA Ops:
  4.7 29.4 %all-to-all-start = ((bf16[128,4,896]{2,1,0:T(4,128)(2,1)}), bf16[128,4,896]{2,1,0:T(4,128)(2,1)S(1)}, u32[]{:S(2)}, u32[]{:S(2)}) async-start(bf16[128,4,896]{2,1,0:T(4,128)(2,1)} %all_to_all.11), calls=%async_computation | async-start | bytes 1835008 | tf_op jit(solution)/shard_map/all_to_all | solution.py:125
  34.7 12.5 %collective-permute-start.1 = (bf16[512,768]{1,0:T(8,128)(2,1)S(1)}, bf16[512,768]{1,0:T(8,128)(2,1)S(1)}, u32[]{:S(2)}, u32[]{:S(2)}) collective-permute-start(bf16[512,768]{1,0:T(8,128)(2,1)S(1)} %slice.71), channel_id=1, source_target_pairs={{0,1},{1,2},{2,3},{3,0},{4,12},{5,13},{6,14},{7,15},{8,9},{9,10},{... | collective-permute-start | bytes 2359304 | tf_op jit(solution)/shard_map/ppermute | solution.py:131
  34.7 12.4 %collective-permute-start.3 = (bf16[512,768]{1,0:T(8,128)(2,1)S(1)}, bf16[512,768]{1,0:T(8,128)(2,1)S(1)}, u32[]{:S(2)}, u32[]{:S(2)}) collective-permute-start(bf16[512,768]{1,0:T(8,128)(2,1)S(1)} %slice.71), channel_id=1, source_target_pairs={{1,0},{2,1},{3,2},{0,3},{12,4},{13,5},{14,6},{15,7},{9,8},{10,9},{... | collective-permute-start | bytes 2359304 | tf_op jit(solution)/shard_map/ppermute | solution.py:132
  37.4 9.7 %collective-permute-start = (f32[2,512]{1,0:T(2,128)S(1)}, f32[2,512]{1,0:T(2,128)S(1)}, u32[]{:S(2)}, u32[]{:S(2)}) collective-permute-start(f32[2,512]{1,0:T(2,128)S(1)} %pad_maximum_fusion.1), channel_id=1, source_target_pairs={{0,1},{1,2},{2,3},{3,0},{4,12},{5,13},{6,14},{7,15},{8,9},{9,10},{... | collective-permute-start | bytes 12296 | tf_op jit(solution)/shard_map/ppermute | solution.py:133
  37.5 9.6 %collective-permute-start.2 = (f32[2,512]{1,0:T(2,128)S(1)}, f32[2,512]{1,0:T(2,128)S(1)}, u32[]{:S(2)}, u32[]{:S(2)}) collective-permute-start(f32[2,512]{1,0:T(2,128)S(1)} %pad_maximum_fusion.1), channel_id=1, source_target_pairs={{1,0},{2,1},{3,2},{0,3},{12,4},{13,5},{14,6},{15,7},{9,8},{10,9},{... | collective-permute-start | bytes 12296 | tf_op jit(solution)/shard_map/ppermute | solution.py:134
  48.7 8.9 %copy-start = (s32[1,256]{1,0:T(1,128)S(1)}, s32[1,256]{1,0:T(1,128)}, u32[]{:S(2)}) copy-start(s32[1,256]{1,0:T(1,128)} %get-tuple-element.10) | copy-start | bytes 3076
  48.7 8.9 %copy-start.1 = (s32[1,256]{1,0:T(1,128)S(1)}, s32[1,256]{1,0:T(1,128)}, u32[]{:S(2)}) copy-start(s32[1,256]{1,0:T(1,128)} %get-tuple-element.11) | copy-start | bytes 3076
  48.7 8.9 %copy-start.2 = (s32[1,256]{1,0:T(1,128)S(1)}, s32[1,256]{1,0:T(1,128)}, u32[]{:S(2)}) copy-start(s32[1,256]{1,0:T(1,128)} %get-tuple-element.12) | copy-start | bytes 3076
  50.9 16.4 %all-to-all-start.1 = ((f32[128,1,128]{2,1,0:T(1,128)}), f32[128,1,128]{2,1,0:T(1,128)S(1)}, u32[]{:S(2)}, u32[]{:S(2)}) async-start(f32[128,1,128]{2,1,0:T(1,128)} %pad_maximum_fusion), calls=%async_computation.1 | async-start | bytes 131072 | tf_op jit(solution)/shard_map/all_to_all | solution.py:159

commit v17 on v16

--- a/solution.py
+++ b/solution.py
@@ -135,14 +135,16 @@
     prev = (prev_data, prev_labels[0], prev_labels[1])
     next_ = (next_data, next_labels[0], next_labels[1])
     best = best_over(query, query)
-    best = jnp.maximum(best, best_over(query, prev))
+    near = best_over(query, prev)
+    best = jnp.maximum(best, near)
     best = jnp.maximum(best, best_over(query, next_))
     half = slots // 2
     here = lax.axis_index(("dp", "blk"))
     me = jnp.where((here // ys) % 2 == 0, here % ys, (here // (2 * ys)) % xs)
     inner = (me == 1) | (me == 2)
-    rows = tuple(jnp.where(inner, p[:half], n[half:]) for p, n in zip(prev, next_))
-    cols = tuple(jnp.where(inner, n, p) for p, n in zip(prev, next_))
+    far_prev = (prev[0],) + lax.optimization_barrier(prev[1:])
+    rows = tuple(jnp.where(inner, p[:half], n[half:]) for p, n in zip(far_prev, next_))
+    cols = tuple(jnp.where(inner, n, p) for p, n in zip(far_prev, next_))
     scores, same_c, earlier = masks(rows, cols)
     row_part = jnp.max(jnp.where(same_c & earlier, scores, -2.0), axis=1)
     col_ok = same_c & (rows[2][:, None] < cols[2][None, :])

time: 68.6 us -> 71.9 us (1.048)
  waiting for transfers between devices: 33.8 us -> 36.4 us
    ppermute x1, waiting for transfers between devices: 0.01 us -> 8.93 us  [body(): prev_data = lax.ppermute(data, ('dp', 'blk'), forward)]
    ppermute x1, waiting for transfers between devices: 6.31 us -> 0.01 us  [body(): prev_labels = lax.ppermute(labels, ('dp', 'blk'), forward)]
where the time goes in v17:
time: 71.9 us; the launch traced here: 71.7 us
  waiting for transfers between devices  36.4 us (51%)
  starting transfers between devices  24.2 us (34%)
  matrix products  4.55 us (6%)
  other arithmetic  2.15 us (3%)
  Pallas kernels  2.05 us (3%)
  local copies, waits for them, and re-layouts  1.95 us (3%)
    all_to_all x1, waiting for transfers between devices, body(): lax.all_to_all(send, ('dp', 'blk'), split_axis=0, concat_axis=0, tiled=True)  17.9 us
    all_to_all x1, starting transfers between devices, body(): lax.all_to_all(send, ('dp', 'blk'), split_axis=0, concat_axis=0, tiled=True)  11.5 us
    all_to_all x1, waiting for transfers between devices, body(): lax.all_to_all(payload, ('dp', 'blk'), split_axis=0, concat_axis=0, tiled...  9.62 us
    ppermute x1, waiting for transfers between devices, body(): prev_data = lax.ppermute(data, ('dp', 'blk'), forward)  8.93 us
    all_to_all x1, starting transfers between devices, body(): lax.all_to_all(payload, ('dp', 'blk'), split_axis=0, concat_axis=0, tiled...  7.29 us
    ppermute x1, starting transfers between devices, body(): next_labels = lax.ppermute(labels, ('dp', 'blk'), backward)  2.66 us
    ppermute x1, starting transfers between devices, body(): next_data = lax.ppermute(data, ('dp', 'blk'), backward)  2.66 us
    dot_general x4, matrix products, masks(): lax.dot_general(query_rows, key_rows, (((1,), (1,)), ((), ())), preferred...  2.59 us
  transfers between devices with their start and end apart: 6, of which 3 were waited for; matrix products, arithmetic and copies ran while one was open for 1% of the time, Pallas kernels for 0%

profile of v17, /device:TPU:1, one launch (start us, length us, event | category | flops | bytes accessed | tf_op | source)
XLA Modules:
  0.0 71.7 jit_solution(8447188478163932020)
XLA Ops:
  0.0 2.1 %shard_map.46 = (bf16[256,896]{1,0:T(8,128)(2,1)}, s32[1,256]{1,0:T(1,128)}, s32[1,256]{1,0:T(1,128)}, s32[1,256]{1,0:T(1,128)}, s32[1,256]{1,0:T(1,128)}) custom-call(bf16[256,768]{1,0:T(8,128)(2,1)} %emb_ref.1, s32[1,256]{1,0:T(1,128)} %bitcast.41, s32[1,256]{1,0:T(1,128)} %bitcast.42, s32[1,256]{1,0:T(1,128)} %bitcast.43), custom_call_target="tpu_custom_call" | custom-call | tf_op jit(solution)/shard_map/pallas_call | solution.py:79
  2.1 1.5 %convolution_convert_fusion = bf16[512,896]{1,0:T(8,128)(2,1)S(1)} fusion(bf16[256,896]{1,0:T(8,128)(2,1)} %get-tuple-element.16, s32[256]{0:T(256)} %bitcast.44), kind=kOutput, calls=%fused_computation | convolution fusion | flops 235470848 | bytes 1377280 | tf_op jit(solution)/shard_map/dot_general | solution.py:91
  3.5 1.1 %all_to_all.11 = bf16[128,4,896]{2,1,0:T(4,128)(2,1)} reshape(bf16[512,896]{1,0:T(8,128)(2,1)S(1)} %convolution_convert_fusion) | data formatting | bytes 1835008 | tf_op jit(solution)/shard_map/all_to_all | solution.py:125
  4.7 11.5 %all-to-all-start = ((bf16[128,4,896]{2,1,0:T(4,128)(2,1)}), bf16[128,4,896]{2,1,0:T(4,128)(2,1)S(1)}, u32[]{:S(2)}, u32[]{:S(2)}) async-start(bf16[128,4,896]{2,1,0:T(4,128)(2,1)} %all_to_all.11), calls=%async_computation | async-start | bytes 1835008 | tf_op jit(solution)/shard_map/all_to_all | solution.py:125
  16.2 17.9 %all-to-all-done = bf16[128,4,896]{2,1,0:T(4,128)(2,1)S(1)} async-done(((bf16[128,4,896]{2,1,0:T(4,128)(2,1)}), bf16[128,4,896]{2,1,0:T(4,128)(2,1)S(1)}, u32[]{:S(2)}, u32[]{:S(2)}) %all-to-all-start) | async-done | bytes 917536 | tf_op jit(solution)/shard_map/all_to_all | solution.py:125
  34.1 0.2 all_to_all.13
  34.3 0.3 add_reduce_fusion.1
  34.7 2.7 %collective-permute-start.2 = (f32[2,512]{1,0:T(2,128)S(1)}, f32[2,512]{1,0:T(2,128)S(1)}, u32[]{:S(2)}, u32[]{:S(2)}) collective-permute-start(f32[2,512]{1,0:T(2,128)S(1)} %pad_maximum_fusion.1), channel_id=1, source_target_pairs={{1,0},{2,1},{3,2},{0,3},{12,4},{13,5},{14,6},{15,7},{9,8},{10,9},{... | collective-permute-start | bytes 12296 | tf_op jit(solution)/shard_map/ppermute | solution.py:134
  37.5 2.7 %collective-permute-start.3 = (bf16[512,768]{1,0:T(8,128)(2,1)S(1)}, bf16[512,768]{1,0:T(8,128)(2,1)S(1)}, u32[]{:S(2)}, u32[]{:S(2)}) collective-permute-start(bf16[512,768]{1,0:T(8,128)(2,1)S(1)} %slice.73), channel_id=1, source_target_pairs={{1,0},{2,1},{3,2},{0,3},{12,4},{13,5},{14,6},{15,7},{9,8},{10,9},{... | collective-permute-start | bytes 2359304 | tf_op jit(solution)/shard_map/ppermute | solution.py:132
  40.2 0.6 fusion
  40.9 8.9 %collective-permute-done.1 = bf16[512,768]{1,0:T(8,128)(2,1)S(1)} collective-permute-done((bf16[512,768]{1,0:T(8,128)(2,1)S(1)}, bf16[512,768]{1,0:T(8,128)(2,1)S(1)}, u32[]{:S(2)}, u32[]{:S(2)}) %collective-permute-start.1) | collective-permute-done | bytes 786464 | tf_op jit(solution)/shard_map/ppermute | solution.py:131
  49.8 0.6 select_reduce_fusion.3
  50.5 0.1 reshape.172
  50.6 0.1 reshape.173
  50.7 0.7 select_reduce_fusion
  51.4 0.7 select_reduce_fusion.1
  52.1 0.1 max.26
  52.2 0.1 fusion.10
  52.3 0.2 broadcast_in_dim.24
  52.5 1.1 %pad_maximum_fusion = f32[128,1,128]{2,1,0:T(1,128)} fusion(f32[128,1,116]{2,1,0:T(1,128)S(1)} %broadcast_in_dim.24, f32[128,1,4]{2,1,0:T(1,128)S(1)} %bitcast.25, f32[128,1,4]{2,1,0:T(1,128)S(1)} %bitcast.24, f32[128,1,4]{2,1,0:T(1,128)S(1)} %bitcast.23), kind=kLoop, calls=%fused_computation.27 | loop fusion | flops 49152 | bytes 131072 | tf_op jit(solution)/shard_map/concatenate | solution.py:156
  53.6 7.3 %all-to-all-start.1 = ((f32[128,1,128]{2,1,0:T(1,128)}), f32[128,1,128]{2,1,0:T(1,128)S(1)}, u32[]{:S(2)}, u32[]{:S(2)}) async-start(f32[128,1,128]{2,1,0:T(1,128)} %pad_maximum_fusion), calls=%async_computation.1 | async-start | bytes 131072 | tf_op jit(solution)/shard_map/all_to_all | solution.py:161
  60.9 9.6 %all-to-all-done.1 = f32[128,1,128]{2,1,0:T(1,128)S(1)} async-done(((f32[128,1,128]{2,1,0:T(1,128)}), f32[128,1,128]{2,1,0:T(1,128)S(1)}, u32[]{:S(2)}, u32[]{:S(2)}) %all-to-all-start.1) | async-done | bytes 65568 | tf_op jit(solution)/shard_map/all_to_all | solution.py:161
  70.6 0.5 fusion.1
  71.1 0.6 compare_select_fusion
  (23 shorter events, 0.3 us)
Async XLA Ops:
  4.7 29.4 %all-to-all-start = ((bf16[128,4,896]{2,1,0:T(4,128)(2,1)}), bf16[128,4,896]{2,1,0:T(4,128)(2,1)S(1)}, u32[]{:S(2)}, u32[]{:S(2)}) async-start(bf16[128,4,896]{2,1,0:T(4,128)(2,1)} %all_to_all.11), calls=%async_computation | async-start | bytes 1835008 | tf_op jit(solution)/shard_map/all_to_all | solution.py:125
  34.6 6.2 %collective-permute-start = (f32[2,512]{1,0:T(2,128)S(1)}, f32[2,512]{1,0:T(2,128)S(1)}, u32[]{:S(2)}, u32[]{:S(2)}) collective-permute-start(f32[2,512]{1,0:T(2,128)S(1)} %pad_maximum_fusion.1), channel_id=1, source_target_pairs={{0,1},{1,2},{2,3},{3,0},{4,12},{5,13},{6,14},{7,15},{8,9},{9,10},{... | collective-permute-start | bytes 12296 | tf_op jit(solution)/shard_map/ppermute | solution.py:133
  34.7 6.1 %collective-permute-start.2 = (f32[2,512]{1,0:T(2,128)S(1)}, f32[2,512]{1,0:T(2,128)S(1)}, u32[]{:S(2)}, u32[]{:S(2)}) collective-permute-start(f32[2,512]{1,0:T(2,128)S(1)} %pad_maximum_fusion.1), channel_id=1, source_target_pairs={{1,0},{2,1},{3,2},{0,3},{12,4},{13,5},{14,6},{15,7},{9,8},{10,9},{... | collective-permute-start | bytes 12296 | tf_op jit(solution)/shard_map/ppermute | solution.py:134
  37.4 12.4 %collective-permute-start.1 = (bf16[512,768]{1,0:T(8,128)(2,1)S(1)}, bf16[512,768]{1,0:T(8,128)(2,1)S(1)}, u32[]{:S(2)}, u32[]{:S(2)}) collective-permute-start(bf16[512,768]{1,0:T(8,128)(2,1)S(1)} %slice.73), channel_id=1, source_target_pairs={{0,1},{1,2},{2,3},{3,0},{4,12},{5,13},{6,14},{7,15},{8,9},{9,10},{... | collective-permute-start | bytes 2359304 | tf_op jit(solution)/shard_map/ppermute | solution.py:131
  37.5 12.3 %collective-permute-start.3 = (bf16[512,768]{1,0:T(8,128)(2,1)S(1)}, bf16[512,768]{1,0:T(8,128)(2,1)S(1)}, u32[]{:S(2)}, u32[]{:S(2)}) collective-permute-start(bf16[512,768]{1,0:T(8,128)(2,1)S(1)} %slice.73), channel_id=1, source_target_pairs={{1,0},{2,1},{3,2},{0,3},{12,4},{13,5},{14,6},{15,7},{9,8},{10,9},{... | collective-permute-start | bytes 2359304 | tf_op jit(solution)/shard_map/ppermute | solution.py:132
  51.4 9.5 %copy-start = (s32[1,256]{1,0:T(1,128)S(1)}, s32[1,256]{1,0:T(1,128)}, u32[]{:S(2)}) copy-start(s32[1,256]{1,0:T(1,128)} %get-tuple-element.12) | copy-start | bytes 3076
  51.4 9.5 %copy-start.1 = (s32[1,256]{1,0:T(1,128)S(1)}, s32[1,256]{1,0:T(1,128)}, u32[]{:S(2)}) copy-start(s32[1,256]{1,0:T(1,128)} %get-tuple-element.13) | copy-start | bytes 3076
  51.4 9.5 %copy-start.2 = (s32[1,256]{1,0:T(1,128)S(1)}, s32[1,256]{1,0:T(1,128)}, u32[]{:S(2)}) copy-start(s32[1,256]{1,0:T(1,128)} %get-tuple-element.14) | copy-start | bytes 3076
  53.6 17.0 %all-to-all-start.1 = ((f32[128,1,128]{2,1,0:T(1,128)}), f32[128,1,128]{2,1,0:T(1,128)S(1)}, u32[]{:S(2)}, u32[]{:S(2)}) async-start(f32[128,1,128]{2,1,0:T(1,128)} %pad_maximum_fusion), calls=%async_computation.1 | async-start | bytes 131072 | tf_op jit(solution)/shard_map/all_to_all | solution.py:161
